TPU v7x, 512 devices: a whole 4x4x16 slice. The times are simulated.
512 devices in a mesh: dp: 16 (over x, y), seq: 32 (over z, core).
Axes of the slice: x: 4, y: 4, z: 16, core: 2. Of those that a mesh axis runs over, the one named last changes fastest.
Arguments:
- query_rows: bfloat16 [32, 2048, 2048], P('seq', 'dp'), may hold values from -8 to 8
- key_rows: bfloat16 [32, 2048, 2048], P('seq', 'dp'), may hold values from -8 to 8
- value_rows: bfloat16 [32, 2048, 2048], P('seq', 'dp'), may hold values from -6 to 6
- out_grad: bfloat16 [32, 2048, 3072], P('seq', 'dp'), may hold values from -96 to 96
- out_weight: bfloat16 [2, 2048, 3072], P(None, ('dp', 'seq')), may hold values from -0.125 to 0.125
- text_length: int32 [32], P('seq'), may hold values from 65 to 512
Outputs:
- query_grad: bfloat16 [32, 2048, 2048], P('seq', 'dp')
- key_grad: bfloat16 [32, 2048, 2048], P('seq', 'dp')
- value_grad: bfloat16 [32, 2048, 2048], P('seq', 'dp')
All inputs are finite; a program needn't handle non-finite values.
Results may differ from a plain program's by a relative error of at most 0.0076.
Values may be sent and summed in bfloat16 or wider, within the bound.
No kernel may reach another device: no remote copies, remote signals or barrier semaphores. Data moves between devices by JAX's collectives and lax.ppermute only.
A program may use at most 128 MiB of HBM per device.

v0:
```python
import math

import jax
import jax.numpy as jnp
from jax import lax
from jax.sharding import PartitionSpec as P

HEADS = 16
HEAD_DIM = 128
TXT = 512


def attention_grads(query_heads, key_heads, value_heads, grad_heads, key_valid):
    total_rows = query_heads.shape[0]
    block_rows = min(512, total_rows)
    factor = 1.0 / math.sqrt(query_heads.shape[2])
    key_total = jnp.zeros(key_heads.shape, jnp.float32)
    value_total = jnp.zeros(value_heads.shape, jnp.float32)
    query_parts = []
    for first_row in range(0, total_rows, block_rows):
        query_block = query_heads[first_row : first_row + block_rows]
        grad_block = grad_heads[first_row : first_row + block_rows]
        scores = (
            jnp.einsum("qhc,khc->hqk", query_block, key_heads, preferred_element_type=jnp.float32)
            * factor
        )
        scores = jnp.where(key_valid[None, None, :], scores, -jnp.inf)
        shifted = jnp.exp(scores - jnp.max(scores, axis=2, keepdims=True))
        attention = shifted / jnp.sum(shifted, axis=2, keepdims=True)
        value_total = value_total + jnp.einsum(
            "hqk,qhc->khc",
            attention.astype(jnp.bfloat16),
            grad_block,
            preferred_element_type=jnp.float32,
        )
        weight_grad = jnp.einsum(
            "qhc,khc->hqk", grad_block, value_heads, preferred_element_type=jnp.float32
        )
        row_dot = jnp.sum(attention * weight_grad, axis=2, keepdims=True)
        score_grad = (attention * (weight_grad - row_dot) * factor).astype(jnp.bfloat16)
        query_parts.append(
            jnp.einsum(
                "hqk,khc->qhc", score_grad, key_heads, preferred_element_type=jnp.float32
            ).astype(jnp.bfloat16)
        )
        key_total = key_total + jnp.einsum(
            "hqk,qhc->khc", score_grad, query_block, preferred_element_type=jnp.float32
        )
    return (
        jnp.concatenate(query_parts, axis=0),
        key_total.astype(jnp.bfloat16),
        value_total.astype(jnp.bfloat16),
    )


def per_device(query_rows, key_rows, value_rows, out_grad, out_weight, text_length):
    devices = lax.axis_size("dp")
    tok_rows = query_rows.shape[1]
    total_rows = tok_rows * devices
    positions = jnp.arange(total_rows)
    key_valid = (positions >= TXT) | (positions < text_length[0])

    def by_heads(array):
        return array[0].reshape(tok_rows, HEADS, HEAD_DIM)

    slot_text = (jnp.arange(devices) * tok_rows < TXT)[:, None, None]
    outgoing = jnp.where(slot_text, out_weight[0][None], out_weight[1][None])
    stream_rows = lax.all_to_all(outgoing, "dp", split_axis=0, concat_axis=0, tiled=True)
    projected = jnp.einsum(
        "te,kre->tkr",
        out_grad[0],
        lax.all_gather(stream_rows, "seq", axis=1, tiled=True),
        preferred_element_type=jnp.float32,
    )
    grad_tokens = projected.astype(jnp.bfloat16)
    query_heads, key_heads, value_heads, grad_heads = (
        lax.all_to_all(by_heads(query_rows), "dp", split_axis=1, concat_axis=0, tiled=True),
        lax.all_to_all(by_heads(key_rows), "dp", split_axis=1, concat_axis=0, tiled=True),
        lax.all_to_all(by_heads(value_rows), "dp", split_axis=1, concat_axis=0, tiled=True),
        lax.all_to_all(grad_tokens, "dp", split_axis=1, concat_axis=0, tiled=True),
    )
    query_grad, key_grad, value_grad = attention_grads(
        query_heads, key_heads, value_heads, grad_heads, key_valid
    )
    returned = (
        lax.all_to_all(query_grad, "dp", split_axis=0, concat_axis=1, tiled=True),
        lax.all_to_all(key_grad, "dp", split_axis=0, concat_axis=1, tiled=True),
        lax.all_to_all(value_grad, "dp", split_axis=0, concat_axis=1, tiled=True),
    )
    return (
        returned[0].reshape(1, tok_rows, HEADS * HEAD_DIM),
        returned[1].reshape(1, tok_rows, HEADS * HEAD_DIM),
        returned[2].reshape(1, tok_rows, HEADS * HEAD_DIM),
    )


def solution(mesh):
    in_specs = (
        P("seq", "dp", None),
        P("seq", "dp", None),
        P("seq", "dp", None),
        P("seq", "dp", None),
        P(None, ("dp", "seq"), None),
        P("seq"),
    )
    out_specs = (P("seq", "dp", None), P("seq", "dp", None), P("seq", "dp", None))
    return jax.shard_map(
        per_device, mesh=mesh, in_specs=in_specs, out_specs=out_specs, check_vma=False
    )
```

profile of v0, /device:TPU:1, one launch (start us, length us, event | category | flops | bytes accessed | tf_op | source)
XLA Modules:
  0.0 233.4 jit_solution(1114282494881835689)
XLA Ops:
  8.4 15.4 %all_to_all.110 = bf16[16,4,3072]{2,1,0:T(4,128)(2,1)S(1)} all-to-all(bf16[16,4,3072]{2,1,0:T(4,128)(2,1)S(1)} %broadcast_select_fusion), channel_id=1, replica_groups=mesh['dp'=16,'seq'=32] {'dp'}, dimensions={0} | all-to-all | bytes 786432 | tf_op jit(solution)/shard_map/all_to_all | solution.py:68
  26.7 3.7 %all-to-all-start = ((bf16[128,16,128]{0,2,1:T(8,128)(2,1)}), bf16[128,16,128]{0,2,1:T(8,128)(2,1)S(1)}, u32[]{:S(2)}, u32[]{:S(2)}) async-start(bf16[128,16,128]{0,2,1:T(8,128)(2,1)} %bitcast.1), calls=%async_computation | async-start | bytes 1048576 | tf_op jit(solution)/shard_map/all_to_all | solution.py:77
  31.5 7.9 %all-to-all-done = bf16[128,16,128]{0,2,1:T(8,128)(2,1)S(1)} async-done(((bf16[128,16,128]{0,2,1:T(8,128)(2,1)}), bf16[128,16,128]{0,2,1:T(8,128)(2,1)S(1)}, u32[]{:S(2)}, u32[]{:S(2)}) %all-to-all-start) | async-done | bytes 524320 | tf_op jit(solution)/shard_map/all_to_all | solution.py:77
  39.4 3.6 %all-to-all-start.1 = ((bf16[128,16,128]{0,2,1:T(8,128)(2,1)}), bf16[128,16,128]{0,2,1:T(8,128)(2,1)S(1)}, u32[]{:S(2)}, u32[]{:S(2)}) async-start(bf16[128,16,128]{0,2,1:T(8,128)(2,1)} %bitcast.5), calls=%async_computation.1 | async-start | bytes 1048576 | tf_op jit(solution)/shard_map/all_to_all | solution.py:78
  45.3 6.6 %all-to-all-done.1 = bf16[128,16,128]{0,2,1:T(8,128)(2,1)S(1)} async-done(((bf16[128,16,128]{0,2,1:T(8,128)(2,1)}), bf16[128,16,128]{0,2,1:T(8,128)(2,1)S(1)}, u32[]{:S(2)}, u32[]{:S(2)}) %all-to-all-start.1) | async-done | bytes 524320 | tf_op jit(solution)/shard_map/all_to_all | solution.py:78
  51.9 3.6 %all-to-all-start.4 = ((bf16[128,16,128]{0,2,1:T(8,128)(2,1)}), bf16[128,16,128]{0,2,1:T(8,128)(2,1)S(1)}, u32[]{:S(2)}, u32[]{:S(2)}) async-start(bf16[128,16,128]{0,2,1:T(8,128)(2,1)} %bitcast.17), calls=%async_computation.4 | async-start | bytes 1048576 | tf_op jit(solution)/shard_map/all_to_all | solution.py:79
  63.8 51.8 %all-gather.2.cloned.1.call-done = bf16[16,128,3072]{2,0,1:T(8,128)(2,1)} async-done(((bf16[16,4,3072]{2,0,1:T(8,128)(2,1)}), bf16[16,128,3072]{2,0,1:T(8,128)(2,1)}) %all-gather.2.cloned.1.call-update) | async-done | bytes 12582928 | tf_op jit(solution)/shard_map/all_gather | solution.py:72
  115.6 6.5 %fusion.21 = bf16[128,16,128]{0,1,2:T(8,128)(2,1)S(1)} fusion(bf16[16,128,3072]{2,0,1:T(8,128)(2,1)} %all-gather.2.cloned.1.call-done, bf16[1,128,3072]{2,1,0:T(8,128)(2,1)S(1)} %copy-done), kind=kOutput, calls=%fused_computation.44 | convolution fusion | flops 1610874880 | bytes 13893632 | tf_op jit(solution)/shard_map/te,kre->tkr/dot_general | solution.py:69
  123.0 6.4 %all-to-all-start.3 = ((bf16[128,16,128]{0,2,1:T(8,128)(2,1)}), bf16[128,16,128]{0,2,1:T(8,128)(2,1)S(1)}, u32[]{:S(2)}, u32[]{:S(2)}) async-start(bf16[128,16,128]{0,2,1:T(8,128)(2,1)} %copy.98), calls=%async_computation.3 | async-start | bytes 1048576 | tf_op jit(solution)/shard_map/all_to_all | solution.py:80
  132.4 3.1 %fusion.5 = f32[512]{0:T(512)S(1)} fusion(f32[512,2048]{1,0:T(8,128)} %get-tuple-element.33, f32[512]{0:T(512)S(1)} %get-tuple-element.32, pred[2048]{0:T(1024)(128)(4,1)S(1)} %fusion.27), kind=kLoop, calls=%fused_computation.21 | loop fusion | flops 4193792 | bytes 4200448 | tf_op jit(solution)/shard_map/reduce_sum | solution.py:29
  135.5 4.2 %all-to-all-done.3 = bf16[128,16,128]{0,2,1:T(8,128)(2,1)S(1)} async-done(((bf16[128,16,128]{0,2,1:T(8,128)(2,1)}), bf16[128,16,128]{0,2,1:T(8,128)(2,1)S(1)}, u32[]{:S(2)}, u32[]{:S(2)}) %all-to-all-start.3) | async-done | bytes 524320 | tf_op jit(solution)/shard_map/all_to_all | solution.py:80
  140.8 3.0 %copy-done.2 = f32[512,2048]{1,0:T(8,128)S(1)} copy-done((f32[512,2048]{1,0:T(8,128)S(1)}, f32[512,2048]{1,0:T(8,128)}, u32[]{:S(2)}) %copy-start.2) | copy-done | bytes 4194328
  148.8 3.9 %multiply_reduce_fusion.3 = (f32[512]{0:T(512)S(1)}, f32[512]{0:T(512)S(1)}, f32[512]{0:T(512)S(1)}, f32[512]{0:T(512)S(1)}, f32[512,2048]{1,0:T(8,128)}) fusion(f32[512]{0:T(512)S(1)} %fusion.5, f32[512]{0:T(512)S(1)} %get-tuple-element.32, f32[512,2048]{1,0:T(8,128)S(1)} %copy-done.2, pred[2048]{0:T(1024)(128)(4,1)S(1)} %fusion.27, ...), kind=kOutput, calls=%fused_computation.13 | convolution fusion | flops 284162048 | bytes 21641216 | tf_op jit(solution)/shard_map/qhc,khc->hqk/dot_general | solution.py:36
  153.7 4.5 %multiply_reduce_fusion.2 = (f32[512]{0:T(512)S(1)}, f32[512]{0:T(512)S(1)}, f32[512]{0:T(512)S(1)}, f32[512,2048]{1,0:T(8,128)}) fusion(f32[512]{0:T(512)S(1)} %fusion.7, f32[512]{0:T(512)S(1)} %get-tuple-element.10, f32[512,2048]{1,0:T(8,128)S(1)} %copy-done.3, pred[2048]{0:T(1024)(128)(4,1)S(1)} %fusion.27, f32[512]{0:T(512)S(1)} %get-tuple-element.11, ...), kind=kOutput, calls=%fused_computation.9 | convolution fusion | flops 283113984 | bytes 17448960 | tf_op jit(solution)/shard_map/qhc,khc->hqk/dot_general | solution.py:36
  158.1 7.4 %multiply_reduce_fusion.1 = (f32[512]{0:T(512)S(1)}, f32[512]{0:T(512)S(1)}, bf16[512,2048]{1,0:T(8,128)(2,1)}, f32[512,2048]{1,0:T(8,128)}) fusion(f32[512]{0:T(512)S(1)} %get-tuple-element.14, f32[512]{0:T(512)S(1)} %get-tuple-element.11, f32[512,2048]{1,0:T(8,128)S(1)} %copy-done.5, pred[2048]{0:T(1024)(128)(4,1)S(1)} %fusion.27, ...), kind=kOutput, calls=%fused_computation.5 | convolution fusion | flops 289405952 | bytes 27938816 | tf_op jit(solution)/shard_map/qhc,khc->hqk/dot_general | solution.py:36
  165.5 8.2 %multiply_convert_fusion.3 = (bf16[512,2048]{1,0:T(8,128)(2,1)S(1)}, bf16[512,2048]{1,0:T(8,128)(2,1)S(1)}, bf16[512,2048]{1,0:T(8,128)(2,1)S(1)}) fusion(f32[512,2048]{1,0:T(8,128)} %get-tuple-element.34, f32[512]{0:T(512)S(1)} %get-tuple-element.9, f32[512]{0:T(512)S(1)} %fusion.5, f32[512]{0:T(512)S(1)} %get-tuple-element.32, ...), kind=kLoop, calls=%fused_computation.12 | loop fusion | flops 25165824 | bytes 31477760 | tf_op jit(solution)/shard_map/convert_element_type | solution.py:40
  186.3 3.9 %all-to-all-start.5 = ((bf16[16,2,8192]{2,1,0:T(2,128)(2,1)}), bf16[16,2,8192]{2,1,0:T(2,128)(2,1)S(1)}, u32[]{:S(2)}, u32[]{:S(2)}) async-start(bf16[16,2,8192]{2,1,0:T(2,128)(2,1)} %reshape.290), calls=%async_computation.5 | async-start | bytes 1048576 | tf_op jit(solution)/shard_map/all_to_all | solution.py:86
  190.2 4.8 %convolution_add_fusion.1 = f32[128,2048]{1,0:T(8,128)} fusion(f32[128,2048]{1,0:T(8,128)} %convolution_add_fusion.2, bf16[512,128]{1,0:T(8,128)(2,1)S(1)} %bitcast.153, f32[512,2048]{1,0:T(8,128)} %fusion.35, f32[512]{0:T(512)S(1)} %get-tuple-element.14, f32[512]{0:T(512)S(1)} %get-tuple-element.11, pred[2048]{0:T(1024)(128)(4,1)S(1)} %fusion.27), kind=kOutput, calls=%fused_computation.29 | convolution fusion | flops 273940480 | bytes 6428672 | tf_op jit(solution)/shard_map/hqk,qhc->khc/dot_general | solution.py:30
  195.0 4.4 %all-to-all-done.5 = bf16[16,2,8192]{2,1,0:T(2,128)(2,1)S(1)} async-done(((bf16[16,2,8192]{2,1,0:T(2,128)(2,1)}), bf16[16,2,8192]{2,1,0:T(2,128)(2,1)S(1)}, u32[]{:S(2)}, u32[]{:S(2)}) %all-to-all-start.5) | async-done | bytes 524320 | tf_op jit(solution)/shard_map/all_to_all | solution.py:86
  199.4 3.8 %all-to-all-start.6 = ((bf16[16,2,8192]{2,1,0:T(2,128)(2,1)}), bf16[16,2,8192]{2,1,0:T(2,128)(2,1)S(1)}, u32[]{:S(2)}, u32[]{:S(2)}) async-start(bf16[16,2,8192]{2,1,0:T(2,128)(2,1)} %reshape.292), calls=%async_computation.6 | async-start | bytes 1048576 | tf_op jit(solution)/shard_map/all_to_all | solution.py:87
  203.1 3.7 %fusion.14 = bf16[2048,1,128]{0,2,1:T(8,128)(2,1)S(1)} fusion(f32[128,2048]{1,0:T(8,128)} %convolution_add_fusion.1, bf16[512,128]{1,0:T(8,128)(2,1)S(1)} %bitcast.151, f32[512,2048]{1,0:T(8,128)} %fusion.36, f32[512]{0:T(512)S(1)} %get-tuple-element.15, f32[512]{0:T(512)S(1)} %get-tuple-element.12, pred[2048]{0:T(1024)(128)(4,1)S(1)} %fusion.27), kind=kOutput, calls=%fused_computation.36 | convolution fusion | flops 274202624 | bytes 5904384 | tf_op jit(solution)/shard_map/hqk,qhc->khc/dot_general | solution.py:30
  209.0 3.1 %all-to-all-done.6 = bf16[16,2,8192]{2,1,0:T(2,128)(2,1)S(1)} async-done(((bf16[16,2,8192]{2,1,0:T(2,128)(2,1)}), bf16[16,2,8192]{2,1,0:T(2,128)(2,1)S(1)}, u32[]{:S(2)}, u32[]{:S(2)}) %all-to-all-start.6) | async-done | bytes 524320 | tf_op jit(solution)/shard_map/all_to_all | solution.py:87
  212.1 3.6 %all-to-all-start.7 = ((bf16[16,2,8192]{2,1,0:T(2,128)(2,1)}), bf16[16,2,8192]{2,1,0:T(2,128)(2,1)S(1)}, u32[]{:S(2)}, u32[]{:S(2)}) async-start(bf16[16,2,8192]{2,1,0:T(2,128)(2,1)} %reshape.294), calls=%async_computation.7 | async-start | bytes 1048576 | tf_op jit(solution)/shard_map/all_to_all | solution.py:88
  219.5 5.2 %all-to-all-done.7 = bf16[16,2,8192]{2,1,0:T(2,128)(2,1)S(1)} async-done(((bf16[16,2,8192]{2,1,0:T(2,128)(2,1)}), bf16[16,2,8192]{2,1,0:T(2,128)(2,1)S(1)}, u32[]{:S(2)}, u32[]{:S(2)}) %all-to-all-start.7) | async-done | bytes 524320 | tf_op jit(solution)/shard_map/all_to_all | solution.py:88
  (99 shorter events, 46.1 us)
Async XLA Ops:
  7.2 108.4 %copy-start = (bf16[1,128,3072]{2,1,0:T(8,128)(2,1)S(1)}, bf16[1,128,3072]{2,1,0:T(8,128)(2,1)}, u32[]{:S(2)}) copy-start(bf16[1,128,3072]{2,1,0:T(8,128)(2,1)} %param.9) | copy-start | bytes 2359300
  7.2 23.3 %copy-start.12 = (bf16[1,128,2048]{2,1,0:T(8,128)(2,1)S(1)}, bf16[1,128,2048]{2,1,0:T(8,128)(2,1)}, u32[]{:S(2)}) copy-start(bf16[1,128,2048]{2,1,0:T(8,128)(2,1)} %param.7) | copy-start | bytes 1572868
  7.2 36.4 %copy-start.13 = (bf16[1,128,2048]{2,1,0:T(8,128)(2,1)S(1)}, bf16[1,128,2048]{2,1,0:T(8,128)(2,1)}, u32[]{:S(2)}) copy-start(bf16[1,128,2048]{2,1,0:T(8,128)(2,1)} %param.8) | copy-start | bytes 1572868
  7.2 108.4 %all-gather.2.cloned.1.call-start = ((), (), s32[]{:S(2)}) async-start(), calls=%async_computation.8 | async-start | bytes 12976128 | tf_op jit(solution)/shard_map/all_gather | solution.py:72
  26.7 12.7 %all-to-all-start = ((bf16[128,16,128]{0,2,1:T(8,128)(2,1)}), bf16[128,16,128]{0,2,1:T(8,128)(2,1)S(1)}, u32[]{:S(2)}, u32[]{:S(2)}) async-start(bf16[128,16,128]{0,2,1:T(8,128)(2,1)} %bitcast.1), calls=%async_computation | async-start | bytes 1048576 | tf_op jit(solution)/shard_map/all_to_all | solution.py:77
  39.4 12.5 %all-to-all-start.1 = ((bf16[128,16,128]{0,2,1:T(8,128)(2,1)}), bf16[128,16,128]{0,2,1:T(8,128)(2,1)S(1)}, u32[]{:S(2)}, u32[]{:S(2)}) async-start(bf16[128,16,128]{0,2,1:T(8,128)(2,1)} %bitcast.5), calls=%async_computation.1 | async-start | bytes 1048576 | tf_op jit(solution)/shard_map/all_to_all | solution.py:78
  44.8 16.3 %copy-start.10 = (bf16[4,128,1,128]{3,1,0,2:T(8,128)(2,1)}, bf16[4,128,1,128]{3,1,0,2:T(8,128)(2,1)S(1)}, u32[]{:S(2)}) copy-start(bf16[4,128,1,128]{3,1,0,2:T(8,128)(2,1)S(1)} %copy.104) | copy-start | bytes 393220
  45.3 15.9 %copy-start.8 = (bf16[4,128,1,128]{3,1,0,2:T(8,128)(2,1)}, bf16[4,128,1,128]{3,1,0,2:T(8,128)(2,1)S(1)}, u32[]{:S(2)}) copy-start(bf16[4,128,1,128]{3,1,0,2:T(8,128)(2,1)S(1)} %copy.94) | copy-start | bytes 393220
  51.9 71.1 %all-to-all-start.4 = ((bf16[128,16,128]{0,2,1:T(8,128)(2,1)}), bf16[128,16,128]{0,2,1:T(8,128)(2,1)S(1)}, u32[]{:S(2)}, u32[]{:S(2)}) async-start(bf16[128,16,128]{0,2,1:T(8,128)(2,1)} %bitcast.17), calls=%async_computation.4 | async-start | bytes 1048576 | tf_op jit(solution)/shard_map/all_to_all | solution.py:79
  123.0 16.7 %all-to-all-start.3 = ((bf16[128,16,128]{0,2,1:T(8,128)(2,1)}), bf16[128,16,128]{0,2,1:T(8,128)(2,1)S(1)}, u32[]{:S(2)}, u32[]{:S(2)}) async-start(bf16[128,16,128]{0,2,1:T(8,128)(2,1)} %copy.98), calls=%async_computation.3 | async-start | bytes 1048576 | tf_op jit(solution)/shard_map/all_to_all | solution.py:80
  140.0 3.8 %copy-start.2 = (f32[512,2048]{1,0:T(8,128)S(1)}, f32[512,2048]{1,0:T(8,128)}, u32[]{:S(2)}) copy-start(f32[512,2048]{1,0:T(8,128)} %get-tuple-element.33) | copy-start | bytes 12582916
  140.1 6.0 %copy-start.14 = (bf16[4,128,1,128]{3,1,0,2:T(8,128)(2,1)}, bf16[4,128,1,128]{3,1,0,2:T(8,128)(2,1)S(1)}, u32[]{:S(2)}) copy-start(bf16[4,128,1,128]{3,1,0,2:T(8,128)(2,1)S(1)} %get-tuple-element.23) | copy-start | bytes 393220
  140.1 13.6 %copy-start.18 = (bf16[4,128,1,128]{3,1,0,2:T(8,128)(2,1)}, bf16[4,128,1,128]{3,1,0,2:T(8,128)(2,1)S(1)}, u32[]{:S(2)}) copy-start(bf16[4,128,1,128]{3,1,0,2:T(8,128)(2,1)S(1)} %get-tuple-element.25) | copy-start | bytes 393220
  140.1 18.0 %copy-start.16 = (bf16[4,128,1,128]{3,1,0,2:T(8,128)(2,1)}, bf16[4,128,1,128]{3,1,0,2:T(8,128)(2,1)S(1)}, u32[]{:S(2)}) copy-start(bf16[4,128,1,128]{3,1,0,2:T(8,128)(2,1)S(1)} %get-tuple-element.24) | copy-start | bytes 393220
  140.8 17.3 %copy-start.6 = (f32[512,2048]{1,0:T(8,128)}, f32[512,2048]{1,0:T(8,128)S(1)}, u32[]{:S(2)}) copy-start(f32[512,2048]{1,0:T(8,128)S(1)} %fusion.37) | copy-start | bytes 12582916
  143.8 3.8 %copy-start.4 = (f32[512,2048]{1,0:T(8,128)S(1)}, f32[512,2048]{1,0:T(8,128)}, u32[]{:S(2)}) copy-start(f32[512,2048]{1,0:T(8,128)} %fusion.36) | copy-start | bytes 12582916
  143.8 5.0 %copy-start.5 = (f32[512,2048]{1,0:T(8,128)S(1)}, f32[512,2048]{1,0:T(8,128)}, u32[]{:S(2)}) copy-start(f32[512,2048]{1,0:T(8,128)} %fusion.35) | copy-start | bytes 12582916
  165.5 9.0 %copy-start.9 = (bf16[4,128,1,128]{3,1,0,2:T(8,128)(2,1)S(1)}, bf16[4,128,1,128]{3,1,0,2:T(8,128)(2,1)}, u32[]{:S(2)}) copy-start(bf16[4,128,1,128]{3,1,0,2:T(8,128)(2,1)} %copy-done.8) | copy-start | bytes 393220
  181.2 9.0 %copy-start.17 = (bf16[4,128,1,128]{3,1,0,2:T(8,128)(2,1)S(1)}, bf16[4,128,1,128]{3,1,0,2:T(8,128)(2,1)}, u32[]{:S(2)}) copy-start(bf16[4,128,1,128]{3,1,0,2:T(8,128)(2,1)} %copy-done.16) | copy-start | bytes 393220
  186.3 13.1 %all-to-all-start.5 = ((bf16[16,2,8192]{2,1,0:T(2,128)(2,1)}), bf16[16,2,8192]{2,1,0:T(2,128)(2,1)S(1)}, u32[]{:S(2)}, u32[]{:S(2)}) async-start(bf16[16,2,8192]{2,1,0:T(2,128)(2,1)} %reshape.290), calls=%async_computation.5 | async-start | bytes 1048576 | tf_op jit(solution)/shard_map/all_to_all | solution.py:86
  190.2 12.9 %copy-start.15 = (bf16[4,128,1,128]{3,1,0,2:T(8,128)(2,1)S(1)}, bf16[4,128,1,128]{3,1,0,2:T(8,128)(2,1)}, u32[]{:S(2)}) copy-start(bf16[4,128,1,128]{3,1,0,2:T(8,128)(2,1)} %copy-done.14) | copy-start | bytes 393220
  199.4 12.7 %all-to-all-start.6 = ((bf16[16,2,8192]{2,1,0:T(2,128)(2,1)}), bf16[16,2,8192]{2,1,0:T(2,128)(2,1)S(1)}, u32[]{:S(2)}, u32[]{:S(2)}) async-start(bf16[16,2,8192]{2,1,0:T(2,128)(2,1)} %reshape.292), calls=%async_computation.6 | async-start | bytes 1048576 | tf_op jit(solution)/shard_map/all_to_all | solution.py:87
  212.1 12.6 %all-to-all-start.7 = ((bf16[16,2,8192]{2,1,0:T(2,128)(2,1)}), bf16[16,2,8192]{2,1,0:T(2,128)(2,1)S(1)}, u32[]{:S(2)}, u32[]{:S(2)}) async-start(bf16[16,2,8192]{2,1,0:T(2,128)(2,1)} %reshape.294), calls=%async_computation.7 | async-start | bytes 1048576 | tf_op jit(solution)/shard_map/all_to_all | solution.py:88
  217.6 9.0 %copy-start.1 = (bf16[1,128,3072]{2,1,0:T(8,128)(2,1)S(1)}, bf16[1,128,3072]{2,1,0:T(8,128)(2,1)}, u32[]{:S(2)}) copy-start(bf16[1,128,3072]{2,1,0:T(8,128)(2,1)} %param.9) | copy-start | bytes 2359300
  (5 other events, 9.0 us)
Sparse Core Ops, SparseCore 0:
  24.8 90.7 all-gather.1
where the time goes:
time: 237 us; the launch traced here: 233 us
  waiting for transfers between devices  83.2 us (35%)
  matrix products  52.5 us (22%)
  starting transfers between devices  28.6 us (12%)
  local copies, waits for them, and re-layouts  23.3 us (10%)
  blocking collectives  15.4 us (6%)
  other arithmetic  15.3 us (6%)
  between operations  15.2 us (6%)
    all_gather x1, waiting for transfers between devices, per_device(): lax.all_gather(stream_rows, 'seq', axis=1, tiled=True)  51.8 us
    unnamed x58, local copies, waits for them, and re-layouts  17.8 us
    dot_general x4, matrix products, attention_grads(): jnp.einsum('qhc,khc->hqk', grad_block, value_heads, preferred_element_typ...  16.5 us
    all_to_all x1, blocking collectives, per_device(): lax.all_to_all(outgoing, 'dp', split_axis=0, concat_axis=0, tiled=True)  15.4 us
    dot_general x4, matrix products, attention_grads(): jnp.einsum('hqk,qhc->khc', attention.astype(jnp.bfloat16), grad_block, pr...  13 us
    dot_general x4, matrix products, attention_grads(): jnp.einsum('qhc,khc->hqk', query_block, key_heads, preferred_element_type...  10.7 us
    convert_element_type x1, other arithmetic, attention_grads(): (attention * (weight_grad - row_dot) * factor).astype(jnp.bfloat16)  8.21 us
    all_to_all x1, waiting for transfers between devices, per_device(): lax.all_to_all(by_heads(query_rows), 'dp', split_axis=1, concat_axis=0, t...  7.94 us
  transfers between devices with their start and end apart: 8, of which 7 were waited for; matrix products, arithmetic and copies ran while one was open for 17% of the time, Pallas kernels for 0%

commit v1 on v0

v1 whole, which is shorter than its diff:
```python
import functools
import math

import jax
import jax.numpy as jnp
from jax import lax
from jax.experimental import pallas as pl
from jax.experimental.pallas import tpu as pltpu
from jax.sharding import PartitionSpec as P

HEADS = 16
HEAD_DIM = 128
TXT = 512
BLOCK_ROWS = 256


def attention_kernel(length_ref, q_ref, k_ref, v_ref, g_ref, dq_ref, dk_ref, dv_ref, dkt_acc, dvt_acc):
    step = pl.program_id(0)
    factor = 1.0 / math.sqrt(q_ref.shape[1])
    nt = (((1,), (1,)), ((), ()))

    @pl.when(step == 0)
    def _():
        dkt_acc[...] = jnp.zeros_like(dkt_acc)
        dvt_acc[...] = jnp.zeros_like(dvt_acc)

    query_block = q_ref[...]
    grad_block = g_ref[...]
    keys = k_ref[...]
    values = v_ref[...]
    scores = lax.dot_general(query_block, keys, nt, preferred_element_type=jnp.float32) * factor
    column = lax.broadcasted_iota(jnp.int32, scores.shape, 1)
    valid = (column >= TXT) | (column < length_ref[0])
    scores = jnp.where(valid, scores, -jnp.inf)
    shifted = jnp.exp(scores - jnp.max(scores, axis=1, keepdims=True))
    attention = shifted / jnp.sum(shifted, axis=1, keepdims=True)
    attention_low = attention.astype(jnp.bfloat16)
    grad_t = grad_block.astype(jnp.float32).T.astype(jnp.bfloat16)
    dvt_acc[...] += jnp.dot(grad_t, attention_low, preferred_element_type=jnp.float32)
    weight_grad = lax.dot_general(grad_block, values, nt, preferred_element_type=jnp.float32)
    row_dot = jnp.sum(attention * weight_grad, axis=1, keepdims=True)
    score_grad = (attention * (weight_grad - row_dot) * factor).astype(jnp.bfloat16)
    dq_ref[...] = jnp.dot(score_grad, keys, preferred_element_type=jnp.float32).astype(dq_ref.dtype)
    query_t = query_block.astype(jnp.float32).T.astype(jnp.bfloat16)
    dkt_acc[...] += jnp.dot(query_t, score_grad, preferred_element_type=jnp.float32)

    @pl.when(step == pl.num_programs(0) - 1)
    def _():
        dk_ref[...] = dkt_acc[...].T.astype(dk_ref.dtype)
        dv_ref[...] = dvt_acc[...].T.astype(dv_ref.dtype)


def attention_grads(query, key, value, grad, length):
    rows, width = query.shape
    block = min(BLOCK_ROWS, rows)
    row_spec = pl.BlockSpec((block, width), lambda i: (i, 0))
    full_spec = pl.BlockSpec((rows, width), lambda i: (0, 0))
    out = jax.ShapeDtypeStruct((rows, width), jnp.bfloat16)
    flops = 10 * rows * rows * width
    return pl.pallas_call(
        attention_kernel,
        grid=(rows // block,),
        in_specs=[
            pl.BlockSpec(memory_space=pltpu.SMEM),
            row_spec,
            full_spec,
            full_spec,
            row_spec,
        ],
        out_specs=[row_spec, full_spec, full_spec],
        out_shape=[out, out, out],
        scratch_shapes=[
            pltpu.VMEM((width, rows), jnp.float32),
            pltpu.VMEM((width, rows), jnp.float32),
        ],
        compiler_params=pltpu.CompilerParams(
            dimension_semantics=("arbitrary",), vmem_limit_bytes=48 * 1024 * 1024
        ),
        cost_estimate=pl.CostEstimate(
            flops=flops, transcendentals=rows * rows, bytes_accessed=7 * rows * width * 2
        ),
    )(length, query, key, value, grad)


def per_device(query_rows, key_rows, value_rows, out_grad, out_weight, text_length):
    devices = lax.axis_size("dp")
    tok_rows = query_rows.shape[1]

    def by_heads(array):
        return array[0].reshape(tok_rows, HEADS, HEAD_DIM)

    both_streams = lax.all_gather(out_weight, "dp", axis=1, tiled=False)
    stream = (lax.axis_index("dp") * tok_rows >= TXT).astype(jnp.int32)
    stream_rows = lax.dynamic_index_in_dim(both_streams, stream, 0, keepdims=False)
    weight = lax.all_gather(stream_rows, "seq", axis=1, tiled=True)

    qkv = jnp.stack([by_heads(query_rows), by_heads(key_rows), by_heads(value_rows)])
    qkv_heads = lax.all_to_all(qkv, "dp", split_axis=2, concat_axis=1, tiled=True)

    projected = jnp.einsum(
        "te,kre->tkr", out_grad[0], weight, preferred_element_type=jnp.float32
    )
    grad_heads = lax.all_to_all(
        projected.astype(jnp.bfloat16), "dp", split_axis=1, concat_axis=0, tiled=True
    )
    total_rows = tok_rows * devices
    query_grad, key_grad, value_grad = attention_grads(
        qkv_heads[0].reshape(total_rows, HEAD_DIM),
        qkv_heads[1].reshape(total_rows, HEAD_DIM),
        qkv_heads[2].reshape(total_rows, HEAD_DIM),
        grad_heads.reshape(total_rows, HEAD_DIM),
        text_length,
    )
    grads = jnp.stack([query_grad, key_grad, value_grad]).reshape(3, total_rows, 1, HEAD_DIM)
    returned = lax.all_to_all(grads, "dp", split_axis=1, concat_axis=2, tiled=True)
    returned = returned.reshape(3, 1, tok_rows, HEADS * HEAD_DIM)
    return (returned[0], returned[1], returned[2])


def solution(mesh):
    in_specs = (
        P("seq", "dp", None),
        P("seq", "dp", None),
        P("seq", "dp", None),
        P("seq", "dp", None),
        P(None, ("dp", "seq"), None),
        P("seq"),
    )
    out_specs = (P("seq", "dp", None), P("seq", "dp", None), P("seq", "dp", None))
    return jax.shard_map(
        per_device, mesh=mesh, in_specs=in_specs, out_specs=out_specs, check_vma=False
    )
```

time: 237 us -> 235 us (level)
  blocking collectives: 15.4 us -> 50 us
  matrix products: 52.5 us -> 19.5 us
  Pallas kernels: 0 us -> 17.1 us
  starting transfers between devices: 28.6 us -> 11.7 us
  other arithmetic: 15.3 us -> 1.39 us
  waiting for transfers between devices: 83.2 us -> 93.7 us
    all_gather x1, waiting for transfers between devices: 51.8 us -> 85.5 us  [per_device(): weight = lax.all_gather(stream_rows, 'seq', axis=1, tiled=True)]
    dot_general x21 -> x1, matrix products: 52.5 us -> 19.5 us  [per_device(): jnp.einsum('te,kre->tkr', out_grad[0], weight, preferred_element_type=jnp...]
    all_to_all x7 -> x2, waiting for transfers between devices: 31.4 us -> 8.19 us  [the longest x1 8.19 us: per_device(): lax.all_to_all(projected.astype(jnp.bfloat16), 'dp', split_axis=1, concat...]
    all_gather x0 -> x1, blocking collectives: none -> 20.3 us  [per_device(): both_streams = lax.all_gather(out_weight, 'dp', axis=1, tiled=False)]
    pallas_call x0 -> x1, Pallas kernels: none -> 17.1 us  [attention_grads(): pl.pallas_call(attention_kernel, grid=(rows // block,), in_specs=[pl.Bloc...]
    all_to_all x7 -> x2, starting transfers between devices: 28.5 us -> 11.7 us  [the longest x1 6.39 us: per_device(): lax.all_to_all(projected.astype(jnp.bfloat16), 'dp', split_axis=1, concat...]
    all_to_all x1, blocking collectives: 15.4 us -> 29.6 us  [per_device(): lax.all_to_all(grads, 'dp', split_axis=1, concat_axis=2, tiled=True)]
    unnamed x58 -> x15, local copies, waits for them, and re-layouts: 17.8 us -> 3.64 us
  transfers between devices with their start and end apart: 8 -> 3, of which waited for: 7 -> 2; matrix products, arithmetic and copies ran while one was open for 17% -> 11% of each run, Pallas kernels for 0% -> 0%
where the time goes in v1:
time: 235 us; the launch traced here: 233 us
  waiting for transfers between devices  93.7 us (40%)
  blocking collectives  50 us (21%)
  local copies, waits for them, and re-layouts  25 us (11%)
  matrix products  19.5 us (8%)
  Pallas kernels  17.1 us (7%)
  between operations  14.8 us (6%)
  starting transfers between devices  11.7 us (5%)
    all_gather x1, waiting for transfers between devices, per_device(): weight = lax.all_gather(stream_rows, 'seq', axis=1, tiled=True)  85.5 us
    all_to_all x1, blocking collectives, per_device(): lax.all_to_all(grads, 'dp', split_axis=1, concat_axis=2, tiled=True)  29.6 us
    all_gather x1, blocking collectives, per_device(): both_streams = lax.all_gather(out_weight, 'dp', axis=1, tiled=False)  20.3 us
    dot_general x1, matrix products, per_device(): jnp.einsum('te,kre->tkr', out_grad[0], weight, preferred_element_type=jnp...  19.5 us
    pallas_call x1, Pallas kernels, attention_grads(): pl.pallas_call(attention_kernel, grid=(rows // block,), in_specs=[pl.Bloc...  17.1 us
    reshape x1, local copies, waits for them, and re-layouts, per_device(): jnp.stack([query_grad, key_grad, value_grad])  9.76 us
    all_to_all x1, waiting for transfers between devices, per_device(): lax.all_to_all(projected.astype(jnp.bfloat16), 'dp', split_axis=1, concat...  8.19 us
    all_to_all x1, starting transfers between devices, per_device(): lax.all_to_all(projected.astype(jnp.bfloat16), 'dp', split_axis=1, concat...  6.39 us
  transfers between devices with their start and end apart: 3, of which 2 were waited for; matrix products, arithmetic and copies ran while one was open for 11% of the time, Pallas kernels for 0%

profile of v1, /device:TPU:1, one launch (start us, length us, event | category | flops | bytes accessed | tf_op | source)
XLA Modules:
  0.0 233.2 jit_solution(9562634681995417065)
XLA Ops:
  7.2 0.9 copy.28
  8.1 20.3 %all-gather = bf16[2,64,3072]{2,0,1:T(2,128)(2,1)S(1)} all-gather(bf16[2,4,3072]{2,0,1:T(2,128)(2,1)S(1)} %copy.28), channel_id=2, replica_groups=mesh['dp'=16,'seq'=32] {'dp'}, dimensions={1}, use_global_device_ids=true | all-gather | bytes 835584 | tf_op jit(solution)/shard_map/all_gather | solution.py:92
  28.5 0.9 constant_dynamic-slice_fusion
  29.4 1.2 copy.36
  31.2 1.0 copy.26
  32.2 1.2 pad_maximum_fusion
  33.4 1.6 copy.27
  35.0 5.3 %all-to-all-start = ((bf16[3,128,16,128]{3,1,0,2:T(8,128)(2,1)}), bf16[3,128,16,128]{3,1,0,2:T(8,128)(2,1)S(1)}, u32[]{:S(2)}, u32[]{:S(2)}) async-start(bf16[3,128,16,128]{3,1,0,2:T(8,128)(2,1)} %copy.27), calls=%async_computation | async-start | bytes 3145728 | tf_op jit(solution)/shard_map/all_to_all | solution.py:98
  40.3 85.5 %all-gather.4.cloned.1.call-done = bf16[1,16,128,3072]{3,1,0,2:T(8,128)(2,1)} async-done(((bf16[1,16,4,3072]{3,1,0,2:T(8,128)(2,1)}), bf16[1,16,128,3072]{3,1,0,2:T(8,128)(2,1)}) %all-gather.4.cloned.1.call-update) | async-done | bytes 12582928 | tf_op jit(solution)/shard_map/all_gather | solution.py:95
  125.8 19.5 %fusion.6 = bf16[128,16,128]{0,2,1:T(8,128)(2,1)} fusion(bf16[1,16,128,3072]{3,1,0,2:T(8,128)(2,1)} %all-gather.4.cloned.1.call-done, bf16[1,128,3072]{2,1,0:T(8,128)(2,1)S(1)} %copy-done), kind=kOutput, calls=%fused_computation.6 | convolution fusion | flops 1610874880 | bytes 13893632 | tf_op jit(solution)/shard_map/te,kre->tkr/dot_general | solution.py:100
  145.3 6.4 %all-to-all-start.1 = ((bf16[128,16,128]{0,2,1:T(8,128)(2,1)}), bf16[128,16,128]{0,2,1:T(8,128)(2,1)S(1)}, u32[]{:S(2)}, u32[]{:S(2)}) async-start(bf16[128,16,128]{0,2,1:T(8,128)(2,1)} %fusion.6), calls=%async_computation.1 | async-start | bytes 1048576 | tf_op jit(solution)/shard_map/all_to_all | solution.py:103
  152.3 1.5 fusion.11
  153.8 8.2 %all-to-all-done.1 = bf16[128,16,128]{0,2,1:T(8,128)(2,1)S(1)} async-done(((bf16[128,16,128]{0,2,1:T(8,128)(2,1)}), bf16[128,16,128]{0,2,1:T(8,128)(2,1)S(1)}, u32[]{:S(2)}, u32[]{:S(2)}) %all-to-all-start.1) | async-done | bytes 524320 | tf_op jit(solution)/shard_map/all_to_all | solution.py:103
  162.0 0.3 copy.31
  162.3 17.1 %shard_map.85 = (bf16[2048,128]{1,0:T(8,128)(2,1)S(1)}, bf16[2048,128]{1,0:T(8,128)(2,1)S(1)}, bf16[2048,128]{1,0:T(8,128)(2,1)S(1)}) custom-call(s32[1]{0:T(128)S(6)} %copy.45.length_ref, bf16[2048,128]{1,0:T(8,128)(2,1)S(1)} %bitcast.50, bf16[2048,128]{1,0:T(8,128)(2,1)S(1)} %bitcast.49, bf16[2048,128]{1,0:T(8,128)(2,1)S(1)} %bitcast.48, ...), custom_call_target="tpu_custom_call" | custom-call | flops 5368709120 | bytes 3670016 | tf_op jit(solution)/shard_map/pallas_call | solution.py:60
  179.6 9.8 %copy.32 = bf16[3,2048,1,128]{3,0,2,1:T(4,128)(2,1)S(1)} copy(bf16[3,2048,1,128]{3,1,0,2:T(8,128)(2,1)S(1)} %maximum_bitcast_fusion) | data formatting | bytes 3145728 | tf_op jit(solution)/shard_map/reshape | solution.py:114
  189.4 29.6 %all_to_all.45 = bf16[3,2048,1,128]{3,0,2,1:T(4,128)(2,1)S(1)} all-to-all(bf16[3,2048,1,128]{3,0,2,1:T(4,128)(2,1)S(1)} %copy.32), channel_id=1, replica_groups=mesh['dp'=16,'seq'=32] {'dp'}, dimensions={1} | all-to-all | bytes 3145728 | tf_op jit(solution)/shard_map/all_to_all | solution.py:115
  219.0 2.5 %fusion.10 = (bf16[1,128,16,1,128]{4,0,1,2,3:T(2,128)(2,1)S(1)}, bf16[1,128,16,1,128]{4,0,1,2,3:T(2,128)(2,1)S(1)}, bf16[1,128,16,1,128]{4,0,1,2,3:T(2,128)(2,1)S(1)}) fusion(bf16[3,128,16,1,128]{4,0,1,2,3:T(4,128)(2,1)S(1)} %bitcast.54), kind=kLoop, calls=%fused_computation.9 | loop fusion | bytes 3145728 | tf_op jit(solution)/shard_map/slice | solution.py:117
  221.5 0.6 copy.33
  222.1 1.0 squeeze.18
  223.1 0.6 copy.34
  223.7 1.0 squeeze.19
  224.7 0.6 copy.35
  225.3 1.0 squeeze.20
  (16 shorter events, 0.8 us)
Async XLA Ops:
  7.2 118.7 %copy-start = (bf16[1,128,3072]{2,1,0:T(8,128)(2,1)S(1)}, bf16[1,128,3072]{2,1,0:T(8,128)(2,1)}, u32[]{:S(2)}) copy-start(bf16[1,128,3072]{2,1,0:T(8,128)(2,1)} %param.9) | copy-start | bytes 2359300
  7.2 118.6 %all-gather.4.cloned.1.call-start = ((), (), s32[]{:S(2)}) async-start(), calls=%async_computation.3 | async-start | bytes 12976128 | tf_op jit(solution)/shard_map/all_gather | solution.py:95
  28.5 2.2 copy-start.2
  29.4 1.5 copy-start.3
  29.4 1.8 copy-start.4
  35.0 110.3 %all-to-all-start = ((bf16[3,128,16,128]{3,1,0,2:T(8,128)(2,1)}), bf16[3,128,16,128]{3,1,0,2:T(8,128)(2,1)S(1)}, u32[]{:S(2)}, u32[]{:S(2)}) async-start(bf16[3,128,16,128]{3,1,0,2:T(8,128)(2,1)} %copy.27), calls=%async_computation | async-start | bytes 3145728 | tf_op jit(solution)/shard_map/all_to_all | solution.py:98
  145.3 7.0 %copy-start.1 = (bf16[3,128,16,128]{3,1,0,2:T(8,128)(2,1)}, bf16[3,128,16,128]{3,1,0,2:T(8,128)(2,1)S(1)}, u32[]{:S(2)}) copy-start(bf16[3,128,16,128]{3,1,0,2:T(8,128)(2,1)S(1)} %all-to-all-done) | copy-start | bytes 4718596
  145.3 16.7 %all-to-all-start.1 = ((bf16[128,16,128]{0,2,1:T(8,128)(2,1)}), bf16[128,16,128]{0,2,1:T(8,128)(2,1)S(1)}, u32[]{:S(2)}, u32[]{:S(2)}) async-start(bf16[128,16,128]{0,2,1:T(8,128)(2,1)} %fusion.6), calls=%async_computation.1 | async-start | bytes 1048576 | tf_op jit(solution)/shard_map/all_to_all | solution.py:103
Sparse Core Ops, SparseCore 0:
  30.7 95.0 all-gather.3

commit v2 on v1

--- a/solution.py
+++ b/solution.py
@@ -82,6 +82,34 @@
     )(length, query, key, value, grad)
 
 
+def projection_kernel(grad_ref, weight_ref, out_ref):
+    nt = (((1,), (1,)), ((), ()))
+    out_ref[0] = lax.dot_general(
+        grad_ref[...], weight_ref[0], nt, preferred_element_type=jnp.float32
+    ).astype(out_ref.dtype)
+
+
+def project(out_grad, weight):
+    rows, depth = out_grad.shape
+    heads, width, _ = weight.shape
+    return pl.pallas_call(
+        projection_kernel,
+        grid=(heads,),
+        in_specs=[
+            pl.BlockSpec((rows, depth), lambda h: (0, 0)),
+            pl.BlockSpec((1, width, depth), lambda h: (h, 0, 0)),
+        ],
+        out_specs=pl.BlockSpec((1, rows, width), lambda h: (h, 0, 0)),
+        out_shape=jax.ShapeDtypeStruct((heads, rows, width), jnp.bfloat16),
+        compiler_params=pltpu.CompilerParams(dimension_semantics=("arbitrary",)),
+        cost_estimate=pl.CostEstimate(
+            flops=2 * rows * depth * heads * width,
+            transcendentals=0,
+            bytes_accessed=(rows * depth + heads * width * depth + heads * rows * width) * 2,
+        ),
+    )(out_grad, weight)
+
+
 def per_device(query_rows, key_rows, value_rows, out_grad, out_weight, text_length):
     devices = lax.axis_size("dp")
     tok_rows = query_rows.shape[1]
@@ -89,20 +117,16 @@
     def by_heads(array):
         return array[0].reshape(tok_rows, HEADS, HEAD_DIM)
 
-    both_streams = lax.all_gather(out_weight, "dp", axis=1, tiled=False)
-    stream = (lax.axis_index("dp") * tok_rows >= TXT).astype(jnp.int32)
-    stream_rows = lax.dynamic_index_in_dim(both_streams, stream, 0, keepdims=False)
+    slot_text = (jnp.arange(devices) * tok_rows < TXT)[:, None, None]
+    outgoing = jnp.where(slot_text, out_weight[0][None], out_weight[1][None])
+    stream_rows = lax.all_to_all(outgoing, "dp", split_axis=0, concat_axis=0, tiled=True)
     weight = lax.all_gather(stream_rows, "seq", axis=1, tiled=True)
 
     qkv = jnp.stack([by_heads(query_rows), by_heads(key_rows), by_heads(value_rows)])
     qkv_heads = lax.all_to_all(qkv, "dp", split_axis=2, concat_axis=1, tiled=True)
 
-    projected = jnp.einsum(
-        "te,kre->tkr", out_grad[0], weight, preferred_element_type=jnp.float32
-    )
-    grad_heads = lax.all_to_all(
-        projected.astype(jnp.bfloat16), "dp", split_axis=1, concat_axis=0, tiled=True
-    )
+    projected = project(out_grad[0], weight)
+    grad_heads = lax.all_to_all(projected, "dp", split_axis=0, concat_axis=0, tiled=True)
     total_rows = tok_rows * devices
     query_grad, key_grad, value_grad = attention_grads(
         qkv_heads[0].reshape(total_rows, HEAD_DIM),
@@ -111,10 +135,13 @@
         grad_heads.reshape(total_rows, HEAD_DIM),
         text_length,
     )
-    grads = jnp.stack([query_grad, key_grad, value_grad]).reshape(3, total_rows, 1, HEAD_DIM)
-    returned = lax.all_to_all(grads, "dp", split_axis=1, concat_axis=2, tiled=True)
-    returned = returned.reshape(3, 1, tok_rows, HEADS * HEAD_DIM)
-    return (returned[0], returned[1], returned[2])
+    returned = [
+        lax.all_to_all(
+            grad.reshape(total_rows, 1, HEAD_DIM), "dp", split_axis=0, concat_axis=1, tiled=True
+        ).reshape(1, tok_rows, HEADS * HEAD_DIM)
+        for grad in (query_grad, key_grad, value_grad)
+    ]
+    return tuple(returned)
 
 
 def solution(mesh):

time: 235 us -> 233 us (level); the launches traced: 233 us -> 229 us
  blocking collectives: 50 us -> 15.5 us
  matrix products: 19.5 us -> 0 us
  waiting for transfers between devices: 93.7 us -> 111 us
  Pallas kernels: 17.1 us -> 31.1 us
  starting transfers between devices: 11.7 us -> 21.3 us
  local copies, waits for them, and re-layouts: 25 us -> 31.1 us
    all_gather x1 -> x0, blocking collectives: 20.3 us -> none  [per_device(): both_streams = lax.all_gather(out_weight, 'dp', axis=1, tiled=False)]
    dot_general x1 -> x0, matrix products: 19.5 us -> none  [per_device(): jnp.einsum('te,kre->tkr', out_grad[0], weight, preferred_element_type=jnp...]
    all_to_all x1 -> x4, waiting for transfers between devices: 8.19 us -> 26.7 us  [the longest x3 19.4 us: per_device(): lax.all_to_all(grad.reshape(total_rows, 1, HEAD_DIM), 'dp', split_axis=0,...]
    all_gather x0 -> x1, local copies, waits for them, and re-layouts: none -> 14.7 us  [per_device(): weight = lax.all_gather(stream_rows, 'seq', axis=1, tiled=True)]
    all_to_all x1, blocking collectives: 29.6 us -> 15.5 us  [per_device(): lax.all_to_all(outgoing, 'dp', split_axis=0, concat_axis=0, tiled=True)]
    pallas_call x0 -> x1, Pallas kernels: none -> 14 us  [project(): pl.pallas_call(projection_kernel, grid=(heads,), in_specs=[pl.BlockSpec((...]
    all_to_all x1 -> x4, starting transfers between devices: 6.39 us -> 17.6 us  [the longest x3 11.2 us: per_device(): lax.all_to_all(grad.reshape(total_rows, 1, HEAD_DIM), 'dp', split_axis=0,...]
    reshape x1, local copies, waits for them, and re-layouts: 9.76 us -> 0.51 us  [per_device(): grad.reshape(total_rows, 1, HEAD_DIM)]
  transfers between devices with their start and end apart: 3 -> 6, of which waited for: 2 -> 5; matrix products, arithmetic and copies ran while one was open for 11% -> 12% of each run, Pallas kernels for 0% -> 6%
where the time goes in v2:
time: 233 us; the launch traced here: 229 us
  waiting for transfers between devices  111 us (48%)
  local copies, waits for them, and re-layouts  31.1 us (13%)
  Pallas kernels  31.1 us (13%)
  starting transfers between devices  21.3 us (9%)
  blocking collectives  15.5 us (7%)
  between operations  14.9 us (6%)
  other arithmetic  3.46 us (1%)
    all_gather x1, waiting for transfers between devices, per_device(): weight = lax.all_gather(stream_rows, 'seq', axis=1, tiled=True)  84.6 us
    all_to_all x3, waiting for transfers between devices, per_device(): lax.all_to_all(grad.reshape(total_rows, 1, HEAD_DIM), 'dp', split_axis=0,...  19.4 us
    pallas_call x1, Pallas kernels, attention_grads(): pl.pallas_call(attention_kernel, grid=(rows // block,), in_specs=[pl.Bloc...  17.1 us
    all_to_all x1, blocking collectives, per_device(): lax.all_to_all(outgoing, 'dp', split_axis=0, concat_axis=0, tiled=True)  15.5 us
    all_gather x1, local copies, waits for them, and re-layouts, per_device(): weight = lax.all_gather(stream_rows, 'seq', axis=1, tiled=True)  14.7 us
    pallas_call x1, Pallas kernels, project(): pl.pallas_call(projection_kernel, grid=(heads,), in_specs=[pl.BlockSpec((...  14 us
    all_to_all x3, starting transfers between devices, per_device(): lax.all_to_all(grad.reshape(total_rows, 1, HEAD_DIM), 'dp', split_axis=0,...  11.2 us
    unnamed x25, local copies, waits for them, and re-layouts  9.44 us
  transfers between devices with their start and end apart: 6, of which 5 were waited for; matrix products, arithmetic and copies ran while one was open for 12% of the time, Pallas kernels for 6%

profile of v2, /device:TPU:1, one launch (start us, length us, event | category | flops | bytes accessed | tf_op | source)
XLA Modules:
  0.0 228.7 jit_solution(9625391219910070614)
XLA Ops:
  8.3 15.5 %all_to_all.70 = bf16[16,4,3072]{2,1,0:T(4,128)(2,1)S(1)} all-to-all(bf16[16,4,3072]{2,1,0:T(4,128)(2,1)S(1)} %broadcast_select_fusion), channel_id=1, replica_groups=mesh['dp'=16,'seq'=32] {'dp'}, dimensions={0} | all-to-all | bytes 786432 | tf_op jit(solution)/shard_map/all_to_all | solution.py:122
  25.7 1.6 copy.47
  27.3 3.7 %all-to-all-start = ((bf16[3,128,16,128]{3,1,0,2:T(8,128)(2,1)}), bf16[3,128,16,128]{3,1,0,2:T(8,128)(2,1)S(1)}, u32[]{:S(2)}, u32[]{:S(2)}) async-start(bf16[3,128,16,128]{3,1,0,2:T(8,128)(2,1)} %copy.47), calls=%async_computation | async-start | bytes 3145728 | tf_op jit(solution)/shard_map/all_to_all | solution.py:126
  31.0 84.6 %all-gather.2.cloned.1.call-done = bf16[16,128,3072]{2,0,1:T(8,128)(2,1)} async-done(((bf16[16,4,3072]{2,0,1:T(8,128)(2,1)}), bf16[16,128,3072]{2,0,1:T(8,128)(2,1)}) %all-gather.2.cloned.1.call-update) | async-done | bytes 12582928 | tf_op jit(solution)/shard_map/all_gather | solution.py:123
  115.6 14.7 %copy.49.weight_ref = bf16[16,128,3072]{2,1,0:T(8,128)(2,1)} copy(bf16[16,128,3072]{2,0,1:T(8,128)(2,1)} %all-gather.2.cloned.1.call-done) | data formatting | bytes 25165824 | tf_op jit(solution)/shard_map/all_gather | solution.py:123
  130.3 14.0 %shard_map.85 = bf16[16,128,128]{2,1,0:T(8,128)(2,1)} custom-call(bf16[128,3072]{1,0:T(8,128)(2,1)} %bitcast.47, bf16[16,128,3072]{2,1,0:T(8,128)(2,1)} %copy.49.weight_ref), custom_call_target="tpu_custom_call" | custom-call | flops 1610612736 | bytes 13893632 | tf_op jit(solution)/shard_map/pallas_call | solution.py:95
  144.3 6.4 %all-to-all-start.2 = ((bf16[16,128,128]{2,1,0:T(8,128)(2,1)}), bf16[16,128,128]{2,1,0:T(8,128)(2,1)S(1)}, u32[]{:S(2)}, u32[]{:S(2)}) async-start(bf16[16,128,128]{2,1,0:T(8,128)(2,1)} %shard_map.85), calls=%async_computation.2 | async-start | bytes 1048576 | tf_op jit(solution)/shard_map/all_to_all | solution.py:129
  151.4 2.3 %fusion = (bf16[1,16,128,1,128]{4,2,0,1,3:T(8,128)(2,1)S(1)}, bf16[1,16,128,1,128]{4,2,0,1,3:T(8,128)(2,1)S(1)}, bf16[1,16,128,1,128]{4,2,0,1,3:T(8,128)(2,1)}) fusion(bf16[3,16,128,1,128]{4,2,0,1,3:T(8,128)(2,1)} %bitcast.37), kind=kLoop, calls=%fused_computation.5 | loop fusion | bytes 3145728 | tf_op jit(solution)/shard_map/slice | solution.py:134
  153.7 7.4 %all-to-all-done.2 = bf16[16,128,128]{2,1,0:T(8,128)(2,1)S(1)} async-done(((bf16[16,128,128]{2,1,0:T(8,128)(2,1)}), bf16[16,128,128]{2,1,0:T(8,128)(2,1)S(1)}, u32[]{:S(2)}, u32[]{:S(2)}) %all-to-all-start.2) | async-done | bytes 524320 | tf_op jit(solution)/shard_map/all_to_all | solution.py:129
  161.1 1.0 copy-done
  162.1 17.1 %shard_map.86 = (bf16[2048,128]{1,0:T(8,128)(2,1)S(1)}, bf16[2048,128]{1,0:T(8,128)(2,1)S(1)}, bf16[2048,128]{1,0:T(8,128)(2,1)S(1)}) custom-call(s32[1]{0:T(128)S(6)} %copy.65.length_ref, bf16[2048,128]{1,0:T(8,128)(2,1)S(1)} %bitcast.36, bf16[2048,128]{1,0:T(8,128)(2,1)S(1)} %bitcast.35, bf16[2048,128]{1,0:T(8,128)(2,1)S(1)} %bitcast.34, ...), custom_call_target="tpu_custom_call" | custom-call | flops 5368709120 | bytes 3670016 | tf_op jit(solution)/shard_map/pallas_call | solution.py:60
  179.7 1.0 reduce
  181.7 3.9 %all-to-all-start.3 = ((bf16[16,2,8192]{2,1,0:T(2,128)(2,1)}), bf16[16,2,8192]{2,1,0:T(2,128)(2,1)S(1)}, u32[]{:S(2)}, u32[]{:S(2)}) async-start(bf16[16,2,8192]{2,1,0:T(2,128)(2,1)} %reshape.48), calls=%async_computation.3 | async-start | bytes 1048576 | tf_op jit(solution)/shard_map/all_to_all | solution.py:139
  185.6 1.0 reduce.1
  187.5 7.2 %all-to-all-done.3 = bf16[16,2,8192]{2,1,0:T(2,128)(2,1)S(1)} async-done(((bf16[16,2,8192]{2,1,0:T(2,128)(2,1)}), bf16[16,2,8192]{2,1,0:T(2,128)(2,1)S(1)}, u32[]{:S(2)}, u32[]{:S(2)}) %all-to-all-start.3) | async-done | bytes 524320 | tf_op jit(solution)/shard_map/all_to_all | solution.py:139
  194.8 3.7 %all-to-all-start.4 = ((bf16[16,2,8192]{2,1,0:T(2,128)(2,1)}), bf16[16,2,8192]{2,1,0:T(2,128)(2,1)S(1)}, u32[]{:S(2)}, u32[]{:S(2)}) async-start(bf16[16,2,8192]{2,1,0:T(2,128)(2,1)} %reshape.50), calls=%async_computation.4 | async-start | bytes 1048576 | tf_op jit(solution)/shard_map/all_to_all | solution.py:139
  198.5 1.0 reduce.2
  199.5 0.9 reshape.52
  200.4 7.0 %all-to-all-done.4 = bf16[16,2,8192]{2,1,0:T(2,128)(2,1)S(1)} async-done(((bf16[16,2,8192]{2,1,0:T(2,128)(2,1)}), bf16[16,2,8192]{2,1,0:T(2,128)(2,1)S(1)}, u32[]{:S(2)}, u32[]{:S(2)}) %all-to-all-start.4) | async-done | bytes 524320 | tf_op jit(solution)/shard_map/all_to_all | solution.py:139
  207.4 3.6 %all-to-all-start.5 = ((bf16[16,2,8192]{2,1,0:T(2,128)(2,1)}), bf16[16,2,8192]{2,1,0:T(2,128)(2,1)S(1)}, u32[]{:S(2)}, u32[]{:S(2)}) async-start(bf16[16,2,8192]{2,1,0:T(2,128)(2,1)} %reshape.52), calls=%async_computation.5 | async-start | bytes 1048576 | tf_op jit(solution)/shard_map/all_to_all | solution.py:139
  211.9 1.0 copy.56
  213.8 1.0 copy.57
  214.8 5.1 %all-to-all-done.5 = bf16[16,2,8192]{2,1,0:T(2,128)(2,1)S(1)} async-done(((bf16[16,2,8192]{2,1,0:T(2,128)(2,1)}), bf16[16,2,8192]{2,1,0:T(2,128)(2,1)S(1)}, u32[]{:S(2)}, u32[]{:S(2)}) %all-to-all-start.5) | async-done | bytes 524320 | tf_op jit(solution)/shard_map/all_to_all | solution.py:139
  220.8 1.0 copy.58
  (32 shorter events, 7.9 us)
Async XLA Ops:
  7.2 17.5 %copy-start.2 = (bf16[1,128,2048]{2,1,0:T(8,128)(2,1)S(1)}, bf16[1,128,2048]{2,1,0:T(8,128)(2,1)}, u32[]{:S(2)}) copy-start(bf16[1,128,2048]{2,1,0:T(8,128)(2,1)} %param.6) | copy-start | bytes 1572868
  7.2 108.4 %all-gather.2.cloned.1.call-start = ((), (), s32[]{:S(2)}) async-start(), calls=%async_computation.6 | async-start | bytes 12976128 | tf_op jit(solution)/shard_map/all_gather | solution.py:123
  8.3 16.7 %copy-start.3 = (bf16[1,128,2048]{2,1,0:T(8,128)(2,1)S(1)}, bf16[1,128,2048]{2,1,0:T(8,128)(2,1)}, u32[]{:S(2)}) copy-start(bf16[1,128,2048]{2,1,0:T(8,128)(2,1)} %param.7) | copy-start | bytes 1572868
  23.8 1.5 copy-start.4
  27.3 117.0 %all-to-all-start = ((bf16[3,128,16,128]{3,1,0,2:T(8,128)(2,1)}), bf16[3,128,16,128]{3,1,0,2:T(8,128)(2,1)S(1)}, u32[]{:S(2)}, u32[]{:S(2)}) async-start(bf16[3,128,16,128]{3,1,0,2:T(8,128)(2,1)} %copy.47), calls=%async_computation | async-start | bytes 3145728 | tf_op jit(solution)/shard_map/all_to_all | solution.py:126
  144.3 7.1 %copy-start.1 = (bf16[3,128,16,128]{3,1,0,2:T(8,128)(2,1)}, bf16[3,128,16,128]{3,1,0,2:T(8,128)(2,1)S(1)}, u32[]{:S(2)}) copy-start(bf16[3,128,16,128]{3,1,0,2:T(8,128)(2,1)S(1)} %all-to-all-done) | copy-start | bytes 4718596
  144.3 16.7 %all-to-all-start.2 = ((bf16[16,128,128]{2,1,0:T(8,128)(2,1)}), bf16[16,128,128]{2,1,0:T(8,128)(2,1)S(1)}, u32[]{:S(2)}, u32[]{:S(2)}) async-start(bf16[16,128,128]{2,1,0:T(8,128)(2,1)} %shard_map.85), calls=%async_computation.2 | async-start | bytes 1048576 | tf_op jit(solution)/shard_map/all_to_all | solution.py:129
  161.1 1.0 copy-start
  181.7 13.1 %all-to-all-start.3 = ((bf16[16,2,8192]{2,1,0:T(2,128)(2,1)}), bf16[16,2,8192]{2,1,0:T(2,128)(2,1)S(1)}, u32[]{:S(2)}, u32[]{:S(2)}) async-start(bf16[16,2,8192]{2,1,0:T(2,128)(2,1)} %reshape.48), calls=%async_computation.3 | async-start | bytes 1048576 | tf_op jit(solution)/shard_map/all_to_all | solution.py:139
  194.8 12.7 %all-to-all-start.4 = ((bf16[16,2,8192]{2,1,0:T(2,128)(2,1)}), bf16[16,2,8192]{2,1,0:T(2,128)(2,1)S(1)}, u32[]{:S(2)}, u32[]{:S(2)}) async-start(bf16[16,2,8192]{2,1,0:T(2,128)(2,1)} %reshape.50), calls=%async_computation.4 | async-start | bytes 1048576 | tf_op jit(solution)/shard_map/all_to_all | solution.py:139
  207.4 12.5 %all-to-all-start.5 = ((bf16[16,2,8192]{2,1,0:T(2,128)(2,1)}), bf16[16,2,8192]{2,1,0:T(2,128)(2,1)S(1)}, u32[]{:S(2)}, u32[]{:S(2)}) async-start(bf16[16,2,8192]{2,1,0:T(2,128)(2,1)} %reshape.52), calls=%async_computation.5 | async-start | bytes 1048576 | tf_op jit(solution)/shard_map/all_to_all | solution.py:139
Sparse Core Ops, SparseCore 0:
  24.8 90.7 all-gather.1

commit v3 on v1

--- a/solution.py
+++ b/solution.py
@@ -89,9 +89,9 @@
     def by_heads(array):
         return array[0].reshape(tok_rows, HEADS, HEAD_DIM)
 
-    both_streams = lax.all_gather(out_weight, "dp", axis=1, tiled=False)
-    stream = (lax.axis_index("dp") * tok_rows >= TXT).astype(jnp.int32)
-    stream_rows = lax.dynamic_index_in_dim(both_streams, stream, 0, keepdims=False)
+    slot_text = (jnp.arange(devices) * tok_rows < TXT)[:, None, None]
+    outgoing = jnp.where(slot_text, out_weight[0][None], out_weight[1][None])
+    stream_rows = lax.all_to_all(outgoing, "dp", split_axis=0, concat_axis=0, tiled=True)
     weight = lax.all_gather(stream_rows, "seq", axis=1, tiled=True)
 
     qkv = jnp.stack([by_heads(query_rows), by_heads(key_rows), by_heads(value_rows)])
@@ -111,9 +111,9 @@
         grad_heads.reshape(total_rows, HEAD_DIM),
         text_length,
     )
-    grads = jnp.stack([query_grad, key_grad, value_grad]).reshape(3, total_rows, 1, HEAD_DIM)
-    returned = lax.all_to_all(grads, "dp", split_axis=1, concat_axis=2, tiled=True)
-    returned = returned.reshape(3, 1, tok_rows, HEADS * HEAD_DIM)
+    grads = jnp.stack([query_grad, key_grad, value_grad]).reshape(3, devices, tok_rows, HEAD_DIM)
+    returned = lax.all_to_all(grads, "dp", split_axis=1, concat_axis=1, tiled=True)
+    returned = returned.transpose(0, 2, 1, 3).reshape(3, 1, tok_rows, HEADS * HEAD_DIM)
     return (returned[0], returned[1], returned[2])
 
 

time: 235 us -> 197 us (0.84)
  matrix products: 19.5 us -> 6.46 us
  local copies, waits for them, and re-layouts: 25 us -> 14.5 us
  blocking collectives: 50 us -> 39.6 us
  waiting for transfers between devices: 93.7 us -> 91 us
    all_gather x1 -> x0, blocking collectives: 20.3 us -> none  [per_device(): both_streams = lax.all_gather(out_weight, 'dp', axis=1, tiled=False)]
    dot_general x1, matrix products: 19.5 us -> 6.46 us  [per_device(): jnp.einsum('te,kre->tkr', out_grad[0], weight, preferred_element_type=jnp...]
    all_to_all x1 -> x2, blocking collectives: 29.6 us -> 39.6 us  [the longest x1 24.1 us: per_device(): lax.all_to_all(grads, 'dp', split_axis=1, concat_axis=1, tiled=True)]
    reshape x1 -> x0, local copies, waits for them, and re-layouts: 9.76 us -> none  [per_device(): jnp.stack([query_grad, key_grad, value_grad])]
    slice x4 -> x1, local copies, waits for them, and re-layouts: 4.29 us -> 0.95 us  [per_device(): return (returned[0], returned[1], returned[2])]
    squeeze x3 -> x0, local copies, waits for them, and re-layouts: 3.05 us -> none  [per_device(): return (returned[0], returned[1], returned[2])]
    all_to_all x0 -> x2, local copies, waits for them, and re-layouts: none -> 2.77 us  [the longest x1 1.91 us: per_device(): lax.all_to_all(grads, 'dp', split_axis=1, concat_axis=1, tiled=True)]
    all_gather x1, waiting for transfers between devices: 85.5 us -> 82.8 us  [per_device(): weight = lax.all_gather(stream_rows, 'seq', axis=1, tiled=True)]
  transfers between devices with their start and end apart: 3 -> 3, of which waited for: 2 -> 2; matrix products, arithmetic and copies ran while one was open for 11% -> 7% of each run, Pallas kernels for 0% -> 0%
where the time goes in v3:
time: 197 us; the launch traced here: 195 us
  waiting for transfers between devices  91 us (46%)
  blocking collectives  39.6 us (20%)
  Pallas kernels  17.1 us (9%)
  between operations  14.8 us (8%)
  local copies, waits for them, and re-layouts  14.5 us (7%)
  starting transfers between devices  10.2 us (5%)
  matrix products  6.46 us (3%)
    all_gather x1, waiting for transfers between devices, per_device(): weight = lax.all_gather(stream_rows, 'seq', axis=1, tiled=True)  82.8 us
    all_to_all x1, blocking collectives, per_device(): lax.all_to_all(grads, 'dp', split_axis=1, concat_axis=1, tiled=True)  24.1 us
    pallas_call x1, Pallas kernels, attention_grads(): pl.pallas_call(attention_kernel, grid=(rows // block,), in_specs=[pl.Bloc...  17.1 us
    all_to_all x1, blocking collectives, per_device(): lax.all_to_all(outgoing, 'dp', split_axis=0, concat_axis=0, tiled=True)  15.5 us
    all_to_all x1, waiting for transfers between devices, per_device(): lax.all_to_all(projected.astype(jnp.bfloat16), 'dp', split_axis=1, concat...  8.19 us
    dot_general x1, matrix products, per_device(): jnp.einsum('te,kre->tkr', out_grad[0], weight, preferred_element_type=jnp...  6.46 us
    all_to_all x1, starting transfers between devices, per_device(): lax.all_to_all(projected.astype(jnp.bfloat16), 'dp', split_axis=1, concat...  6.39 us
    unnamed x16, local copies, waits for them, and re-layouts  5.62 us
  transfers between devices with their start and end apart: 3, of which 2 were waited for; matrix products, arithmetic and copies ran while one was open for 7% of the time, Pallas kernels for 0%

profile of v3, /device:TPU:1, one launch (start us, length us, event | category | flops | bytes accessed | tf_op | source)
XLA Modules:
  0.0 195.3 jit_solution(3146690100017337117)
XLA Ops:
  7.2 0.9 slice_bitcast_fusion.1
  8.1 0.2 broadcast_select_fusion
  8.4 15.5 %all_to_all.40 = bf16[16,4,3072]{2,1,0:T(4,128)(2,1)S(1)} all-to-all(bf16[16,4,3072]{2,1,0:T(4,128)(2,1)S(1)} %broadcast_select_fusion), channel_id=1, replica_groups=mesh['dp'=16,'seq'=32] {'dp'}, dimensions={0} | all-to-all | bytes 786432 | tf_op jit(solution)/shard_map/all_to_all | solution.py:94
  23.9 0.9 copy.37
  24.8 0.3 copy.33
  25.0 0.3 copy.34
  25.3 1.0 copy.35
  26.3 1.2 pad_maximum_fusion
  27.5 1.6 copy.36
  29.1 3.7 %all-to-all-start = ((bf16[3,128,16,128]{3,1,0,2:T(8,128)(2,1)}), bf16[3,128,16,128]{3,1,0,2:T(8,128)(2,1)S(1)}, u32[]{:S(2)}, u32[]{:S(2)}) async-start(bf16[3,128,16,128]{3,1,0,2:T(8,128)(2,1)} %copy.36), calls=%async_computation | async-start | bytes 3145728 | tf_op jit(solution)/shard_map/all_to_all | solution.py:98
  32.9 82.8 %all-gather.2.cloned.1.call-done = bf16[16,128,3072]{2,0,1:T(8,128)(2,1)} async-done(((bf16[16,4,3072]{2,0,1:T(8,128)(2,1)}), bf16[16,128,3072]{2,0,1:T(8,128)(2,1)}) %all-gather.2.cloned.1.call-update) | async-done | bytes 12582928 | tf_op jit(solution)/shard_map/all_gather | solution.py:95
  115.7 6.5 %fusion = bf16[128,16,128]{0,1,2:T(8,128)(2,1)S(1)} fusion(bf16[16,128,3072]{2,0,1:T(8,128)(2,1)} %all-gather.2.cloned.1.call-done, bf16[1,128,3072]{2,1,0:T(8,128)(2,1)S(1)} %copy-done), kind=kOutput, calls=%fused_computation.3 | convolution fusion | flops 1610874880 | bytes 13893632 | tf_op jit(solution)/shard_map/te,kre->tkr/dot_general | solution.py:100
  122.1 0.9 copy.38
  123.1 6.4 %all-to-all-start.2 = ((bf16[128,16,128]{0,2,1:T(8,128)(2,1)}), bf16[128,16,128]{0,2,1:T(8,128)(2,1)S(1)}, u32[]{:S(2)}, u32[]{:S(2)}) async-start(bf16[128,16,128]{0,2,1:T(8,128)(2,1)} %copy.38), calls=%async_computation.2 | async-start | bytes 1048576 | tf_op jit(solution)/shard_map/all_to_all | solution.py:103
  130.1 1.5 fusion.3
  131.6 8.2 %all-to-all-done.2 = bf16[128,16,128]{0,2,1:T(8,128)(2,1)S(1)} async-done(((bf16[128,16,128]{0,2,1:T(8,128)(2,1)}), bf16[128,16,128]{0,2,1:T(8,128)(2,1)S(1)}, u32[]{:S(2)}, u32[]{:S(2)}) %all-to-all-start.2) | async-done | bytes 524320 | tf_op jit(solution)/shard_map/all_to_all | solution.py:103
  139.8 0.3 copy.39
  140.1 17.1 %shard_map.85 = (bf16[2048,128]{1,0:T(8,128)(2,1)S(1)}, bf16[2048,128]{1,0:T(8,128)(2,1)S(1)}, bf16[2048,128]{1,0:T(8,128)(2,1)S(1)}) custom-call(s32[1]{0:T(128)S(6)} %copy.47.length_ref, bf16[2048,128]{1,0:T(8,128)(2,1)S(1)} %bitcast.40, bf16[2048,128]{1,0:T(8,128)(2,1)S(1)} %bitcast.39, bf16[2048,128]{1,0:T(8,128)(2,1)S(1)} %bitcast.38, ...), custom_call_target="tpu_custom_call" | custom-call | flops 5368709120 | bytes 3670016 | tf_op jit(solution)/shard_map/pallas_call | solution.py:60
  157.4 24.1 %all_to_all.41 = bf16[3,16,128,128]{3,2,0,1:T(8,128)(2,1)} all-to-all(bf16[3,16,128,128]{3,2,0,1:T(8,128)(2,1)S(1)} %pad_maximum_fusion.1), channel_id=1, replica_groups=mesh['dp'=16,'seq'=32] {'dp'}, dimensions={1} | all-to-all | bytes 3145728 | tf_op jit(solution)/shard_map/all_to_all | solution.py:115
  181.5 1.9 copy.43
  183.4 0.9 fusion.2
  184.4 2.0 %copy.46 = bf16[1,128,2048]{2,1,0:T(8,128)(2,1)} copy(bf16[1,128,2048]{1,2,0:T(8,128)(2,1)} %bitcast.49) | data formatting | bytes 1048576
  186.4 1.0 copy.45
  187.4 1.0 copy.44
  (15 shorter events, 0.3 us)
Async XLA Ops:
  7.2 108.5 %copy-start = (bf16[1,128,3072]{2,1,0:T(8,128)(2,1)S(1)}, bf16[1,128,3072]{2,1,0:T(8,128)(2,1)}, u32[]{:S(2)}) copy-start(bf16[1,128,3072]{2,1,0:T(8,128)(2,1)} %param.9) | copy-start | bytes 2359300
  7.2 17.6 %copy-start.2 = (bf16[1,128,2048]{2,1,0:T(8,128)(2,1)S(1)}, bf16[1,128,2048]{2,1,0:T(8,128)(2,1)}, u32[]{:S(2)}) copy-start(bf16[1,128,2048]{2,1,0:T(8,128)(2,1)} %param.6) | copy-start | bytes 1572868
  7.2 108.5 %all-gather.2.cloned.1.call-start = ((), (), s32[]{:S(2)}) async-start(), calls=%async_computation.4 | async-start | bytes 12976128 | tf_op jit(solution)/shard_map/all_gather | solution.py:95
  8.3 16.7 %copy-start.3 = (bf16[1,128,2048]{2,1,0:T(8,128)(2,1)S(1)}, bf16[1,128,2048]{2,1,0:T(8,128)(2,1)}, u32[]{:S(2)}) copy-start(bf16[1,128,2048]{2,1,0:T(8,128)(2,1)} %param.7) | copy-start | bytes 1572868
  23.9 1.5 copy-start.4
  29.1 94.0 %all-to-all-start = ((bf16[3,128,16,128]{3,1,0,2:T(8,128)(2,1)}), bf16[3,128,16,128]{3,1,0,2:T(8,128)(2,1)S(1)}, u32[]{:S(2)}, u32[]{:S(2)}) async-start(bf16[3,128,16,128]{3,1,0,2:T(8,128)(2,1)} %copy.36), calls=%async_computation | async-start | bytes 3145728 | tf_op jit(solution)/shard_map/all_to_all | solution.py:98
  123.1 7.0 %copy-start.1 = (bf16[3,128,16,128]{3,1,0,2:T(8,128)(2,1)}, bf16[3,128,16,128]{3,1,0,2:T(8,128)(2,1)S(1)}, u32[]{:S(2)}) copy-start(bf16[3,128,16,128]{3,1,0,2:T(8,128)(2,1)S(1)} %all-to-all-done) | copy-start | bytes 4718596
  123.1 16.7 %all-to-all-start.2 = ((bf16[128,16,128]{0,2,1:T(8,128)(2,1)}), bf16[128,16,128]{0,2,1:T(8,128)(2,1)S(1)}, u32[]{:S(2)}, u32[]{:S(2)}) async-start(bf16[128,16,128]{0,2,1:T(8,128)(2,1)} %copy.38), calls=%async_computation.2 | async-start | bytes 1048576 | tf_op jit(solution)/shard_map/all_to_all | solution.py:103
Sparse Core Ops, SparseCore 0:
  24.9 90.7 all-gather.1

commit v4 on v3

--- a/solution.py
+++ b/solution.py
@@ -92,14 +92,37 @@
     slot_text = (jnp.arange(devices) * tok_rows < TXT)[:, None, None]
     outgoing = jnp.where(slot_text, out_weight[0][None], out_weight[1][None])
     stream_rows = lax.all_to_all(outgoing, "dp", split_axis=0, concat_axis=0, tiled=True)
-    weight = lax.all_gather(stream_rows, "seq", axis=1, tiled=True)
+
+    ring = 4
+    place = lax.axis_index("dp") % ring
+    near_rows = stream_rows[:, : HEAD_DIM // 32 - 1]
+    far_rows = lax.dynamic_slice_in_dim(
+        stream_rows[:, HEAD_DIM // 32 - 1 :], place * (HEADS // ring), HEADS // ring, axis=0
+    )
+    far_gathered = lax.all_gather(far_rows, "seq", axis=0, tiled=False)
+    near_rows, far_gathered = lax.optimization_barrier((near_rows, far_gathered))
+    near_gathered = lax.all_gather(near_rows, "seq", axis=0, tiled=False)
+    far_parts = [far_gathered]
+    for shift in range(1, ring):
+        pairs = [
+            (row * ring + col, row * ring + (col + shift) % ring)
+            for row in range(devices // ring)
+            for col in range(ring)
+        ]
+        far_parts.append(lax.ppermute(far_gathered, "dp", pairs))
+    far_parts = jnp.stack([far_parts[0]] + far_parts[:0:-1])
 
     qkv = jnp.stack([by_heads(query_rows), by_heads(key_rows), by_heads(value_rows)])
     qkv_heads = lax.all_to_all(qkv, "dp", split_axis=2, concat_axis=1, tiled=True)
 
-    projected = jnp.einsum(
-        "te,kre->tkr", out_grad[0], weight, preferred_element_type=jnp.float32
+    near_part = jnp.einsum(
+        "te,qhre->thqr", out_grad[0], near_gathered, preferred_element_type=jnp.float32
     )
+    far_part = jnp.einsum(
+        "te,kqjre->tkjqr", out_grad[0], far_parts, preferred_element_type=jnp.float32
+    )
+    far_part = jnp.roll(far_part, place, axis=1).reshape(tok_rows, HEADS, -1, 1)
+    projected = jnp.concatenate([near_part, far_part], axis=3).reshape(tok_rows, HEADS, HEAD_DIM)
     grad_heads = lax.all_to_all(
         projected.astype(jnp.bfloat16), "dp", split_axis=1, concat_axis=0, tiled=True
     )

time: 197 us -> 229 us (1.16)
  blocking collectives: 39.6 us -> 67.2 us
  waiting for transfers between devices: 91 us -> 66.7 us
  starting transfers between devices: 10.2 us -> 27.5 us
  other arithmetic: 1.59 us -> 7.17 us
  matrix products: 6.46 us -> 9.18 us
  local copies, waits for them, and re-layouts: 14.5 us -> 17.2 us
    all_gather x1, waiting for transfers between devices: 82.8 us -> 13.1 us  [per_device(): near_gathered = lax.all_gather(near_rows, 'seq', axis=0, tiled=False)]
    all_gather x0 -> x1, blocking collectives: none -> 43.1 us  [per_device(): far_gathered = lax.all_gather(far_rows, 'seq', axis=0, tiled=False)]
    ppermute x0 -> x3, waiting for transfers between devices: none -> 37.5 us  [per_device(): far_parts.append(lax.ppermute(far_gathered, 'dp', pairs))]
    all_to_all x1 -> x0, blocking collectives: 15.5 us -> none  [per_device(): lax.all_to_all(outgoing, 'dp', split_axis=0, concat_axis=0, tiled=True)]
    all_to_all x0 -> x1, waiting for transfers between devices: none -> 7.94 us  [per_device(): lax.all_to_all(outgoing, 'dp', split_axis=0, concat_axis=0, tiled=True)]
    ppermute x0 -> x3, starting transfers between devices: none -> 7.89 us  [per_device(): far_parts.append(lax.ppermute(far_gathered, 'dp', pairs))]
    all_to_all x0 -> x1, starting transfers between devices: none -> 7.58 us  [per_device(): lax.all_to_all(outgoing, 'dp', split_axis=0, concat_axis=0, tiled=True)]
    all_gather x0 -> x1, other arithmetic: none -> 4.71 us  [per_device(): far_gathered = lax.all_gather(far_rows, 'seq', axis=0, tiled=False)]
  transfers between devices with their start and end apart: 3 -> 7, of which waited for: 2 -> 6; matrix products, arithmetic and copies ran while one was open for 7% -> 8% of each run, Pallas kernels for 0% -> 0%
where the time goes in v4:
time: 229 us; the launch traced here: 227 us
  blocking collectives  67.2 us (29%)
  waiting for transfers between devices  66.7 us (29%)
  starting transfers between devices  27.5 us (12%)
  local copies, waits for them, and re-layouts  17.2 us (8%)
  Pallas kernels  17.1 us (7%)
  between operations  14.9 us (7%)
  matrix products  9.18 us (4%)
  other arithmetic  7.17 us (3%)
    all_gather x1, blocking collectives, per_device(): far_gathered = lax.all_gather(far_rows, 'seq', axis=0, tiled=False)  43.1 us
    ppermute x3, waiting for transfers between devices, per_device(): far_parts.append(lax.ppermute(far_gathered, 'dp', pairs))  37.5 us
    all_to_all x1, blocking collectives, per_device(): lax.all_to_all(grads, 'dp', split_axis=1, concat_axis=1, tiled=True)  24.1 us
    pallas_call x1, Pallas kernels, attention_grads(): pl.pallas_call(attention_kernel, grid=(rows // block,), in_specs=[pl.Bloc...  17.1 us
    all_gather x1, waiting for transfers between devices, per_device(): near_gathered = lax.all_gather(near_rows, 'seq', axis=0, tiled=False)  13.1 us
    all_to_all x1, waiting for transfers between devices, per_device(): lax.all_to_all(projected.astype(jnp.bfloat16), 'dp', split_axis=1, concat...  8.19 us
    all_to_all x1, waiting for transfers between devices, per_device(): lax.all_to_all(outgoing, 'dp', split_axis=0, concat_axis=0, tiled=True)  7.94 us
    ppermute x3, starting transfers between devices, per_device(): far_parts.append(lax.ppermute(far_gathered, 'dp', pairs))  7.89 us
  transfers between devices with their start and end apart: 7, of which 6 were waited for; matrix products, arithmetic and copies ran while one was open for 8% of the time, Pallas kernels for 0%

profile of v4, /device:TPU:1, one launch (start us, length us, event | category | flops | bytes accessed | tf_op | source)
XLA Modules:
  0.0 227.0 jit_solution(11987698278804450184)
XLA Ops:
  9.0 7.6 %all-to-all-start.1 = ((bf16[16,4,3072]{2,1,0:T(4,128)(2,1)}), bf16[16,4,3072]{2,1,0:T(4,128)(2,1)S(1)}, u32[]{:S(2)}, u32[]{:S(2)}) async-start(bf16[16,4,3072]{2,1,0:T(4,128)(2,1)} %broadcast_select_fusion), calls=%async_computation.1 | async-start | bytes 786432 | tf_op jit(solution)/shard_map/all_to_all | solution.py:94
  16.7 7.9 %all-to-all-done.1 = bf16[16,4,3072]{2,1,0:T(4,128)(2,1)S(1)} async-done(((bf16[16,4,3072]{2,1,0:T(4,128)(2,1)}), bf16[16,4,3072]{2,1,0:T(4,128)(2,1)S(1)}, u32[]{:S(2)}, u32[]{:S(2)}) %all-to-all-start.1) | async-done | bytes 393248 | tf_op jit(solution)/shard_map/all_to_all | solution.py:94
  24.9 43.1 %all-gather = bf16[128,1,3072]{2,1,0:T(2,128)(2,1)S(1)} all-gather(bf16[4,1,3072]{2,1,0:T(2,128)(2,1)S(1)} %constant_dynamic-slice_fusion), channel_id=2, replica_groups=mesh['dp'=16,'seq'=32] {'seq'}, dimensions={0}, use_global_device_ids=true | all-gather | bytes 811008 | tf_op jit(solution)/shard_map/all_gather | solution.py:102
  68.0 4.7 %reduce = bf16[128,3072]{1,0:T(8,128)(2,1)S(1)} reduce(bf16[128,1,3072]{2,1,0:T(2,128)(2,1)S(1)} %all-gather, bf16[]{:T(256)} %constant.48), dimensions={1}, to_apply=%all-gather.reduce_sub_computation | reduce | bytes 1572866 | tf_op jit(solution)/shard_map/all_gather | solution.py:102
  75.0 2.7 %collective-permute-start = (bf16[32,4,1,3072]{3,0,1,2:T(8,128)(2,1)}, bf16[32,4,1,3072]{3,0,1,2:T(8,128)(2,1)}, u32[]{:S(2)}, u32[]{:S(2)}) collective-permute-start(bf16[32,4,1,3072]{3,0,1,2:T(8,128)(2,1)} %copy.74), channel_id=1, source_target_pairs={{0,96},{32,0},{64,32},{96,64},{128,224},{160,128},{192,160},{224,1... | collective-permute-start | bytes 2359304 | tf_op jit(solution)/shard_map/ppermute | solution.py:112
  77.7 3.1 %collective-permute-start.1 = (bf16[32,4,1,3072]{3,0,1,2:T(8,128)(2,1)}, bf16[32,4,1,3072]{3,0,1,2:T(8,128)(2,1)}, u32[]{:S(2)}, u32[]{:S(2)}) collective-permute-start(bf16[32,4,1,3072]{3,0,1,2:T(8,128)(2,1)} %copy.74), channel_id=1, source_target_pairs={{0,64},{32,96},{64,0},{96,32},{128,192},{160,224},{192,128},{224,1... | collective-permute-start | bytes 2359304 | tf_op jit(solution)/shard_map/ppermute | solution.py:112
  80.8 2.1 collective-permute-start.2
  83.2 1.3 copy.45
  86.7 1.6 copy.47
  88.3 5.2 %all-to-all-start = ((bf16[3,128,16,128]{3,1,0,2:T(8,128)(2,1)}), bf16[3,128,16,128]{3,1,0,2:T(8,128)(2,1)S(1)}, u32[]{:S(2)}, u32[]{:S(2)}) async-start(bf16[3,128,16,128]{3,1,0,2:T(8,128)(2,1)} %copy.47), calls=%async_computation | async-start | bytes 3145728 | tf_op jit(solution)/shard_map/all_to_all | solution.py:116
  93.5 2.8 %collective-permute-done = bf16[32,4,1,3072]{3,0,1,2:T(8,128)(2,1)} collective-permute-done((bf16[32,4,1,3072]{3,0,1,2:T(8,128)(2,1)}, bf16[32,4,1,3072]{3,0,1,2:T(8,128)(2,1)}, u32[]{:S(2)}, u32[]{:S(2)}) %collective-permute-start) | collective-permute-done | bytes 786464 | tf_op jit(solution)/shard_map/ppermute | solution.py:112
  96.3 3.8 %collective-permute-done.1 = bf16[32,4,1,3072]{3,0,1,2:T(8,128)(2,1)} collective-permute-done((bf16[32,4,1,3072]{3,0,1,2:T(8,128)(2,1)}, bf16[32,4,1,3072]{3,0,1,2:T(8,128)(2,1)}, u32[]{:S(2)}, u32[]{:S(2)}) %collective-permute-start.1) | collective-permute-done | bytes 786464 | tf_op jit(solution)/shard_map/ppermute | solution.py:112
  100.1 30.8 %collective-permute-done.2 = bf16[32,4,1,3072]{3,0,1,2:T(8,128)(2,1)} collective-permute-done((bf16[32,4,1,3072]{3,0,1,2:T(8,128)(2,1)}, bf16[32,4,1,3072]{3,0,1,2:T(8,128)(2,1)}, u32[]{:S(2)}, u32[]{:S(2)}) %collective-permute-start.2) | collective-permute-done | bytes 786464 | tf_op jit(solution)/shard_map/ppermute | solution.py:112
  131.0 2.9 %fusion.15 = bf16[128,4,4,32,1]{0,3,2,1,4:T(8,128)(2,1)S(1)} fusion(bf16[1,32,4,1,3072]{4,1,2,0,3:T(8,128)(2,1)} %bitcast.19, bf16[1,32,4,1,3072]{4,1,2,0,3:T(8,128)(2,1)} %bitcast.18, bf16[1,32,4,1,3072]{4,1,2,0,3:T(8,128)(2,1)} %bitcast.17, bf16[1,32,4,1,3072]{4,1,2,0,3:T(8,128)(2,1)} %bitcast.59, bf16[1,128,3072]{2,1,0:T(8,128)(2,1)S(1)} %copy-done), kind=kOutput, calls=%fused_computation.14 | convolution fusion | flops 407371776 | bytes 4063232 | tf_op jit(solution)/shard_map/te,kqjre->tkjqr/dot_general | solution.py:121
  134.0 13.1 %all-gather.4.cloned.1.call-done = bf16[512,3,3072]{2,0,1:T(8,128)(2,1)} async-done(((bf16[16,3,3072]{2,0,1:T(8,128)(2,1)}), bf16[512,3,3072]{2,0,1:T(8,128)(2,1)}) %all-gather.4.cloned.1.call-update) | async-done | bytes 9437200 | tf_op jit(solution)/shard_map/all_gather | solution.py:104
  147.1 6.3 %fusion.12 = bf16[128,16,32,3]{0,1,3,2:T(8,128)(2,1)S(1)} fusion(bf16[32,16,3,3072]{3,1,0,2:T(8,128)(2,1)} %bitcast.79, bf16[1,128,3072]{2,1,0:T(8,128)(2,1)S(1)} %copy-done), kind=kOutput, calls=%fused_computation.13 | convolution fusion | flops 1208156160 | bytes 10616832 | tf_op jit(solution)/shard_map/te,qhre->thqr/dot_general | solution.py:118
  153.5 1.2 copy.55
  154.7 6.8 %all-to-all-start.2 = ((bf16[128,16,128]{2,0,1:T(8,128)(2,1)}), bf16[128,16,128]{2,0,1:T(8,128)(2,1)S(1)}, u32[]{:S(2)}, u32[]{:S(2)}) async-start(bf16[128,16,128]{2,0,1:T(8,128)(2,1)} %copy.55), calls=%async_computation.2 | async-start | bytes 1048576 | tf_op jit(solution)/shard_map/all_to_all | solution.py:126
  162.2 1.5 fusion.22
  163.7 8.2 %all-to-all-done.2 = bf16[128,16,128]{2,0,1:T(8,128)(2,1)S(1)} async-done(((bf16[128,16,128]{2,0,1:T(8,128)(2,1)}), bf16[128,16,128]{2,0,1:T(8,128)(2,1)S(1)}, u32[]{:S(2)}, u32[]{:S(2)}) %all-to-all-start.2) | async-done | bytes 524320 | tf_op jit(solution)/shard_map/all_to_all | solution.py:126
  171.9 17.1 %shard_map.85 = (bf16[2048,128]{1,0:T(8,128)(2,1)S(1)}, bf16[2048,128]{1,0:T(8,128)(2,1)S(1)}, bf16[2048,128]{1,0:T(8,128)(2,1)S(1)}) custom-call(s32[1]{0:T(128)S(6)} %copy.75.length_ref, bf16[2048,128]{1,0:T(8,128)(2,1)S(1)} %bitcast.64, bf16[2048,128]{1,0:T(8,128)(2,1)S(1)} %bitcast.63, bf16[2048,128]{1,0:T(8,128)(2,1)S(1)} %bitcast.62, ...), custom_call_target="tpu_custom_call" | custom-call | flops 5368709120 | bytes 3670016 | tf_op jit(solution)/shard_map/pallas_call | solution.py:60
  189.2 24.1 %all_to_all.40 = bf16[3,16,128,128]{3,2,0,1:T(8,128)(2,1)} all-to-all(bf16[3,16,128,128]{3,2,0,1:T(8,128)(2,1)S(1)} %pad_maximum_fusion.1), channel_id=1, replica_groups=mesh['dp'=16,'seq'=32] {'dp'}, dimensions={1} | all-to-all | bytes 3145728 | tf_op jit(solution)/shard_map/all_to_all | solution.py:138
  213.3 1.9 copy.59
  216.1 2.0 copy.60
  (29 shorter events, 10.2 us)
Async XLA Ops:
  7.2 123.8 %copy-start = (bf16[1,128,3072]{2,1,0:T(8,128)(2,1)S(1)}, bf16[1,128,3072]{2,1,0:T(8,128)(2,1)}, u32[]{:S(2)}) copy-start(bf16[1,128,3072]{2,1,0:T(8,128)(2,1)} %param.9) | copy-start | bytes 2359300
  9.0 15.6 %all-to-all-start.1 = ((bf16[16,4,3072]{2,1,0:T(4,128)(2,1)}), bf16[16,4,3072]{2,1,0:T(4,128)(2,1)S(1)}, u32[]{:S(2)}, u32[]{:S(2)}) async-start(bf16[16,4,3072]{2,1,0:T(4,128)(2,1)} %broadcast_select_fusion), calls=%async_computation.1 | async-start | bytes 786432 | tf_op jit(solution)/shard_map/all_to_all | solution.py:94
  16.6 130.6 %all-gather.4.cloned.1.call-start = ((), (), s32[]{:S(2)}) async-start(), calls=%async_computation.4 | async-start | bytes 9732096 | tf_op jit(solution)/shard_map/all_gather | solution.py:104
  73.0 9.9 %copy-start.2 = (bf16[1,128,2048]{2,1,0:T(8,128)(2,1)S(1)}, bf16[1,128,2048]{2,1,0:T(8,128)(2,1)}, u32[]{:S(2)}) copy-start(bf16[1,128,2048]{2,1,0:T(8,128)(2,1)} %param.6) | copy-start | bytes 1572868
  75.0 9.5 %copy-start.3 = (bf16[1,128,2048]{2,1,0:T(8,128)(2,1)S(1)}, bf16[1,128,2048]{2,1,0:T(8,128)(2,1)}, u32[]{:S(2)}) copy-start(bf16[1,128,2048]{2,1,0:T(8,128)(2,1)} %param.8) | copy-start | bytes 1572868
  75.0 21.3 %collective-permute-start = (bf16[32,4,1,3072]{3,0,1,2:T(8,128)(2,1)}, bf16[32,4,1,3072]{3,0,1,2:T(8,128)(2,1)}, u32[]{:S(2)}, u32[]{:S(2)}) collective-permute-start(bf16[32,4,1,3072]{3,0,1,2:T(8,128)(2,1)} %copy.74), channel_id=1, source_target_pairs={{0,96},{32,0},{64,32},{96,64},{128,224},{160,128},{192,160},{224,1... | collective-permute-start | bytes 2359304 | tf_op jit(solution)/shard_map/ppermute | solution.py:112
  77.7 22.4 %collective-permute-start.1 = (bf16[32,4,1,3072]{3,0,1,2:T(8,128)(2,1)}, bf16[32,4,1,3072]{3,0,1,2:T(8,128)(2,1)}, u32[]{:S(2)}, u32[]{:S(2)}) collective-permute-start(bf16[32,4,1,3072]{3,0,1,2:T(8,128)(2,1)} %copy.74), channel_id=1, source_target_pairs={{0,64},{32,96},{64,0},{96,32},{128,192},{160,224},{192,128},{224,1... | collective-permute-start | bytes 2359304 | tf_op jit(solution)/shard_map/ppermute | solution.py:112
  80.8 50.2 %collective-permute-start.2 = (bf16[32,4,1,3072]{3,0,1,2:T(8,128)(2,1)}, bf16[32,4,1,3072]{3,0,1,2:T(8,128)(2,1)}, u32[]{:S(2)}, u32[]{:S(2)}) collective-permute-start(bf16[32,4,1,3072]{3,0,1,2:T(8,128)(2,1)} %copy.74), channel_id=1, source_target_pairs={{0,32},{32,64},{64,96},{96,0},{128,160},{160,192},{192,224},{224,1... | collective-permute-start | bytes 2359304 | tf_op jit(solution)/shard_map/ppermute | solution.py:112
  88.3 66.4 %all-to-all-start = ((bf16[3,128,16,128]{3,1,0,2:T(8,128)(2,1)}), bf16[3,128,16,128]{3,1,0,2:T(8,128)(2,1)S(1)}, u32[]{:S(2)}, u32[]{:S(2)}) async-start(bf16[3,128,16,128]{3,1,0,2:T(8,128)(2,1)} %copy.47), calls=%async_computation | async-start | bytes 3145728 | tf_op jit(solution)/shard_map/all_to_all | solution.py:116
  154.7 7.5 %copy-start.1 = (bf16[3,128,16,128]{3,1,0,2:T(8,128)(2,1)}, bf16[3,128,16,128]{3,1,0,2:T(8,128)(2,1)S(1)}, u32[]{:S(2)}) copy-start(bf16[3,128,16,128]{3,1,0,2:T(8,128)(2,1)S(1)} %all-to-all-done) | copy-start | bytes 4718596
  154.7 17.2 %all-to-all-start.2 = ((bf16[128,16,128]{2,0,1:T(8,128)(2,1)}), bf16[128,16,128]{2,0,1:T(8,128)(2,1)S(1)}, u32[]{:S(2)}, u32[]{:S(2)}) async-start(bf16[128,16,128]{2,0,1:T(8,128)(2,1)} %copy.55), calls=%async_computation.2 | async-start | bytes 1048576 | tf_op jit(solution)/shard_map/all_to_all | solution.py:126
Sparse Core Ops, SparseCore 0:
  74.0 73.0 all-gather.3

commit v5 on v3

--- a/solution.py
+++ b/solution.py
@@ -14,7 +14,42 @@
 BLOCK_ROWS = 256
 
 
-def attention_kernel(length_ref, q_ref, k_ref, v_ref, g_ref, dq_ref, dk_ref, dv_ref, dkt_acc, dvt_acc):
+def softmax_kernel(length_ref, q_ref, k_ref, p_ref):
+    factor = 1.0 / math.sqrt(q_ref.shape[1])
+    nt = (((1,), (1,)), ((), ()))
+    scores = lax.dot_general(q_ref[...], k_ref[...], nt, preferred_element_type=jnp.float32) * factor
+    column = lax.broadcasted_iota(jnp.int32, scores.shape, 1)
+    valid = (column >= TXT) | (column < length_ref[0])
+    scores = jnp.where(valid, scores, -jnp.inf)
+    shifted = jnp.exp(scores - jnp.max(scores, axis=1, keepdims=True))
+    p_ref[...] = shifted / jnp.sum(shifted, axis=1, keepdims=True)
+
+
+def attention_probs(query, key, length):
+    rows, width = query.shape
+    block = min(BLOCK_ROWS, rows)
+    return pl.pallas_call(
+        softmax_kernel,
+        grid=(rows // block,),
+        in_specs=[
+            pl.BlockSpec(memory_space=pltpu.SMEM),
+            pl.BlockSpec((block, width), lambda i: (i, 0)),
+            pl.BlockSpec((rows, width), lambda i: (0, 0)),
+        ],
+        out_specs=pl.BlockSpec((block, rows), lambda i: (i, 0)),
+        out_shape=jax.ShapeDtypeStruct((rows, rows), jnp.float32),
+        compiler_params=pltpu.CompilerParams(
+            dimension_semantics=("arbitrary",), vmem_limit_bytes=48 * 1024 * 1024
+        ),
+        cost_estimate=pl.CostEstimate(
+            flops=2 * rows * rows * width,
+            transcendentals=rows * rows,
+            bytes_accessed=2 * rows * width * 2 + rows * rows * 4,
+        ),
+    )(length, query, key)
+
+
+def gradient_kernel(p_ref, q_ref, k_ref, v_ref, g_ref, dq_ref, dk_ref, dv_ref, dkt_acc, dvt_acc):
     step = pl.program_id(0)
     factor = 1.0 / math.sqrt(q_ref.shape[1])
     nt = (((1,), (1,)), ((), ()))
@@ -24,24 +59,17 @@
         dkt_acc[...] = jnp.zeros_like(dkt_acc)
         dvt_acc[...] = jnp.zeros_like(dvt_acc)
 
-    query_block = q_ref[...]
+    attention = p_ref[...]
     grad_block = g_ref[...]
     keys = k_ref[...]
-    values = v_ref[...]
-    scores = lax.dot_general(query_block, keys, nt, preferred_element_type=jnp.float32) * factor
-    column = lax.broadcasted_iota(jnp.int32, scores.shape, 1)
-    valid = (column >= TXT) | (column < length_ref[0])
-    scores = jnp.where(valid, scores, -jnp.inf)
-    shifted = jnp.exp(scores - jnp.max(scores, axis=1, keepdims=True))
-    attention = shifted / jnp.sum(shifted, axis=1, keepdims=True)
     attention_low = attention.astype(jnp.bfloat16)
     grad_t = grad_block.astype(jnp.float32).T.astype(jnp.bfloat16)
     dvt_acc[...] += jnp.dot(grad_t, attention_low, preferred_element_type=jnp.float32)
-    weight_grad = lax.dot_general(grad_block, values, nt, preferred_element_type=jnp.float32)
+    weight_grad = lax.dot_general(grad_block, v_ref[...], nt, preferred_element_type=jnp.float32)
     row_dot = jnp.sum(attention * weight_grad, axis=1, keepdims=True)
     score_grad = (attention * (weight_grad - row_dot) * factor).astype(jnp.bfloat16)
     dq_ref[...] = jnp.dot(score_grad, keys, preferred_element_type=jnp.float32).astype(dq_ref.dtype)
-    query_t = query_block.astype(jnp.float32).T.astype(jnp.bfloat16)
+    query_t = q_ref[...].astype(jnp.float32).T.astype(jnp.bfloat16)
     dkt_acc[...] += jnp.dot(query_t, score_grad, preferred_element_type=jnp.float32)
 
     @pl.when(step == pl.num_programs(0) - 1)
@@ -50,18 +78,19 @@
         dv_ref[...] = dvt_acc[...].T.astype(dv_ref.dtype)
 
 
-def attention_grads(query, key, value, grad, length):
+def attention_grads(query, key, value, grad, length, probs=None):
     rows, width = query.shape
+    if probs is None:
+        probs = attention_probs(query, key, length)
     block = min(BLOCK_ROWS, rows)
     row_spec = pl.BlockSpec((block, width), lambda i: (i, 0))
     full_spec = pl.BlockSpec((rows, width), lambda i: (0, 0))
     out = jax.ShapeDtypeStruct((rows, width), jnp.bfloat16)
-    flops = 10 * rows * rows * width
     return pl.pallas_call(
-        attention_kernel,
+        gradient_kernel,
         grid=(rows // block,),
         in_specs=[
-            pl.BlockSpec(memory_space=pltpu.SMEM),
+            pl.BlockSpec((block, rows), lambda i: (i, 0)),
             row_spec,
             full_spec,
             full_spec,
@@ -77,9 +106,11 @@
             dimension_semantics=("arbitrary",), vmem_limit_bytes=48 * 1024 * 1024
         ),
         cost_estimate=pl.CostEstimate(
-            flops=flops, transcendentals=rows * rows, bytes_accessed=7 * rows * width * 2
+            flops=8 * rows * rows * width,
+            transcendentals=0,
+            bytes_accessed=7 * rows * width * 2 + rows * rows * 4,
         ),
-    )(length, query, key, value, grad)
+    )(probs, query, key, value, grad)
 
 
 def per_device(query_rows, key_rows, value_rows, out_grad, out_weight, text_length):
@@ -104,12 +135,16 @@
         projected.astype(jnp.bfloat16), "dp", split_axis=1, concat_axis=0, tiled=True
     )
     total_rows = tok_rows * devices
+    query_heads = qkv_heads[0].reshape(total_rows, HEAD_DIM)
+    key_heads = qkv_heads[1].reshape(total_rows, HEAD_DIM)
+    probs = attention_probs(query_heads, key_heads, text_length)
     query_grad, key_grad, value_grad = attention_grads(
-        qkv_heads[0].reshape(total_rows, HEAD_DIM),
-        qkv_heads[1].reshape(total_rows, HEAD_DIM),
+        query_heads,
+        key_heads,
         qkv_heads[2].reshape(total_rows, HEAD_DIM),
         grad_heads.reshape(total_rows, HEAD_DIM),
         text_length,
+        probs,
     )
     grads = jnp.stack([query_grad, key_grad, value_grad]).reshape(3, devices, tok_rows, HEAD_DIM)
     returned = lax.all_to_all(grads, "dp", split_axis=1, concat_axis=1, tiled=True)

time: 197 us -> 198 us (level)
  waiting for transfers between devices: 91 us -> 82.8 us
  Pallas kernels: 17.1 us -> 23.3 us
  blocking collectives: 39.6 us -> 43.6 us
    all_to_all x1, waiting for transfers between devices: 8.19 us -> 0.01 us  [per_device(): lax.all_to_all(projected.astype(jnp.bfloat16), 'dp', split_axis=1, concat...]
    pallas_call x1 -> x2, Pallas kernels: 17.1 us -> 23.3 us  [the longest x1 13.2 us: attention_grads(): pl.pallas_call(gradient_kernel, grid=(rows // block,), in_specs=[pl.Block...]
    all_to_all x1, blocking collectives: 24.1 us -> 28.1 us  [per_device(): lax.all_to_all(grads, 'dp', split_axis=1, concat_axis=1, tiled=True)]
  transfers between devices with their start and end apart: 3 -> 3, of which waited for: 2 -> 1; matrix products, arithmetic and copies ran while one was open for 7% -> 7% of each run, Pallas kernels for 0% -> 5%
where the time goes in v5:
time: 198 us; the launch traced here: 197 us
  waiting for transfers between devices  82.8 us (42%)
  blocking collectives  43.6 us (22%)
  Pallas kernels  23.3 us (12%)
  between operations  14.8 us (7%)
  local copies, waits for them, and re-layouts  14.5 us (7%)
  starting transfers between devices  10.2 us (5%)
  matrix products  6.46 us (3%)
    all_gather x1, waiting for transfers between devices, per_device(): weight = lax.all_gather(stream_rows, 'seq', axis=1, tiled=True)  82.8 us
    all_to_all x1, blocking collectives, per_device(): lax.all_to_all(grads, 'dp', split_axis=1, concat_axis=1, tiled=True)  28.1 us
    all_to_all x1, blocking collectives, per_device(): lax.all_to_all(outgoing, 'dp', split_axis=0, concat_axis=0, tiled=True)  15.5 us
    pallas_call x1, Pallas kernels, attention_grads(): pl.pallas_call(gradient_kernel, grid=(rows // block,), in_specs=[pl.Block...  13.2 us
    pallas_call x1, Pallas kernels, attention_probs(): pl.pallas_call(softmax_kernel, grid=(rows // block,), in_specs=[pl.BlockS...  10.1 us
    dot_general x1, matrix products, per_device(): jnp.einsum('te,kre->tkr', out_grad[0], weight, preferred_element_type=jnp...  6.46 us
    all_to_all x1, starting transfers between devices, per_device(): lax.all_to_all(projected.astype(jnp.bfloat16), 'dp', split_axis=1, concat...  6.39 us
    unnamed x16, local copies, waits for them, and re-layouts  5.62 us
  transfers between devices with their start and end apart: 3, of which 1 were waited for; matrix products, arithmetic and copies ran while one was open for 7% of the time, Pallas kernels for 5%

profile of v5, /device:TPU:1, one launch (start us, length us, event | category | flops | bytes accessed | tf_op | source)
XLA Modules:
  0.0 197.2 jit_solution(3928892583053836891)
XLA Ops:
  7.2 0.9 slice_bitcast_fusion.1
  8.1 0.2 broadcast_select_fusion
  8.4 15.5 %all_to_all.40 = bf16[16,4,3072]{2,1,0:T(4,128)(2,1)S(1)} all-to-all(bf16[16,4,3072]{2,1,0:T(4,128)(2,1)S(1)} %broadcast_select_fusion), channel_id=1, replica_groups=mesh['dp'=16,'seq'=32] {'dp'}, dimensions={0} | all-to-all | bytes 786432 | tf_op jit(solution)/shard_map/all_to_all | solution.py:125
  23.9 0.9 copy.37
  24.8 0.3 copy.33
  25.0 0.3 copy.34
  25.3 1.0 copy.35
  26.3 1.2 pad_maximum_fusion
  27.5 1.6 copy.36
  29.1 3.7 %all-to-all-start = ((bf16[3,128,16,128]{3,1,0,2:T(8,128)(2,1)}), bf16[3,128,16,128]{3,1,0,2:T(8,128)(2,1)S(1)}, u32[]{:S(2)}, u32[]{:S(2)}) async-start(bf16[3,128,16,128]{3,1,0,2:T(8,128)(2,1)} %copy.36), calls=%async_computation | async-start | bytes 3145728 | tf_op jit(solution)/shard_map/all_to_all | solution.py:129
  32.9 82.8 %all-gather.2.cloned.1.call-done = bf16[16,128,3072]{2,0,1:T(8,128)(2,1)} async-done(((bf16[16,4,3072]{2,0,1:T(8,128)(2,1)}), bf16[16,128,3072]{2,0,1:T(8,128)(2,1)}) %all-gather.2.cloned.1.call-update) | async-done | bytes 12582928 | tf_op jit(solution)/shard_map/all_gather | solution.py:126
  115.7 6.5 %fusion = bf16[128,16,128]{0,1,2:T(8,128)(2,1)S(1)} fusion(bf16[16,128,3072]{2,0,1:T(8,128)(2,1)} %all-gather.2.cloned.1.call-done, bf16[1,128,3072]{2,1,0:T(8,128)(2,1)S(1)} %copy-done), kind=kOutput, calls=%fused_computation.3 | convolution fusion | flops 1610874880 | bytes 13893632 | tf_op jit(solution)/shard_map/te,kre->tkr/dot_general | solution.py:131
  122.1 0.9 copy.38
  123.1 6.4 %all-to-all-start.2 = ((bf16[128,16,128]{0,2,1:T(8,128)(2,1)}), bf16[128,16,128]{0,2,1:T(8,128)(2,1)S(1)}, u32[]{:S(2)}, u32[]{:S(2)}) async-start(bf16[128,16,128]{0,2,1:T(8,128)(2,1)} %copy.38), calls=%async_computation.2 | async-start | bytes 1048576 | tf_op jit(solution)/shard_map/all_to_all | solution.py:134
  130.1 1.5 fusion.3
  131.6 10.1 %shard_map.85.p_ref = f32[2048,2048]{1,0:T(8,128)} custom-call(s32[1]{0:T(128)S(6)} %copy.47.length_ref, bf16[2048,128]{1,0:T(8,128)(2,1)S(1)} %bitcast.39, bf16[2048,128]{1,0:T(8,128)(2,1)S(1)} %bitcast.37), custom_call_target="tpu_custom_call" | custom-call | flops 1073741824 | bytes 17825792 | tf_op jit(solution)/shard_map/pallas_call | solution.py:31
  141.7 0.3 copy.39
  141.9 13.2 %shard_map.86 = (bf16[2048,128]{1,0:T(8,128)(2,1)S(1)}, bf16[2048,128]{1,0:T(8,128)(2,1)S(1)}, bf16[2048,128]{1,0:T(8,128)(2,1)S(1)}) custom-call(f32[2048,2048]{1,0:T(8,128)} %shard_map.85.p_ref, bf16[2048,128]{1,0:T(8,128)(2,1)S(1)} %bitcast.40, bf16[2048,128]{1,0:T(8,128)(2,1)S(1)} %bitcast.38, bf16[2048,128]{1,0:T(8,128)(2,1)S(1)} %bitcast.42, ...), custom_call_target="tpu_custom_call" | custom-call | flops 4294967296 | bytes 20447232 | tf_op jit(solution)/shard_map/pallas_call | solution.py:89
  155.4 28.1 %all_to_all.41 = bf16[3,16,128,128]{3,2,0,1:T(8,128)(2,1)} all-to-all(bf16[3,16,128,128]{3,2,0,1:T(8,128)(2,1)S(1)} %pad_maximum_fusion.1), channel_id=1, replica_groups=mesh['dp'=16,'seq'=32] {'dp'}, dimensions={1} | all-to-all | bytes 3145728 | tf_op jit(solution)/shard_map/all_to_all | solution.py:150
  183.4 1.9 copy.43
  185.4 0.9 fusion.2
  186.3 2.0 %copy.46 = bf16[1,128,2048]{2,1,0:T(8,128)(2,1)} copy(bf16[1,128,2048]{1,2,0:T(8,128)(2,1)} %bitcast.51) | data formatting | bytes 1048576
  188.3 1.0 copy.45
  189.4 1.0 copy.44
  (16 shorter events, 0.3 us)
Async XLA Ops:
  7.2 108.5 %copy-start = (bf16[1,128,3072]{2,1,0:T(8,128)(2,1)S(1)}, bf16[1,128,3072]{2,1,0:T(8,128)(2,1)}, u32[]{:S(2)}) copy-start(bf16[1,128,3072]{2,1,0:T(8,128)(2,1)} %param.9) | copy-start | bytes 2359300
  7.2 17.6 %copy-start.2 = (bf16[1,128,2048]{2,1,0:T(8,128)(2,1)S(1)}, bf16[1,128,2048]{2,1,0:T(8,128)(2,1)}, u32[]{:S(2)}) copy-start(bf16[1,128,2048]{2,1,0:T(8,128)(2,1)} %param.6) | copy-start | bytes 1572868
  7.2 108.5 %all-gather.2.cloned.1.call-start = ((), (), s32[]{:S(2)}) async-start(), calls=%async_computation.4 | async-start | bytes 12976128 | tf_op jit(solution)/shard_map/all_gather | solution.py:126
  8.3 16.7 %copy-start.3 = (bf16[1,128,2048]{2,1,0:T(8,128)(2,1)S(1)}, bf16[1,128,2048]{2,1,0:T(8,128)(2,1)}, u32[]{:S(2)}) copy-start(bf16[1,128,2048]{2,1,0:T(8,128)(2,1)} %param.7) | copy-start | bytes 1572868
  23.9 1.5 copy-start.4
  29.1 94.0 %all-to-all-start = ((bf16[3,128,16,128]{3,1,0,2:T(8,128)(2,1)}), bf16[3,128,16,128]{3,1,0,2:T(8,128)(2,1)S(1)}, u32[]{:S(2)}, u32[]{:S(2)}) async-start(bf16[3,128,16,128]{3,1,0,2:T(8,128)(2,1)} %copy.36), calls=%async_computation | async-start | bytes 3145728 | tf_op jit(solution)/shard_map/all_to_all | solution.py:129
  123.1 7.0 %copy-start.1 = (bf16[3,128,16,128]{3,1,0,2:T(8,128)(2,1)}, bf16[3,128,16,128]{3,1,0,2:T(8,128)(2,1)S(1)}, u32[]{:S(2)}) copy-start(bf16[3,128,16,128]{3,1,0,2:T(8,128)(2,1)S(1)} %all-to-all-done) | copy-start | bytes 4718596
  123.1 18.6 %all-to-all-start.2 = ((bf16[128,16,128]{0,2,1:T(8,128)(2,1)}), bf16[128,16,128]{0,2,1:T(8,128)(2,1)S(1)}, u32[]{:S(2)}, u32[]{:S(2)}) async-start(bf16[128,16,128]{0,2,1:T(8,128)(2,1)} %copy.38), calls=%async_computation.2 | async-start | bytes 1048576 | tf_op jit(solution)/shard_map/all_to_all | solution.py:134
Sparse Core Ops, SparseCore 0:
  24.9 90.7 all-gather.1

commit v6 on v5

--- a/solution.py
+++ b/solution.py
@@ -123,14 +123,38 @@
     slot_text = (jnp.arange(devices) * tok_rows < TXT)[:, None, None]
     outgoing = jnp.where(slot_text, out_weight[0][None], out_weight[1][None])
     stream_rows = lax.all_to_all(outgoing, "dp", split_axis=0, concat_axis=0, tiled=True)
-    weight = lax.all_gather(stream_rows, "seq", axis=1, tiled=True)
+
+    ring = 4
+    near = 2
+    place = lax.axis_index("dp") % ring
+    near_rows = stream_rows[:, :near]
+    far_rows = lax.dynamic_slice_in_dim(
+        stream_rows[:, near:], place * (HEADS // ring), HEADS // ring, axis=0
+    )
+    far_gathered = lax.all_gather(far_rows, "seq", axis=0, tiled=False)
+    near_rows, far_gathered = lax.optimization_barrier((near_rows, far_gathered))
+    near_gathered = lax.all_gather(near_rows, "seq", axis=0, tiled=False)
+    far_parts = [far_gathered]
+    for shift in range(1, ring):
+        pairs = [
+            (row * ring + col, row * ring + (col + shift) % ring)
+            for row in range(devices // ring)
+            for col in range(ring)
+        ]
+        far_parts.append(lax.ppermute(far_gathered, "dp", pairs))
+    far_parts = jnp.stack([far_parts[0]] + far_parts[:0:-1])
 
     qkv = jnp.stack([by_heads(query_rows), by_heads(key_rows), by_heads(value_rows)])
     qkv_heads = lax.all_to_all(qkv, "dp", split_axis=2, concat_axis=1, tiled=True)
 
-    projected = jnp.einsum(
-        "te,kre->tkr", out_grad[0], weight, preferred_element_type=jnp.float32
+    near_part = jnp.einsum(
+        "te,qhre->thqr", out_grad[0], near_gathered, preferred_element_type=jnp.float32
     )
+    far_part = jnp.einsum(
+        "te,kqjre->tkjqr", out_grad[0], far_parts, preferred_element_type=jnp.float32
+    )
+    far_part = jnp.roll(far_part, place, axis=1).reshape(tok_rows, HEADS, far_part.shape[3], -1)
+    projected = jnp.concatenate([near_part, far_part], axis=3).reshape(tok_rows, HEADS, HEAD_DIM)
     grad_heads = lax.all_to_all(
         projected.astype(jnp.bfloat16), "dp", split_axis=1, concat_axis=0, tiled=True
     )

time: 198 us -> 277 us (1.40); the launches traced: 197 us -> 273 us
  waiting for transfers between devices: 82.8 us -> 151 us
  blocking collectives: 43.6 us -> 24.5 us
  starting transfers between devices: 10.2 us -> 28.4 us
  local copies, waits for them, and re-layouts: 14.5 us -> 19.1 us
    ppermute x0 -> x3, waiting for transfers between devices: none -> 69 us  [per_device(): far_parts.append(lax.ppermute(far_gathered, 'dp', pairs))]
    all_to_all x1 -> x0, blocking collectives: 15.5 us -> none  [per_device(): lax.all_to_all(outgoing, 'dp', split_axis=0, concat_axis=0, tiled=True)]
    ppermute x0 -> x3, starting transfers between devices: none -> 10 us  [per_device(): far_parts.append(lax.ppermute(far_gathered, 'dp', pairs))]
    all_gather x1 -> x2, waiting for transfers between devices: 82.8 us -> 74.4 us  [the longest x1 74.4 us: per_device(): far_gathered = lax.all_gather(far_rows, 'seq', axis=0, tiled=False)]
    all_to_all x0 -> x1, waiting for transfers between devices: none -> 7.94 us  [per_device(): lax.all_to_all(outgoing, 'dp', split_axis=0, concat_axis=0, tiled=True)]
    all_to_all x0 -> x1, starting transfers between devices: none -> 7.58 us  [per_device(): lax.all_to_all(outgoing, 'dp', split_axis=0, concat_axis=0, tiled=True)]
    optimization_barrier x0 -> x2, local copies, waits for them, and re-layouts: none -> 4.3 us  [per_device(): lax.optimization_barrier((near_rows, far_gathered))]
    all_to_all x1, blocking collectives: 28.1 us -> 24.5 us  [per_device(): lax.all_to_all(grads, 'dp', split_axis=1, concat_axis=1, tiled=True)]
  transfers between devices with their start and end apart: 3 -> 8, of which waited for: 1 -> 4; matrix products, arithmetic and copies ran while one was open for 7% -> 7% of each run, Pallas kernels for 5% -> 4%
where the time goes in v6:
time: 277 us; the launch traced here: 273 us
  waiting for transfers between devices  151 us (55%)
  starting transfers between devices  28.4 us (10%)
  blocking collectives  24.5 us (9%)
  Pallas kernels  23.3 us (8%)
  local copies, waits for them, and re-layouts  19.1 us (7%)
  between operations  14.9 us (5%)
  matrix products  8.44 us (3%)
    all_gather x1, waiting for transfers between devices, per_device(): far_gathered = lax.all_gather(far_rows, 'seq', axis=0, tiled=False)  74.4 us
    ppermute x3, waiting for transfers between devices, per_device(): far_parts.append(lax.ppermute(far_gathered, 'dp', pairs))  69 us
    all_to_all x1, blocking collectives, per_device(): lax.all_to_all(grads, 'dp', split_axis=1, concat_axis=1, tiled=True)  24.5 us
    pallas_call x1, Pallas kernels, attention_grads(): pl.pallas_call(gradient_kernel, grid=(rows // block,), in_specs=[pl.Block...  13.2 us
    pallas_call x1, Pallas kernels, attention_probs(): pl.pallas_call(softmax_kernel, grid=(rows // block,), in_specs=[pl.BlockS...  10.1 us
    ppermute x3, starting transfers between devices, per_device(): far_parts.append(lax.ppermute(far_gathered, 'dp', pairs))  10 us
    all_to_all x1, waiting for transfers between devices, per_device(): lax.all_to_all(outgoing, 'dp', split_axis=0, concat_axis=0, tiled=True)  7.94 us
    all_to_all x1, starting transfers between devices, per_device(): lax.all_to_all(outgoing, 'dp', split_axis=0, concat_axis=0, tiled=True)  7.58 us
  transfers between devices with their start and end apart: 8, of which 4 were waited for; matrix products, arithmetic and copies ran while one was open for 7% of the time, Pallas kernels for 4%

profile of v6, /device:TPU:1, one launch (start us, length us, event | category | flops | bytes accessed | tf_op | source)
XLA Modules:
  0.0 272.5 jit_solution(15979180993076294823)
XLA Ops:
  9.0 7.6 %all-to-all-start.1 = ((bf16[16,4,3072]{2,1,0:T(4,128)(2,1)}), bf16[16,4,3072]{2,1,0:T(4,128)(2,1)S(1)}, u32[]{:S(2)}, u32[]{:S(2)}) async-start(bf16[16,4,3072]{2,1,0:T(4,128)(2,1)} %broadcast_select_fusion), calls=%async_computation.1 | async-start | bytes 786432 | tf_op jit(solution)/shard_map/all_to_all | solution.py:125
  16.7 7.9 %all-to-all-done.1 = bf16[16,4,3072]{2,1,0:T(4,128)(2,1)S(1)} async-done(((bf16[16,4,3072]{2,1,0:T(4,128)(2,1)}), bf16[16,4,3072]{2,1,0:T(4,128)(2,1)S(1)}, u32[]{:S(2)}, u32[]{:S(2)}) %all-to-all-start.1) | async-done | bytes 393248 | tf_op jit(solution)/shard_map/all_to_all | solution.py:125
  26.3 74.4 %all-gather.5.cloned.1.call-done = bf16[128,2,3072]{2,1,0:T(2,128)(2,1)} async-done(((bf16[4,2,3072]{2,1,0:T(2,128)(2,1)}), bf16[128,2,3072]{2,1,0:T(2,128)(2,1)}) %all-gather.5.cloned.1.call-update) | async-done | bytes 1572880 | tf_op jit(solution)/shard_map/all_gather | solution.py:134
  100.8 3.6 %copy.72 = bf16[32,4,2,3072]{3,0,2,1:T(8,128)(2,1)} copy(bf16[32,4,2,3072]{3,2,1,0:T(2,128)(2,1)} %bitcast.76) | data formatting | bytes 3145728 | tf_op jit(solution)/shard_map/optimization_barrier | solution.py:135
  104.3 4.5 %collective-permute-start = (bf16[32,4,2,3072]{3,0,2,1:T(8,128)(2,1)}, bf16[32,4,2,3072]{3,0,2,1:T(8,128)(2,1)}, u32[]{:S(2)}, u32[]{:S(2)}) collective-permute-start(bf16[32,4,2,3072]{3,0,2,1:T(8,128)(2,1)} %copy.72), channel_id=1, source_target_pairs={{0,96},{32,0},{64,32},{96,64},{128,224},{160,128},{192,160},{224,1... | collective-permute-start | bytes 4718600 | tf_op jit(solution)/shard_map/ppermute | solution.py:144
  108.8 1.9 collective-permute-start.2
  110.8 3.6 %collective-permute-start.1 = (bf16[32,4,2,3072]{3,0,2,1:T(8,128)(2,1)}, bf16[32,4,2,3072]{3,0,2,1:T(8,128)(2,1)}, u32[]{:S(2)}, u32[]{:S(2)}) collective-permute-start(bf16[32,4,2,3072]{3,0,2,1:T(8,128)(2,1)} %copy.72), channel_id=1, source_target_pairs={{0,64},{32,96},{64,0},{96,32},{128,192},{160,224},{192,128},{224,1... | collective-permute-start | bytes 4718600 | tf_op jit(solution)/shard_map/ppermute | solution.py:144
  116.0 1.2 pad_maximum_fusion
  117.2 1.6 copy.45
  118.8 5.3 %all-to-all-start = ((bf16[3,128,16,128]{3,1,0,2:T(8,128)(2,1)}), bf16[3,128,16,128]{3,1,0,2:T(8,128)(2,1)S(1)}, u32[]{:S(2)}, u32[]{:S(2)}) async-start(bf16[3,128,16,128]{3,1,0,2:T(8,128)(2,1)} %copy.45), calls=%async_computation | async-start | bytes 3145728 | tf_op jit(solution)/shard_map/all_to_all | solution.py:148
  124.1 64.2 %collective-permute-done = bf16[32,4,2,3072]{3,0,2,1:T(8,128)(2,1)} collective-permute-done((bf16[32,4,2,3072]{3,0,2,1:T(8,128)(2,1)}, bf16[32,4,2,3072]{3,0,2,1:T(8,128)(2,1)}, u32[]{:S(2)}, u32[]{:S(2)}) %collective-permute-start) | collective-permute-done | bytes 1572896 | tf_op jit(solution)/shard_map/ppermute | solution.py:144
  188.3 4.8 %collective-permute-done.1 = bf16[32,4,2,3072]{3,0,2,1:T(8,128)(2,1)} collective-permute-done((bf16[32,4,2,3072]{3,0,2,1:T(8,128)(2,1)}, bf16[32,4,2,3072]{3,0,2,1:T(8,128)(2,1)}, u32[]{:S(2)}, u32[]{:S(2)}) %collective-permute-start.1) | collective-permute-done | bytes 1572896 | tf_op jit(solution)/shard_map/ppermute | solution.py:144
  193.1 3.9 %fusion.10 = bf16[128,4,4,32,2]{0,3,4,2,1:T(8,128)(2,1)S(1)} fusion(bf16[1,32,4,2,3072]{4,1,3,2,0:T(8,128)(2,1)} %bitcast.20, bf16[1,32,4,2,3072]{4,1,3,2,0:T(8,128)(2,1)} %bitcast.19, bf16[1,32,4,2,3072]{4,1,3,2,0:T(8,128)(2,1)} %bitcast.18, bf16[1,32,4,2,3072]{4,1,3,2,0:T(8,128)(2,1)} %bitcast.57, bf16[1,128,3072]{2,1,0:T(8,128)(2,1)S(1)} %copy-done), kind=kOutput, calls=%fused_computation.12 | convolution fusion | flops 814743552 | bytes 7340032 | tf_op jit(solution)/shard_map/te,kqjre->tkjqr/dot_general | solution.py:153
  197.4 4.6 %fusion.16 = bf16[128,16,32,2]{0,1,3,2:T(8,128)(2,1)S(1)} fusion(bf16[32,16,2,3072]{3,1,0,2:T(8,128)(2,1)} %bitcast.78, bf16[1,128,3072]{2,1,0:T(8,128)(2,1)S(1)} %copy-done), kind=kOutput, calls=%fused_computation.14 | convolution fusion | flops 805437440 | bytes 7340032 | tf_op jit(solution)/shard_map/te,qhre->thqr/dot_general | solution.py:150
  202.0 1.2 copy.53
  203.2 5.4 %all-to-all-start.2 = ((bf16[128,16,128]{2,0,1:T(8,128)(2,1)}), bf16[128,16,128]{2,0,1:T(8,128)(2,1)S(1)}, u32[]{:S(2)}, u32[]{:S(2)}) async-start(bf16[128,16,128]{2,0,1:T(8,128)(2,1)} %copy.53), calls=%async_computation.2 | async-start | bytes 1048576 | tf_op jit(solution)/shard_map/all_to_all | solution.py:158
  209.3 1.5 fusion.25
  210.7 10.1 %shard_map.85.p_ref = f32[2048,2048]{1,0:T(8,128)} custom-call(s32[1]{0:T(128)S(6)} %copy.73.length_ref, bf16[2048,128]{1,0:T(8,128)(2,1)S(1)} %bitcast.60, bf16[2048,128]{1,0:T(8,128)(2,1)S(1)} %bitcast.58), custom_call_target="tpu_custom_call" | custom-call | flops 1073741824 | bytes 17825792 | tf_op jit(solution)/shard_map/pallas_call | solution.py:31
  220.8 13.2 %shard_map.86 = (bf16[2048,128]{1,0:T(8,128)(2,1)S(1)}, bf16[2048,128]{1,0:T(8,128)(2,1)S(1)}, bf16[2048,128]{1,0:T(8,128)(2,1)S(1)}) custom-call(f32[2048,2048]{1,0:T(8,128)} %shard_map.85.p_ref, bf16[2048,128]{1,0:T(8,128)(2,1)S(1)} %bitcast.61, bf16[2048,128]{1,0:T(8,128)(2,1)S(1)} %bitcast.59, bf16[2048,128]{1,0:T(8,128)(2,1)S(1)} %bitcast.63, ...), custom_call_target="tpu_custom_call" | custom-call | flops 4294967296 | bytes 20447232 | tf_op jit(solution)/shard_map/pallas_call | solution.py:89
  234.2 24.5 %all_to_all.40 = bf16[3,16,128,128]{3,2,0,1:T(8,128)(2,1)} all-to-all(bf16[3,16,128,128]{3,2,0,1:T(8,128)(2,1)S(1)} %pad_maximum_fusion.1), channel_id=1, replica_groups=mesh['dp'=16,'seq'=32] {'dp'}, dimensions={1} | all-to-all | bytes 3145728 | tf_op jit(solution)/shard_map/all_to_all | solution.py:174
  258.8 1.9 copy.57
  261.6 2.0 copy.60
  263.7 1.0 copy.59
  264.7 1.0 copy.58
  (32 shorter events, 6.6 us)
Async XLA Ops:
  7.2 186.0 %copy-start = (bf16[1,128,3072]{2,1,0:T(8,128)(2,1)S(1)}, bf16[1,128,3072]{2,1,0:T(8,128)(2,1)}, u32[]{:S(2)}) copy-start(bf16[1,128,3072]{2,1,0:T(8,128)(2,1)} %param.9) | copy-start | bytes 2359300
  9.0 15.6 %all-to-all-start.1 = ((bf16[16,4,3072]{2,1,0:T(4,128)(2,1)}), bf16[16,4,3072]{2,1,0:T(4,128)(2,1)S(1)}, u32[]{:S(2)}, u32[]{:S(2)}) async-start(bf16[16,4,3072]{2,1,0:T(4,128)(2,1)} %broadcast_select_fusion), calls=%async_computation.1 | async-start | bytes 786432 | tf_op jit(solution)/shard_map/all_to_all | solution.py:125
  16.6 84.1 %all-gather.5.cloned.1.call-start = ((), (), s32[]{:S(2)}) async-start(), calls=%async_computation.4 | async-start | bytes 1622016 | tf_op jit(solution)/shard_map/all_gather | solution.py:134
  25.6 171.8 %all-gather.7.cloned.1.call-start = ((), (), s32[]{:S(2)}) async-start(), calls=%async_computation.5 | async-start | bytes 6488064 | tf_op jit(solution)/shard_map/all_gather | solution.py:136
  100.7 13.7 %copy-start.2 = (bf16[1,128,2048]{2,1,0:T(8,128)(2,1)S(1)}, bf16[1,128,2048]{2,1,0:T(8,128)(2,1)}, u32[]{:S(2)}) copy-start(bf16[1,128,2048]{2,1,0:T(8,128)(2,1)} %param.6) | copy-start | bytes 1572868
  100.7 14.0 %copy-start.3 = (bf16[1,128,2048]{2,1,0:T(8,128)(2,1)S(1)}, bf16[1,128,2048]{2,1,0:T(8,128)(2,1)}, u32[]{:S(2)}) copy-start(bf16[1,128,2048]{2,1,0:T(8,128)(2,1)} %param.7) | copy-start | bytes 1572868
  104.3 10.6 %copy-start.4 = (bf16[1,128,2048]{2,1,0:T(8,128)(2,1)S(1)}, bf16[1,128,2048]{2,1,0:T(8,128)(2,1)}, u32[]{:S(2)}) copy-start(bf16[1,128,2048]{2,1,0:T(8,128)(2,1)} %param.8) | copy-start | bytes 1572868
  104.3 84.0 %collective-permute-start = (bf16[32,4,2,3072]{3,0,2,1:T(8,128)(2,1)}, bf16[32,4,2,3072]{3,0,2,1:T(8,128)(2,1)}, u32[]{:S(2)}, u32[]{:S(2)}) collective-permute-start(bf16[32,4,2,3072]{3,0,2,1:T(8,128)(2,1)} %copy.72), channel_id=1, source_target_pairs={{0,96},{32,0},{64,32},{96,64},{128,224},{160,128},{192,160},{224,1... | collective-permute-start | bytes 4718600 | tf_op jit(solution)/shard_map/ppermute | solution.py:144
  108.8 79.5 %collective-permute-start.2 = (bf16[32,4,2,3072]{3,0,2,1:T(8,128)(2,1)}, bf16[32,4,2,3072]{3,0,2,1:T(8,128)(2,1)}, u32[]{:S(2)}, u32[]{:S(2)}) collective-permute-start(bf16[32,4,2,3072]{3,0,2,1:T(8,128)(2,1)} %copy.72), channel_id=1, source_target_pairs={{0,32},{32,64},{64,96},{96,0},{128,160},{160,192},{192,224},{224,1... | collective-permute-start | bytes 4718600 | tf_op jit(solution)/shard_map/ppermute | solution.py:144
  110.8 82.3 %collective-permute-start.1 = (bf16[32,4,2,3072]{3,0,2,1:T(8,128)(2,1)}, bf16[32,4,2,3072]{3,0,2,1:T(8,128)(2,1)}, u32[]{:S(2)}, u32[]{:S(2)}) collective-permute-start(bf16[32,4,2,3072]{3,0,2,1:T(8,128)(2,1)} %copy.72), channel_id=1, source_target_pairs={{0,64},{32,96},{64,0},{96,32},{128,192},{160,224},{192,128},{224,1... | collective-permute-start | bytes 4718600 | tf_op jit(solution)/shard_map/ppermute | solution.py:144
  118.8 84.4 %all-to-all-start = ((bf16[3,128,16,128]{3,1,0,2:T(8,128)(2,1)}), bf16[3,128,16,128]{3,1,0,2:T(8,128)(2,1)S(1)}, u32[]{:S(2)}, u32[]{:S(2)}) async-start(bf16[3,128,16,128]{3,1,0,2:T(8,128)(2,1)} %copy.45), calls=%async_computation | async-start | bytes 3145728 | tf_op jit(solution)/shard_map/all_to_all | solution.py:148
  203.2 6.0 %copy-start.1 = (bf16[3,128,16,128]{3,1,0,2:T(8,128)(2,1)}, bf16[3,128,16,128]{3,1,0,2:T(8,128)(2,1)S(1)}, u32[]{:S(2)}) copy-start(bf16[3,128,16,128]{3,1,0,2:T(8,128)(2,1)S(1)} %all-to-all-done) | copy-start | bytes 4718596
  203.2 17.6 %all-to-all-start.2 = ((bf16[128,16,128]{2,0,1:T(8,128)(2,1)}), bf16[128,16,128]{2,0,1:T(8,128)(2,1)S(1)}, u32[]{:S(2)}, u32[]{:S(2)}) async-start(bf16[128,16,128]{2,0,1:T(8,128)(2,1)} %copy.53), calls=%async_computation.2 | async-start | bytes 1048576 | tf_op jit(solution)/shard_map/all_to_all | solution.py:158
Sparse Core Ops, SparseCore 0:
  25.7 74.9 all-gather.4
  103.4 73.9 all-gather.6

commit v7 on v5

--- a/solution.py
+++ b/solution.py
@@ -49,7 +49,19 @@
     )(length, query, key)
 
 
-def gradient_kernel(p_ref, q_ref, k_ref, v_ref, g_ref, dq_ref, dk_ref, dv_ref, dkt_acc, dvt_acc):
+def query_grad_kernel(p_ref, k_ref, v_ref, g_ref, dq_ref):
+    factor = 1.0 / math.sqrt(k_ref.shape[1])
+    nt = (((1,), (1,)), ((), ()))
+    attention = p_ref[...]
+    weight_grad = lax.dot_general(g_ref[...], v_ref[...], nt, preferred_element_type=jnp.float32)
+    row_dot = jnp.sum(attention * weight_grad, axis=1, keepdims=True)
+    score_grad = (attention * (weight_grad - row_dot) * factor).astype(jnp.bfloat16)
+    dq_ref[...] = jnp.dot(score_grad, k_ref[...], preferred_element_type=jnp.float32).astype(
+        dq_ref.dtype
+    )
+
+
+def key_value_grad_kernel(p_ref, q_ref, v_ref, g_ref, dk_ref, dv_ref, dkt_acc, dvt_acc):
     step = pl.program_id(0)
     factor = 1.0 / math.sqrt(q_ref.shape[1])
     nt = (((1,), (1,)), ((), ()))
@@ -61,14 +73,12 @@
 
     attention = p_ref[...]
     grad_block = g_ref[...]
-    keys = k_ref[...]
     attention_low = attention.astype(jnp.bfloat16)
     grad_t = grad_block.astype(jnp.float32).T.astype(jnp.bfloat16)
     dvt_acc[...] += jnp.dot(grad_t, attention_low, preferred_element_type=jnp.float32)
     weight_grad = lax.dot_general(grad_block, v_ref[...], nt, preferred_element_type=jnp.float32)
     row_dot = jnp.sum(attention * weight_grad, axis=1, keepdims=True)
     score_grad = (attention * (weight_grad - row_dot) * factor).astype(jnp.bfloat16)
-    dq_ref[...] = jnp.dot(score_grad, keys, preferred_element_type=jnp.float32).astype(dq_ref.dtype)
     query_t = q_ref[...].astype(jnp.float32).T.astype(jnp.bfloat16)
     dkt_acc[...] += jnp.dot(query_t, score_grad, preferred_element_type=jnp.float32)
 
@@ -78,39 +88,60 @@
         dv_ref[...] = dvt_acc[...].T.astype(dv_ref.dtype)
 
 
-def attention_grads(query, key, value, grad, length, probs=None):
+def _params():
+    return pltpu.CompilerParams(dimension_semantics=("arbitrary",), vmem_limit_bytes=48 * 1024 * 1024)
+
+
+def query_grads(probs, key, value, grad):
+    rows, width = key.shape
+    block = min(BLOCK_ROWS, rows)
+    row_spec = pl.BlockSpec((block, width), lambda i: (i, 0))
+    full_spec = pl.BlockSpec((rows, width), lambda i: (0, 0))
+    return pl.pallas_call(
+        query_grad_kernel,
+        grid=(rows // block,),
+        in_specs=[pl.BlockSpec((block, rows), lambda i: (i, 0)), full_spec, full_spec, row_spec],
+        out_specs=row_spec,
+        out_shape=jax.ShapeDtypeStruct((rows, width), jnp.bfloat16),
+        compiler_params=_params(),
+        cost_estimate=pl.CostEstimate(
+            flops=4 * rows * rows * width,
+            transcendentals=0,
+            bytes_accessed=4 * rows * width * 2 + rows * rows * 4,
+        ),
+    )(probs, key, value, grad)
+
+
+def key_value_grads(probs, query, value, grad):
     rows, width = query.shape
-    if probs is None:
-        probs = attention_probs(query, key, length)
     block = min(BLOCK_ROWS, rows)
     row_spec = pl.BlockSpec((block, width), lambda i: (i, 0))
     full_spec = pl.BlockSpec((rows, width), lambda i: (0, 0))
     out = jax.ShapeDtypeStruct((rows, width), jnp.bfloat16)
     return pl.pallas_call(
-        gradient_kernel,
+        key_value_grad_kernel,
         grid=(rows // block,),
-        in_specs=[
-            pl.BlockSpec((block, rows), lambda i: (i, 0)),
-            row_spec,
-            full_spec,
-            full_spec,
-            row_spec,
-        ],
-        out_specs=[row_spec, full_spec, full_spec],
-        out_shape=[out, out, out],
+        in_specs=[pl.BlockSpec((block, rows), lambda i: (i, 0)), row_spec, full_spec, row_spec],
+        out_specs=[full_spec, full_spec],
+        out_shape=[out, out],
         scratch_shapes=[
             pltpu.VMEM((width, rows), jnp.float32),
             pltpu.VMEM((width, rows), jnp.float32),
         ],
-        compiler_params=pltpu.CompilerParams(
-            dimension_semantics=("arbitrary",), vmem_limit_bytes=48 * 1024 * 1024
+        compiler_params=_params(),
+        cost_estimate=pl.CostEstimate(
+            flops=6 * rows * rows * width,
+            transcendentals=0,
+            bytes_accessed=5 * rows * width * 2 + rows * rows * 4,
         ),
-        cost_estimate=pl.CostEstimate(
-            flops=8 * rows * rows * width,
-            transcendentals=0,
-            bytes_accessed=7 * rows * width * 2 + rows * rows * 4,
-        ),
-    )(probs, query, key, value, grad)
+    )(probs, query, value, grad)
+
+
+def attention_grads(query, key, value, grad, length, probs=None):
+    if probs is None:
+        probs = attention_probs(query, key, length)
+    key_grad, value_grad = key_value_grads(probs, query, value, grad)
+    return (query_grads(probs, key, value, grad), key_grad, value_grad)
 
 
 def per_device(query_rows, key_rows, value_rows, out_grad, out_weight, text_length):
@@ -137,19 +168,19 @@
     total_rows = tok_rows * devices
     query_heads = qkv_heads[0].reshape(total_rows, HEAD_DIM)
     key_heads = qkv_heads[1].reshape(total_rows, HEAD_DIM)
+    value_heads = qkv_heads[2].reshape(total_rows, HEAD_DIM)
+    grad_heads = grad_heads.reshape(total_rows, HEAD_DIM)
     probs = attention_probs(query_heads, key_heads, text_length)
-    query_grad, key_grad, value_grad = attention_grads(
-        query_heads,
-        key_heads,
-        qkv_heads[2].reshape(total_rows, HEAD_DIM),
-        grad_heads.reshape(total_rows, HEAD_DIM),
-        text_length,
-        probs,
-    )
-    grads = jnp.stack([query_grad, key_grad, value_grad]).reshape(3, devices, tok_rows, HEAD_DIM)
-    returned = lax.all_to_all(grads, "dp", split_axis=1, concat_axis=1, tiled=True)
-    returned = returned.transpose(0, 2, 1, 3).reshape(3, 1, tok_rows, HEADS * HEAD_DIM)
-    return (returned[0], returned[1], returned[2])
+
+    def send_back(grads):
+        count = len(grads)
+        stacked = jnp.stack(grads).reshape(count, devices, tok_rows, HEAD_DIM)
+        returned = lax.all_to_all(stacked, "dp", split_axis=1, concat_axis=1, tiled=True)
+        return returned.transpose(0, 2, 1, 3).reshape(count, 1, tok_rows, HEADS * HEAD_DIM)
+
+    query_back = send_back([query_grads(probs, key_heads, value_heads, grad_heads)])
+    key_value_back = send_back(list(key_value_grads(probs, query_heads, value_heads, grad_heads)))
+    return (query_back[0], key_value_back[0], key_value_back[1])
 
 
 def solution(mesh):

time: 198 us -> 207 us (1.045)
  blocking collectives: 43.6 us -> 15.5 us
  waiting for transfers between devices: 82.8 us -> 96.7 us
  starting transfers between devices: 10.2 us -> 23.5 us
  Pallas kernels: 23.3 us -> 34.8 us
  local copies, waits for them, and re-layouts: 14.5 us -> 11.7 us
    all_to_all x1 -> x0, blocking collectives: 28.1 us -> none  [per_device(): lax.all_to_all(grads, 'dp', split_axis=1, concat_axis=1, tiled=True)]
    all_to_all x0 -> x2, waiting for transfers between devices: none -> 13.9 us  [send_back(): lax.all_to_all(stacked, 'dp', split_axis=1, concat_axis=1, tiled=True)]
    all_to_all x0 -> x2, starting transfers between devices: none -> 13.3 us  [send_back(): lax.all_to_all(stacked, 'dp', split_axis=1, concat_axis=1, tiled=True)]
    pallas_call x1 -> x2, Pallas kernels: 13.2 us -> 24.7 us  [the longest x1 12.8 us: key_value_grads(): pl.pallas_call(key_value_grad_kernel, grid=(rows // block,), in_specs=[pl...]
  transfers between devices with their start and end apart: 3 -> 5, of which waited for: 1 -> 2; matrix products, arithmetic and copies ran while one was open for 7% -> 8% of each run, Pallas kernels for 5% -> 11%
where the time goes in v7:
time: 207 us; the launch traced here: 206 us
  waiting for transfers between devices  96.7 us (47%)
  Pallas kernels  34.8 us (17%)
  starting transfers between devices  23.5 us (11%)
  blocking collectives  15.5 us (7%)
  between operations  14.8 us (7%)
  local copies, waits for them, and re-layouts  11.7 us (6%)
  matrix products  6.46 us (3%)
  other arithmetic  2.5 us (1%)
    all_gather x1, waiting for transfers between devices, per_device(): weight = lax.all_gather(stream_rows, 'seq', axis=1, tiled=True)  82.8 us
    all_to_all x1, blocking collectives, per_device(): lax.all_to_all(outgoing, 'dp', split_axis=0, concat_axis=0, tiled=True)  15.5 us
    all_to_all x2, waiting for transfers between devices, send_back(): lax.all_to_all(stacked, 'dp', split_axis=1, concat_axis=1, tiled=True)  13.9 us
    all_to_all x2, starting transfers between devices, send_back(): lax.all_to_all(stacked, 'dp', split_axis=1, concat_axis=1, tiled=True)  13.3 us
    pallas_call x1, Pallas kernels, key_value_grads(): pl.pallas_call(key_value_grad_kernel, grid=(rows // block,), in_specs=[pl...  12.8 us
    pallas_call x1, Pallas kernels, query_grads(): pl.pallas_call(query_grad_kernel, grid=(rows // block,), in_specs=[pl.Blo...  12 us
    pallas_call x1, Pallas kernels, attention_probs(): pl.pallas_call(softmax_kernel, grid=(rows // block,), in_specs=[pl.BlockS...  10.1 us
    dot_general x1, matrix products, per_device(): jnp.einsum('te,kre->tkr', out_grad[0], weight, preferred_element_type=jnp...  6.46 us
  transfers between devices with their start and end apart: 5, of which 2 were waited for; matrix products, arithmetic and copies ran while one was open for 8% of the time, Pallas kernels for 11%

profile of v7, /device:TPU:1, one launch (start us, length us, event | category | flops | bytes accessed | tf_op | source)
XLA Modules:
  0.0 205.9 jit_solution(559909285910119822)
XLA Ops:
  7.2 0.9 slice_bitcast_fusion.1
  8.4 15.5 %all_to_all.45 = bf16[16,4,3072]{2,1,0:T(4,128)(2,1)S(1)} all-to-all(bf16[16,4,3072]{2,1,0:T(4,128)(2,1)S(1)} %broadcast_select_fusion), channel_id=1, replica_groups=mesh['dp'=16,'seq'=32] {'dp'}, dimensions={0} | all-to-all | bytes 786432 | tf_op jit(solution)/shard_map/all_to_all | solution.py:156
  23.9 0.9 copy.38
  25.3 1.0 copy.36
  26.3 1.2 pad_maximum_fusion
  27.5 1.6 copy.37
  29.1 3.7 %all-to-all-start = ((bf16[3,128,16,128]{3,1,0,2:T(8,128)(2,1)}), bf16[3,128,16,128]{3,1,0,2:T(8,128)(2,1)S(1)}, u32[]{:S(2)}, u32[]{:S(2)}) async-start(bf16[3,128,16,128]{3,1,0,2:T(8,128)(2,1)} %copy.37), calls=%async_computation | async-start | bytes 3145728 | tf_op jit(solution)/shard_map/all_to_all | solution.py:160
  32.9 82.8 %all-gather.2.cloned.1.call-done = bf16[16,128,3072]{2,0,1:T(8,128)(2,1)} async-done(((bf16[16,4,3072]{2,0,1:T(8,128)(2,1)}), bf16[16,128,3072]{2,0,1:T(8,128)(2,1)}) %all-gather.2.cloned.1.call-update) | async-done | bytes 12582928 | tf_op jit(solution)/shard_map/all_gather | solution.py:157
  115.7 6.5 %fusion = bf16[128,16,128]{0,1,2:T(8,128)(2,1)S(1)} fusion(bf16[16,128,3072]{2,0,1:T(8,128)(2,1)} %all-gather.2.cloned.1.call-done, bf16[1,128,3072]{2,1,0:T(8,128)(2,1)S(1)} %copy-done), kind=kOutput, calls=%fused_computation.2 | convolution fusion | flops 1610874880 | bytes 13893632 | tf_op jit(solution)/shard_map/te,kre->tkr/dot_general | solution.py:162
  122.1 0.9 copy.39
  123.1 6.4 %all-to-all-start.2 = ((bf16[128,16,128]{0,2,1:T(8,128)(2,1)}), bf16[128,16,128]{0,2,1:T(8,128)(2,1)S(1)}, u32[]{:S(2)}, u32[]{:S(2)}) async-start(bf16[128,16,128]{0,2,1:T(8,128)(2,1)} %copy.39), calls=%async_computation.2 | async-start | bytes 1048576 | tf_op jit(solution)/shard_map/all_to_all | solution.py:165
  130.1 1.5 fusion.2
  131.6 10.1 %shard_map.85.p_ref = f32[2048,2048]{1,0:T(8,128)} custom-call(s32[1]{0:T(128)S(6)} %copy.49.length_ref, bf16[2048,128]{1,0:T(8,128)(2,1)S(1)} %bitcast.43, bf16[2048,128]{1,0:T(8,128)(2,1)S(1)} %bitcast.45), custom_call_target="tpu_custom_call" | custom-call | flops 1073741824 | bytes 17825792 | tf_op jit(solution)/shard_map/pallas_call | solution.py:31
  142.0 12.0 %shard_map.86 = bf16[2048,128]{1,0:T(8,128)(2,1)} custom-call(f32[2048,2048]{1,0:T(8,128)} %shard_map.85.p_ref, bf16[2048,128]{1,0:T(8,128)(2,1)S(1)} %bitcast.46, bf16[2048,128]{1,0:T(8,128)(2,1)S(1)} %bitcast.41, bf16[2048,128]{1,0:T(8,128)(2,1)S(1)} %bitcast.39), custom_call_target="tpu_custom_call" | custom-call | flops 2147483648 | bytes 18874368 | tf_op jit(solution)/shard_map/pallas_call | solution.py:100
  153.9 6.7 %all-to-all-start.3 = ((bf16[1,16,128,128]{3,2,0,1:T(8,128)(2,1)}), bf16[1,16,128,128]{3,2,0,1:T(8,128)(2,1)S(1)}, u32[]{:S(2)}, u32[]{:S(2)}) async-start(bf16[1,16,128,128]{3,2,0,1:T(8,128)(2,1)} %bitcast.18), calls=%async_computation.3 | async-start | bytes 1048576 | tf_op jit(solution)/shard_map/all_to_all | solution.py:178
  160.6 12.8 %shard_map.87 = (bf16[2048,128]{1,0:T(8,128)(2,1)S(1)}, bf16[2048,128]{1,0:T(8,128)(2,1)S(1)}) custom-call(f32[2048,2048]{1,0:T(8,128)} %shard_map.85.p_ref, bf16[2048,128]{1,0:T(8,128)(2,1)S(1)} %bitcast.44, bf16[2048,128]{1,0:T(8,128)(2,1)S(1)} %bitcast.42, bf16[2048,128]{1,0:T(8,128)(2,1)S(1)} %bitcast.40), custom_call_target="tpu_custom_call" | custom-call | flops 3221225472 | bytes 19398656 | tf_op jit(solution)/shard_map/pallas_call | solution.py:121
  173.4 1.1 pad_maximum_fusion.1
  174.5 6.7 %all-to-all-start.4 = ((bf16[2,16,128,128]{3,2,0,1:T(8,128)(2,1)}), bf16[2,16,128,128]{3,2,0,1:T(8,128)(2,1)S(1)}, u32[]{:S(2)}, u32[]{:S(2)}) async-start(bf16[2,16,128,128]{3,2,0,1:T(8,128)(2,1)} %pad_maximum_fusion.1), calls=%async_computation.4 | async-start | bytes 2097152 | tf_op jit(solution)/shard_map/all_to_all | solution.py:178
  181.1 0.3 copy.42
  181.4 1.0 copy.46
  182.4 13.9 %all-to-all-done.4 = bf16[2,16,128,128]{3,2,0,1:T(8,128)(2,1)S(1)} async-done(((bf16[2,16,128,128]{3,2,0,1:T(8,128)(2,1)}), bf16[2,16,128,128]{3,2,0,1:T(8,128)(2,1)S(1)}, u32[]{:S(2)}, u32[]{:S(2)}) %all-to-all-start.4) | async-done | bytes 1048608 | tf_op jit(solution)/shard_map/all_to_all | solution.py:178
  196.3 0.7 copy.45
  197.1 1.0 copy.48
  198.1 1.0 copy.47
  (21 shorter events, 1.2 us)
Async XLA Ops:
  7.2 108.5 %copy-start = (bf16[1,128,3072]{2,1,0:T(8,128)(2,1)S(1)}, bf16[1,128,3072]{2,1,0:T(8,128)(2,1)}, u32[]{:S(2)}) copy-start(bf16[1,128,3072]{2,1,0:T(8,128)(2,1)} %param.9) | copy-start | bytes 2359300
  7.2 17.6 %copy-start.2 = (bf16[1,128,2048]{2,1,0:T(8,128)(2,1)S(1)}, bf16[1,128,2048]{2,1,0:T(8,128)(2,1)}, u32[]{:S(2)}) copy-start(bf16[1,128,2048]{2,1,0:T(8,128)(2,1)} %param.6) | copy-start | bytes 1572868
  7.2 108.5 %all-gather.2.cloned.1.call-start = ((), (), s32[]{:S(2)}) async-start(), calls=%async_computation.5 | async-start | bytes 12976128 | tf_op jit(solution)/shard_map/all_gather | solution.py:157
  8.3 16.7 %copy-start.3 = (bf16[1,128,2048]{2,1,0:T(8,128)(2,1)S(1)}, bf16[1,128,2048]{2,1,0:T(8,128)(2,1)}, u32[]{:S(2)}) copy-start(bf16[1,128,2048]{2,1,0:T(8,128)(2,1)} %param.7) | copy-start | bytes 1572868
  23.9 1.5 copy-start.4
  29.1 93.9 %all-to-all-start = ((bf16[3,128,16,128]{3,1,0,2:T(8,128)(2,1)}), bf16[3,128,16,128]{3,1,0,2:T(8,128)(2,1)S(1)}, u32[]{:S(2)}, u32[]{:S(2)}) async-start(bf16[3,128,16,128]{3,1,0,2:T(8,128)(2,1)} %copy.37), calls=%async_computation | async-start | bytes 3145728 | tf_op jit(solution)/shard_map/all_to_all | solution.py:160
  123.1 7.0 %copy-start.1 = (bf16[3,128,16,128]{3,1,0,2:T(8,128)(2,1)}, bf16[3,128,16,128]{3,1,0,2:T(8,128)(2,1)S(1)}, u32[]{:S(2)}) copy-start(bf16[3,128,16,128]{3,1,0,2:T(8,128)(2,1)S(1)} %all-to-all-done) | copy-start | bytes 4718596
  123.1 18.6 %all-to-all-start.2 = ((bf16[128,16,128]{0,2,1:T(8,128)(2,1)}), bf16[128,16,128]{0,2,1:T(8,128)(2,1)S(1)}, u32[]{:S(2)}, u32[]{:S(2)}) async-start(bf16[128,16,128]{0,2,1:T(8,128)(2,1)} %copy.39), calls=%async_computation.2 | async-start | bytes 1048576 | tf_op jit(solution)/shard_map/all_to_all | solution.py:165
  153.9 20.5 %all-to-all-start.3 = ((bf16[1,16,128,128]{3,2,0,1:T(8,128)(2,1)}), bf16[1,16,128,128]{3,2,0,1:T(8,128)(2,1)S(1)}, u32[]{:S(2)}, u32[]{:S(2)}) async-start(bf16[1,16,128,128]{3,2,0,1:T(8,128)(2,1)} %bitcast.18), calls=%async_computation.3 | async-start | bytes 1048576 | tf_op jit(solution)/shard_map/all_to_all | solution.py:178
  174.5 21.8 %all-to-all-start.4 = ((bf16[2,16,128,128]{3,2,0,1:T(8,128)(2,1)}), bf16[2,16,128,128]{3,2,0,1:T(8,128)(2,1)S(1)}, u32[]{:S(2)}, u32[]{:S(2)}) async-start(bf16[2,16,128,128]{3,2,0,1:T(8,128)(2,1)} %pad_maximum_fusion.1), calls=%async_computation.4 | async-start | bytes 2097152 | tf_op jit(solution)/shard_map/all_to_all | solution.py:178
Sparse Core Ops, SparseCore 0:
  24.9 90.7 all-gather.1

commit v8 on v5

--- a/solution.py
+++ b/solution.py
@@ -113,6 +113,26 @@
     )(probs, query, key, value, grad)
 
 
+def relayout_kernel(block_ref, *out_refs):
+    for index, out_ref in enumerate(out_refs):
+        out_ref[...] = block_ref[0, index]
+
+
+def relayout(blocks):
+    heads, count, rows, width = blocks.shape
+    return pl.pallas_call(
+        relayout_kernel,
+        grid=(heads,),
+        in_specs=[pl.BlockSpec((1, count, rows, width), lambda h: (h, 0, 0, 0))],
+        out_specs=[pl.BlockSpec((rows, width), lambda h: (0, h))] * count,
+        out_shape=[jax.ShapeDtypeStruct((rows, heads * width), blocks.dtype)] * count,
+        compiler_params=pltpu.CompilerParams(dimension_semantics=("arbitrary",)),
+        cost_estimate=pl.CostEstimate(
+            flops=0, transcendentals=0, bytes_accessed=2 * blocks.size * blocks.dtype.itemsize
+        ),
+    )(blocks)
+
+
 def per_device(query_rows, key_rows, value_rows, out_grad, out_weight, text_length):
     devices = lax.axis_size("dp")
     tok_rows = query_rows.shape[1]
@@ -147,9 +167,8 @@
         probs,
     )
     grads = jnp.stack([query_grad, key_grad, value_grad]).reshape(3, devices, tok_rows, HEAD_DIM)
-    returned = lax.all_to_all(grads, "dp", split_axis=1, concat_axis=1, tiled=True)
-    returned = returned.transpose(0, 2, 1, 3).reshape(3, 1, tok_rows, HEADS * HEAD_DIM)
-    return (returned[0], returned[1], returned[2])
+    returned = lax.all_to_all(grads.transpose(1, 0, 2, 3), "dp", split_axis=0, concat_axis=0, tiled=True)
+    return tuple(out.reshape(1, tok_rows, HEADS * HEAD_DIM) for out in relayout(returned))
 
 
 def solution(mesh):

time: 198 us -> 201 us (1.015)
  Pallas kernels: 23.3 us -> 32.5 us
  local copies, waits for them, and re-layouts: 14.5 us -> 7.58 us
    pallas_call x0 -> x1, Pallas kernels: none -> 9.25 us  [relayout(): pl.pallas_call(relayout_kernel, grid=(heads,), in_specs=[pl.BlockSpec((1,...]
    unnamed x16 -> x13, local copies, waits for them, and re-layouts: 5.62 us -> 1.57 us
where the time goes in v8:
time: 201 us; the launch traced here: 200 us
  waiting for transfers between devices  82.8 us (41%)
  blocking collectives  43.6 us (22%)
  Pallas kernels  32.5 us (16%)
  between operations  14.8 us (7%)
  starting transfers between devices  10.2 us (5%)
  local copies, waits for them, and re-layouts  7.58 us (4%)
  matrix products  6.46 us (3%)
    all_gather x1, waiting for transfers between devices, per_device(): weight = lax.all_gather(stream_rows, 'seq', axis=1, tiled=True)  82.8 us
    all_to_all x1, blocking collectives, per_device(): lax.all_to_all(grads.transpose(1, 0, 2, 3), 'dp', split_axis=0, concat_ax...  28.1 us
    all_to_all x1, blocking collectives, per_device(): lax.all_to_all(outgoing, 'dp', split_axis=0, concat_axis=0, tiled=True)  15.5 us
    pallas_call x1, Pallas kernels, attention_grads(): pl.pallas_call(gradient_kernel, grid=(rows // block,), in_specs=[pl.Block...  13.2 us
    pallas_call x1, Pallas kernels, attention_probs(): pl.pallas_call(softmax_kernel, grid=(rows // block,), in_specs=[pl.BlockS...  10.1 us
    pallas_call x1, Pallas kernels, relayout(): pl.pallas_call(relayout_kernel, grid=(heads,), in_specs=[pl.BlockSpec((1,...  9.25 us
    dot_general x1, matrix products, per_device(): jnp.einsum('te,kre->tkr', out_grad[0], weight, preferred_element_type=jnp...  6.46 us
    all_to_all x1, starting transfers between devices, per_device(): lax.all_to_all(projected.astype(jnp.bfloat16), 'dp', split_axis=1, concat...  6.39 us
  transfers between devices with their start and end apart: 3, of which 1 were waited for; matrix products, arithmetic and copies ran while one was open for 7% of the time, Pallas kernels for 5%

profile of v8, /device:TPU:1, one launch (start us, length us, event | category | flops | bytes accessed | tf_op | source)
XLA Modules:
  0.0 199.5 jit_solution(10246263592021270769)
XLA Ops:
  7.2 0.0 copy-start
  7.2 0.0 all-gather.2.cloned.1.call-start
  7.2 0.9 slice_bitcast_fusion.1
  8.1 0.2 broadcast_select_fusion
  8.4 15.5 %all_to_all.40 = bf16[16,4,3072]{2,1,0:T(4,128)(2,1)S(1)} all-to-all(bf16[16,4,3072]{2,1,0:T(4,128)(2,1)S(1)} %broadcast_select_fusion), channel_id=1, replica_groups=mesh['dp'=16,'seq'=32] {'dp'}, dimensions={0} | all-to-all | bytes 786432 | tf_op jit(solution)/shard_map/all_to_all | solution.py:145
  23.9 0.9 copy.24
  24.7 0.0 all-gather.2.cloned.1.call-update
  24.8 0.3 copy.20
  25.0 0.3 copy.21
  25.3 1.0 copy.22
  26.3 1.2 pad_maximum_fusion
  27.5 1.6 copy.23
  29.1 3.7 %all-to-all-start = ((bf16[3,128,16,128]{3,1,0,2:T(8,128)(2,1)}), bf16[3,128,16,128]{3,1,0,2:T(8,128)(2,1)S(1)}, u32[]{:S(2)}, u32[]{:S(2)}) async-start(bf16[3,128,16,128]{3,1,0,2:T(8,128)(2,1)} %copy.23), calls=%async_computation | async-start | bytes 3145728 | tf_op jit(solution)/shard_map/all_to_all | solution.py:149
  32.9 82.8 %all-gather.2.cloned.1.call-done = bf16[16,128,3072]{2,0,1:T(8,128)(2,1)} async-done(((bf16[16,4,3072]{2,0,1:T(8,128)(2,1)}), bf16[16,128,3072]{2,0,1:T(8,128)(2,1)}) %all-gather.2.cloned.1.call-update) | async-done | bytes 12582928 | tf_op jit(solution)/shard_map/all_gather | solution.py:146
  115.7 6.5 %fusion = bf16[128,16,128]{0,1,2:T(8,128)(2,1)S(1)} fusion(bf16[16,128,3072]{2,0,1:T(8,128)(2,1)} %all-gather.2.cloned.1.call-done, bf16[1,128,3072]{2,1,0:T(8,128)(2,1)S(1)} %copy-done), kind=kOutput, calls=%fused_computation.3 | convolution fusion | flops 1610874880 | bytes 13893632 | tf_op jit(solution)/shard_map/te,kre->tkr/dot_general | solution.py:151
  122.1 0.9 copy.25
  123.1 6.4 %all-to-all-start.2 = ((bf16[128,16,128]{0,2,1:T(8,128)(2,1)}), bf16[128,16,128]{0,2,1:T(8,128)(2,1)S(1)}, u32[]{:S(2)}, u32[]{:S(2)}) async-start(bf16[128,16,128]{0,2,1:T(8,128)(2,1)} %copy.25), calls=%async_computation.2 | async-start | bytes 1048576 | tf_op jit(solution)/shard_map/all_to_all | solution.py:154
  130.1 1.5 fusion.2
  131.6 10.1 %shard_map.85.p_ref = f32[2048,2048]{1,0:T(8,128)} custom-call(s32[1]{0:T(128)S(6)} %copy.27.length_ref, bf16[2048,128]{1,0:T(8,128)(2,1)S(1)} %bitcast.34, bf16[2048,128]{1,0:T(8,128)(2,1)S(1)} %bitcast.32), custom_call_target="tpu_custom_call" | custom-call | flops 1073741824 | bytes 17825792 | tf_op jit(solution)/shard_map/pallas_call | solution.py:31
  141.7 0.3 copy.26
  141.9 13.2 %shard_map.86 = (bf16[2048,128]{1,0:T(8,128)(2,1)S(1)}, bf16[2048,128]{1,0:T(8,128)(2,1)S(1)}, bf16[2048,128]{1,0:T(8,128)(2,1)S(1)}) custom-call(f32[2048,2048]{1,0:T(8,128)} %shard_map.85.p_ref, bf16[2048,128]{1,0:T(8,128)(2,1)S(1)} %bitcast.35, bf16[2048,128]{1,0:T(8,128)(2,1)S(1)} %bitcast.33, bf16[2048,128]{1,0:T(8,128)(2,1)S(1)} %bitcast.37, ...), custom_call_target="tpu_custom_call" | custom-call | flops 4294967296 | bytes 20447232 | tf_op jit(solution)/shard_map/pallas_call | solution.py:89
  155.2 0.2 maximum_bitcast_fusion
  155.4 28.1 %all_to_all.41.block_ref = bf16[16,3,128,128]{3,2,1,0:T(8,128)(2,1)} all-to-all(bf16[16,3,128,128]{3,2,1,0:T(8,128)(2,1)S(1)} %maximum_bitcast_fusion), channel_id=1, replica_groups=mesh['dp'=16,'seq'=32] {'dp'}, dimensions={0} | all-to-all | bytes 3145728 | tf_op jit(solution)/shard_map/all_to_all | solution.py:170
  183.4 9.3 %shard_map.87 = (bf16[128,2048]{1,0:T(8,128)(2,1)}, bf16[128,2048]{1,0:T(8,128)(2,1)}, bf16[128,2048]{1,0:T(8,128)(2,1)}) custom-call(bf16[16,3,128,128]{3,2,1,0:T(8,128)(2,1)} %all_to_all.41.block_ref), custom_call_target="tpu_custom_call" | custom-call | bytes 3145728 | tf_op jit(solution)/shard_map/pallas_call | solution.py:123
  (12 shorter events, 0.0 us)
Async XLA Ops:
  7.2 108.5 %copy-start = (bf16[1,128,3072]{2,1,0:T(8,128)(2,1)S(1)}, bf16[1,128,3072]{2,1,0:T(8,128)(2,1)}, u32[]{:S(2)}) copy-start(bf16[1,128,3072]{2,1,0:T(8,128)(2,1)} %param.9) | copy-start | bytes 2359300
  7.2 17.6 %copy-start.2 = (bf16[1,128,2048]{2,1,0:T(8,128)(2,1)S(1)}, bf16[1,128,2048]{2,1,0:T(8,128)(2,1)}, u32[]{:S(2)}) copy-start(bf16[1,128,2048]{2,1,0:T(8,128)(2,1)} %param.6) | copy-start | bytes 1572868
  7.2 108.5 %all-gather.2.cloned.1.call-start = ((), (), s32[]{:S(2)}) async-start(), calls=%async_computation.4 | async-start | bytes 12976128 | tf_op jit(solution)/shard_map/all_gather | solution.py:146
  8.3 16.7 %copy-start.3 = (bf16[1,128,2048]{2,1,0:T(8,128)(2,1)S(1)}, bf16[1,128,2048]{2,1,0:T(8,128)(2,1)}, u32[]{:S(2)}) copy-start(bf16[1,128,2048]{2,1,0:T(8,128)(2,1)} %param.7) | copy-start | bytes 1572868
  23.9 1.5 copy-start.4
  29.1 94.0 %all-to-all-start = ((bf16[3,128,16,128]{3,1,0,2:T(8,128)(2,1)}), bf16[3,128,16,128]{3,1,0,2:T(8,128)(2,1)S(1)}, u32[]{:S(2)}, u32[]{:S(2)}) async-start(bf16[3,128,16,128]{3,1,0,2:T(8,128)(2,1)} %copy.23), calls=%async_computation | async-start | bytes 3145728 | tf_op jit(solution)/shard_map/all_to_all | solution.py:149
  123.1 7.0 %copy-start.1 = (bf16[3,128,16,128]{3,1,0,2:T(8,128)(2,1)}, bf16[3,128,16,128]{3,1,0,2:T(8,128)(2,1)S(1)}, u32[]{:S(2)}) copy-start(bf16[3,128,16,128]{3,1,0,2:T(8,128)(2,1)S(1)} %all-to-all-done) | copy-start | bytes 4718596
  123.1 18.6 %all-to-all-start.2 = ((bf16[128,16,128]{0,2,1:T(8,128)(2,1)}), bf16[128,16,128]{0,2,1:T(8,128)(2,1)S(1)}, u32[]{:S(2)}, u32[]{:S(2)}) async-start(bf16[128,16,128]{0,2,1:T(8,128)(2,1)} %copy.25), calls=%async_computation.2 | async-start | bytes 1048576 | tf_op jit(solution)/shard_map/all_to_all | solution.py:154
Sparse Core Ops, SparseCore 0:
  24.9 90.7 all-gather.1

commit v9 on v8

--- a/solution.py
+++ b/solution.py
@@ -114,19 +114,19 @@
 
 
 def relayout_kernel(block_ref, *out_refs):
+    heads, _, _, width = block_ref.shape
     for index, out_ref in enumerate(out_refs):
-        out_ref[...] = block_ref[0, index]
+        for head in range(heads):
+            out_ref[:, head * width : (head + 1) * width] = block_ref[head, index]
 
 
 def relayout(blocks):
     heads, count, rows, width = blocks.shape
     return pl.pallas_call(
         relayout_kernel,
-        grid=(heads,),
-        in_specs=[pl.BlockSpec((1, count, rows, width), lambda h: (h, 0, 0, 0))],
-        out_specs=[pl.BlockSpec((rows, width), lambda h: (0, h))] * count,
+        in_specs=[pl.BlockSpec(memory_space=pltpu.VMEM)],
+        out_specs=[pl.BlockSpec(memory_space=pltpu.VMEM)] * count,
         out_shape=[jax.ShapeDtypeStruct((rows, heads * width), blocks.dtype)] * count,
-        compiler_params=pltpu.CompilerParams(dimension_semantics=("arbitrary",)),
         cost_estimate=pl.CostEstimate(
             flops=0, transcendentals=0, bytes_accessed=2 * blocks.size * blocks.dtype.itemsize
         ),

time: 201 us -> 194 us (0.965)
  Pallas kernels: 32.5 us -> 26.2 us
    pallas_call x1, Pallas kernels: 9.25 us -> 2.95 us  [relayout(): pl.pallas_call(relayout_kernel, in_specs=[pl.BlockSpec(memory_space=pltpu...]
where the time goes in v9:
time: 194 us; the launch traced here: 193 us
  waiting for transfers between devices  82.8 us (43%)
  blocking collectives  43.6 us (22%)
  Pallas kernels  26.2 us (14%)
  between operations  14.8 us (8%)
  starting transfers between devices  10.2 us (5%)
  local copies, waits for them, and re-layouts  7.58 us (4%)
  matrix products  6.46 us (3%)
    all_gather x1, waiting for transfers between devices, per_device(): weight = lax.all_gather(stream_rows, 'seq', axis=1, tiled=True)  82.8 us
    all_to_all x1, blocking collectives, per_device(): lax.all_to_all(grads.transpose(1, 0, 2, 3), 'dp', split_axis=0, concat_ax...  28.1 us
    all_to_all x1, blocking collectives, per_device(): lax.all_to_all(outgoing, 'dp', split_axis=0, concat_axis=0, tiled=True)  15.5 us
    pallas_call x1, Pallas kernels, attention_grads(): pl.pallas_call(gradient_kernel, grid=(rows // block,), in_specs=[pl.Block...  13.2 us
    pallas_call x1, Pallas kernels, attention_probs(): pl.pallas_call(softmax_kernel, grid=(rows // block,), in_specs=[pl.BlockS...  10.1 us
    dot_general x1, matrix products, per_device(): jnp.einsum('te,kre->tkr', out_grad[0], weight, preferred_element_type=jnp...  6.46 us
    all_to_all x1, starting transfers between devices, per_device(): lax.all_to_all(projected.astype(jnp.bfloat16), 'dp', split_axis=1, concat...  6.39 us
  transfers between devices with their start and end apart: 3, of which 1 were waited for; matrix products, arithmetic and copies ran while one was open for 7% of the time, Pallas kernels for 5%

profile of v9, /device:TPU:1, one launch (start us, length us, event | category | flops | bytes accessed | tf_op | source)
XLA Modules:
  0.0 193.2 jit_solution(1809911117610251737)
XLA Ops:
  7.2 0.0 copy-start
  7.2 0.0 all-gather.2.cloned.1.call-start
  7.2 0.9 slice_bitcast_fusion.1
  8.1 0.2 broadcast_select_fusion
  8.4 15.5 %all_to_all.40 = bf16[16,4,3072]{2,1,0:T(4,128)(2,1)S(1)} all-to-all(bf16[16,4,3072]{2,1,0:T(4,128)(2,1)S(1)} %broadcast_select_fusion), channel_id=1, replica_groups=mesh['dp'=16,'seq'=32] {'dp'}, dimensions={0} | all-to-all | bytes 786432 | tf_op jit(solution)/shard_map/all_to_all | solution.py:145
  23.9 0.9 copy.24
  24.7 0.0 all-gather.2.cloned.1.call-update
  24.8 0.3 copy.20
  25.0 0.3 copy.21
  25.3 1.0 copy.22
  26.3 1.2 pad_maximum_fusion
  27.5 1.6 copy.23
  29.1 3.7 %all-to-all-start = ((bf16[3,128,16,128]{3,1,0,2:T(8,128)(2,1)}), bf16[3,128,16,128]{3,1,0,2:T(8,128)(2,1)S(1)}, u32[]{:S(2)}, u32[]{:S(2)}) async-start(bf16[3,128,16,128]{3,1,0,2:T(8,128)(2,1)} %copy.23), calls=%async_computation | async-start | bytes 3145728 | tf_op jit(solution)/shard_map/all_to_all | solution.py:149
  32.9 82.8 %all-gather.2.cloned.1.call-done = bf16[16,128,3072]{2,0,1:T(8,128)(2,1)} async-done(((bf16[16,4,3072]{2,0,1:T(8,128)(2,1)}), bf16[16,128,3072]{2,0,1:T(8,128)(2,1)}) %all-gather.2.cloned.1.call-update) | async-done | bytes 12582928 | tf_op jit(solution)/shard_map/all_gather | solution.py:146
  115.7 6.5 %fusion = bf16[128,16,128]{0,1,2:T(8,128)(2,1)S(1)} fusion(bf16[16,128,3072]{2,0,1:T(8,128)(2,1)} %all-gather.2.cloned.1.call-done, bf16[1,128,3072]{2,1,0:T(8,128)(2,1)S(1)} %copy-done), kind=kOutput, calls=%fused_computation.3 | convolution fusion | flops 1610874880 | bytes 13893632 | tf_op jit(solution)/shard_map/te,kre->tkr/dot_general | solution.py:151
  122.1 0.9 copy.25
  123.1 6.4 %all-to-all-start.2 = ((bf16[128,16,128]{0,2,1:T(8,128)(2,1)}), bf16[128,16,128]{0,2,1:T(8,128)(2,1)S(1)}, u32[]{:S(2)}, u32[]{:S(2)}) async-start(bf16[128,16,128]{0,2,1:T(8,128)(2,1)} %copy.25), calls=%async_computation.2 | async-start | bytes 1048576 | tf_op jit(solution)/shard_map/all_to_all | solution.py:154
  130.1 1.5 fusion.2
  131.6 10.1 %shard_map.85.p_ref = f32[2048,2048]{1,0:T(8,128)} custom-call(s32[1]{0:T(128)S(6)} %copy.27.length_ref, bf16[2048,128]{1,0:T(8,128)(2,1)S(1)} %bitcast.34, bf16[2048,128]{1,0:T(8,128)(2,1)S(1)} %bitcast.32), custom_call_target="tpu_custom_call" | custom-call | flops 1073741824 | bytes 17825792 | tf_op jit(solution)/shard_map/pallas_call | solution.py:31
  141.7 0.3 copy.26
  141.9 13.2 %shard_map.86 = (bf16[2048,128]{1,0:T(8,128)(2,1)S(1)}, bf16[2048,128]{1,0:T(8,128)(2,1)S(1)}, bf16[2048,128]{1,0:T(8,128)(2,1)S(1)}) custom-call(f32[2048,2048]{1,0:T(8,128)} %shard_map.85.p_ref, bf16[2048,128]{1,0:T(8,128)(2,1)S(1)} %bitcast.35, bf16[2048,128]{1,0:T(8,128)(2,1)S(1)} %bitcast.33, bf16[2048,128]{1,0:T(8,128)(2,1)S(1)} %bitcast.37, ...), custom_call_target="tpu_custom_call" | custom-call | flops 4294967296 | bytes 20447232 | tf_op jit(solution)/shard_map/pallas_call | solution.py:89
  155.2 0.2 maximum_bitcast_fusion
  155.4 28.1 %all_to_all.41.block_ref = bf16[16,3,128,128]{3,2,1,0:T(8,128)(2,1)} all-to-all(bf16[16,3,128,128]{3,2,1,0:T(8,128)(2,1)S(1)} %maximum_bitcast_fusion), channel_id=1, replica_groups=mesh['dp'=16,'seq'=32] {'dp'}, dimensions={0} | all-to-all | bytes 3145728 | tf_op jit(solution)/shard_map/all_to_all | solution.py:170
  183.4 3.0 %shard_map.87 = (bf16[128,2048]{1,0:T(8,128)(2,1)}, bf16[128,2048]{1,0:T(8,128)(2,1)}, bf16[128,2048]{1,0:T(8,128)(2,1)}) custom-call(bf16[16,3,128,128]{3,2,1,0:T(8,128)(2,1)} %all_to_all.41.block_ref), custom_call_target="tpu_custom_call" | custom-call | bytes 3145728 | tf_op jit(solution)/shard_map/pallas_call | solution.py:125
  (12 shorter events, 0.0 us)
Async XLA Ops:
  7.2 108.5 %copy-start = (bf16[1,128,3072]{2,1,0:T(8,128)(2,1)S(1)}, bf16[1,128,3072]{2,1,0:T(8,128)(2,1)}, u32[]{:S(2)}) copy-start(bf16[1,128,3072]{2,1,0:T(8,128)(2,1)} %param.9) | copy-start | bytes 2359300
  7.2 17.6 %copy-start.2 = (bf16[1,128,2048]{2,1,0:T(8,128)(2,1)S(1)}, bf16[1,128,2048]{2,1,0:T(8,128)(2,1)}, u32[]{:S(2)}) copy-start(bf16[1,128,2048]{2,1,0:T(8,128)(2,1)} %param.6) | copy-start | bytes 1572868
  7.2 108.5 %all-gather.2.cloned.1.call-start = ((), (), s32[]{:S(2)}) async-start(), calls=%async_computation.4 | async-start | bytes 12976128 | tf_op jit(solution)/shard_map/all_gather | solution.py:146
  8.3 16.7 %copy-start.3 = (bf16[1,128,2048]{2,1,0:T(8,128)(2,1)S(1)}, bf16[1,128,2048]{2,1,0:T(8,128)(2,1)}, u32[]{:S(2)}) copy-start(bf16[1,128,2048]{2,1,0:T(8,128)(2,1)} %param.7) | copy-start | bytes 1572868
  23.9 1.5 copy-start.4
  29.1 94.0 %all-to-all-start = ((bf16[3,128,16,128]{3,1,0,2:T(8,128)(2,1)}), bf16[3,128,16,128]{3,1,0,2:T(8,128)(2,1)S(1)}, u32[]{:S(2)}, u32[]{:S(2)}) async-start(bf16[3,128,16,128]{3,1,0,2:T(8,128)(2,1)} %copy.23), calls=%async_computation | async-start | bytes 3145728 | tf_op jit(solution)/shard_map/all_to_all | solution.py:149
  123.1 7.0 %copy-start.1 = (bf16[3,128,16,128]{3,1,0,2:T(8,128)(2,1)}, bf16[3,128,16,128]{3,1,0,2:T(8,128)(2,1)S(1)}, u32[]{:S(2)}) copy-start(bf16[3,128,16,128]{3,1,0,2:T(8,128)(2,1)S(1)} %all-to-all-done) | copy-start | bytes 4718596
  123.1 18.6 %all-to-all-start.2 = ((bf16[128,16,128]{0,2,1:T(8,128)(2,1)}), bf16[128,16,128]{0,2,1:T(8,128)(2,1)S(1)}, u32[]{:S(2)}, u32[]{:S(2)}) async-start(bf16[128,16,128]{0,2,1:T(8,128)(2,1)} %copy.25), calls=%async_computation.2 | async-start | bytes 1048576 | tf_op jit(solution)/shard_map/all_to_all | solution.py:154
Sparse Core Ops, SparseCore 0:
  24.9 90.7 all-gather.1

commit v10 on v9

--- a/solution.py
+++ b/solution.py
@@ -6,7 +6,7 @@
 from jax import lax
 from jax.experimental import pallas as pl
 from jax.experimental.pallas import tpu as pltpu
-from jax.sharding import PartitionSpec as P
+from jax.sharding import Mesh, PartitionSpec as P
 
 HEADS = 16
 HEAD_DIM = 128
@@ -143,14 +143,22 @@
     slot_text = (jnp.arange(devices) * tok_rows < TXT)[:, None, None]
     outgoing = jnp.where(slot_text, out_weight[0][None], out_weight[1][None])
     stream_rows = lax.all_to_all(outgoing, "dp", split_axis=0, concat_axis=0, tiled=True)
-    weight = lax.all_gather(stream_rows, "seq", axis=1, tiled=True)
+    own_half = lax.all_gather(stream_rows, "z", axis=1, tiled=False)
+    other_half = lax.ppermute(own_half, "core", [(0, 1), (1, 0)])
 
     qkv = jnp.stack([by_heads(query_rows), by_heads(key_rows), by_heads(value_rows)])
     qkv_heads = lax.all_to_all(qkv, "dp", split_axis=2, concat_axis=1, tiled=True)
 
-    projected = jnp.einsum(
-        "te,kre->tkr", out_grad[0], weight, preferred_element_type=jnp.float32
+    own_part = jnp.einsum(
+        "te,kzre->tkzr", out_grad[0], own_half, preferred_element_type=jnp.float32
     )
+    other_part = jnp.einsum(
+        "te,kzre->tkzr", out_grad[0], other_half, preferred_element_type=jnp.float32
+    )
+    first = lax.axis_index("core") == 0
+    projected = jnp.stack(
+        [jnp.where(first, own_part, other_part), jnp.where(first, other_part, own_part)], axis=3
+    ).reshape(tok_rows, HEADS, HEAD_DIM)
     grad_heads = lax.all_to_all(
         projected.astype(jnp.bfloat16), "dp", split_axis=1, concat_axis=0, tiled=True
     )
@@ -172,15 +180,19 @@
 
 
 def solution(mesh):
+    dp, seq = mesh.shape["dp"], mesh.shape["seq"]
+    cores = 2
+    split = Mesh(mesh.devices.reshape(dp, seq // cores, cores), ("dp", "z", "core"))
+    rows = ("z", "core")
     in_specs = (
-        P("seq", "dp", None),
-        P("seq", "dp", None),
-        P("seq", "dp", None),
-        P("seq", "dp", None),
-        P(None, ("dp", "seq"), None),
-        P("seq"),
+        P(rows, "dp", None),
+        P(rows, "dp", None),
+        P(rows, "dp", None),
+        P(rows, "dp", None),
+        P(None, ("dp", "z", "core"), None),
+        P(rows),
     )
-    out_specs = (P("seq", "dp", None), P("seq", "dp", None), P("seq", "dp", None))
+    out_specs = (P(rows, "dp", None), P(rows, "dp", None), P(rows, "dp", None))
     return jax.shard_map(
-        per_device, mesh=mesh, in_specs=in_specs, out_specs=out_specs, check_vma=False
+        per_device, mesh=split, in_specs=in_specs, out_specs=out_specs, check_vma=False
     )

time: 194 us -> 229 us (1.18)
  waiting for transfers between devices: 82.8 us -> 104 us
  local copies, waits for them, and re-layouts: 7.58 us -> 16.9 us
  starting transfers between devices: 10.2 us -> 15.1 us
    all_to_all x1, waiting for transfers between devices: 0.01 us -> 16.1 us  [per_device(): lax.all_to_all(qkv, 'dp', split_axis=2, concat_axis=1, tiled=True)]
    all_gather x0 -> x1, local copies, waits for them, and re-layouts: none -> 8.93 us  [per_device(): own_half = lax.all_gather(stream_rows, 'z', axis=1, tiled=False)]
    all_gather x1, waiting for transfers between devices: 82.8 us -> 87.6 us  [per_device(): own_half = lax.all_gather(stream_rows, 'z', axis=1, tiled=False)]
    ppermute x0 -> x1, starting transfers between devices: none -> 4.72 us  [per_device(): other_half = lax.ppermute(own_half, 'core', [(0, 1), (1, 0)])]
    all_to_all x1, starting transfers between devices: 3.73 us -> 6.56 us  [per_device(): lax.all_to_all(qkv, 'dp', split_axis=2, concat_axis=1, tiled=True)]
    all_to_all x1, starting transfers between devices: 6.39 us -> 3.8 us  [per_device(): lax.all_to_all(projected.astype(jnp.bfloat16), 'dp', split_axis=1, concat...]
    dot_general x1 -> x2, matrix products: 6.46 us -> 6.53 us  [the longest x1 4.72 us: per_device(): jnp.einsum('te,kzre->tkzr', out_grad[0], other_half, preferred_element_ty...]
  transfers between devices with their start and end apart: 3 -> 4, of which waited for: 1 -> 2; matrix products, arithmetic and copies ran while one was open for 7% -> 6% of each run, Pallas kernels for 5% -> 4%
where the time goes in v10:
time: 229 us; the launch traced here: 228 us
  waiting for transfers between devices  104 us (45%)
  blocking collectives  42.5 us (19%)
  Pallas kernels  26.3 us (11%)
  local copies, waits for them, and re-layouts  16.9 us (7%)
  starting transfers between devices  15.1 us (7%)
  between operations  14.9 us (7%)
  matrix products  6.53 us (3%)
    all_gather x1, waiting for transfers between devices, per_device(): own_half = lax.all_gather(stream_rows, 'z', axis=1, tiled=False)  87.6 us
    all_to_all x1, blocking collectives, per_device(): lax.all_to_all(grads.transpose(1, 0, 2, 3), 'dp', split_axis=0, concat_ax...  27.2 us
    all_to_all x1, waiting for transfers between devices, per_device(): lax.all_to_all(qkv, 'dp', split_axis=2, concat_axis=1, tiled=True)  16.1 us
    all_to_all x1, blocking collectives, per_device(): lax.all_to_all(outgoing, 'dp', split_axis=0, concat_axis=0, tiled=True)  15.4 us
    pallas_call x1, Pallas kernels, attention_grads(): pl.pallas_call(gradient_kernel, grid=(rows // block,), in_specs=[pl.Block...  13.2 us
    pallas_call x1, Pallas kernels, attention_probs(): pl.pallas_call(softmax_kernel, grid=(rows // block,), in_specs=[pl.BlockS...  10.1 us
    all_gather x1, local copies, waits for them, and re-layouts, per_device(): own_half = lax.all_gather(stream_rows, 'z', axis=1, tiled=False)  8.93 us
    all_to_all x1, starting transfers between devices, per_device(): lax.all_to_all(qkv, 'dp', split_axis=2, concat_axis=1, tiled=True)  6.56 us
  transfers between devices with their start and end apart: 4, of which 2 were waited for; matrix products, arithmetic and copies ran while one was open for 6% of the time, Pallas kernels for 4%

profile of v10, /device:TPU:1, one launch (start us, length us, event | category | flops | bytes accessed | tf_op | source)
XLA Modules:
  0.0 227.7 jit_solution(5229051460335398399)
XLA Ops:
  7.2 0.8 slice_bitcast_fusion.1
  8.1 0.2 broadcast_select_fusion
  8.3 15.4 %all_to_all.40 = bf16[16,4,3072]{2,1,0:T(4,128)(2,1)S(1)} all-to-all(bf16[16,4,3072]{2,1,0:T(4,128)(2,1)S(1)} %broadcast_select_fusion), channel_id=1, replica_groups=mesh['dp'=16,'z'=16,'core'=2] {'dp'}, dimensions={0} | all-to-all | bytes 786432 | tf_op jit(solution)/shard_map/all_to_all | solution.py:145
  23.7 0.9 copy.30
  24.5 87.6 %all-gather.3.cloned.1.call-done = bf16[16,64,3072]{2,0,1:T(8,128)(2,1)} async-done(((bf16[16,4,3072]{2,0,1:T(8,128)(2,1)}), bf16[16,64,3072]{2,0,1:T(8,128)(2,1)}) %all-gather.3.cloned.1.call-update) | async-done | bytes 6291472 | tf_op jit(solution)/shard_map/all_gather | solution.py:146
  112.1 8.9 %copy.31 = bf16[16,16,4,3072]{3,1,2,0:T(8,128)(2,1)} copy(bf16[16,16,4,3072]{3,0,2,1:T(8,128)(2,1)} %bitcast.57) | data formatting | bytes 12582912 | tf_op jit(solution)/shard_map/all_gather | solution.py:146
  121.1 4.7 %collective-permute-start = (bf16[16,16,4,3072]{3,1,2,0:T(8,128)(2,1)}, bf16[16,16,4,3072]{3,1,2,0:T(8,128)(2,1)}, u32[]{:S(2)}, u32[]{:S(2)}) collective-permute-start(bf16[16,16,4,3072]{3,1,2,0:T(8,128)(2,1)} %copy.31), channel_id=1, source_target_pairs={{0,1},{1,0},{2,3},{3,2},{4,5},{5,4},{6,7},{7,6},{8,9},{9,8},{10,11... | collective-permute-start | bytes 18874376 | tf_op jit(solution)/shard_map/ppermute | solution.py:147
  125.8 0.3 copy.26
  126.1 0.3 copy.27
  126.4 0.3 copy.28
  126.6 1.3 pad_maximum_fusion
  128.0 2.7 %copy.29 = bf16[3,128,16,128]{3,1,0,2:T(8,128)(2,1)} copy(bf16[3,128,16,128]{1,3,2,0:T(8,128)(2,1)} %pad_maximum_fusion) | data formatting | bytes 3145728 | tf_op jit(solution)/shard_map/stack | solution.py:149
  130.7 6.6 %all-to-all-start = ((bf16[3,128,16,128]{3,1,0,2:T(8,128)(2,1)}), bf16[3,128,16,128]{3,1,0,2:T(8,128)(2,1)}, u32[]{:S(2)}, u32[]{:S(2)}) async-start(bf16[3,128,16,128]{3,1,0,2:T(8,128)(2,1)} %copy.29), calls=%async_computation | async-start | bytes 3145728 | tf_op jit(solution)/shard_map/all_to_all | solution.py:150
  137.3 4.7 %fusion = bf16[16,16,4,128]{3,1,2,0:T(8,128)(2,1)S(1)} fusion(bf16[16,16,4,3072]{3,1,2,0:T(8,128)(2,1)} %collective-permute-done, bf16[1,128,3072]{2,1,0:T(8,128)(2,1)S(1)} %copy-done), kind=kOutput, calls=%fused_computation.2 | convolution fusion | flops 805306368 | bytes 7340032 | tf_op jit(solution)/shard_map/te,kzre->tkzr/dot_general | solution.py:155
  142.1 1.8 fusion.4
  144.0 0.9 copy.35
  144.9 16.1 %all-to-all-done = bf16[3,128,16,128]{3,1,0,2:T(8,128)(2,1)} async-done(((bf16[3,128,16,128]{3,1,0,2:T(8,128)(2,1)}), bf16[3,128,16,128]{3,1,0,2:T(8,128)(2,1)}, u32[]{:S(2)}, u32[]{:S(2)}) %all-to-all-start) | async-done | bytes 1572896 | tf_op jit(solution)/shard_map/all_to_all | solution.py:150
  161.0 3.8 %all-to-all-start.2 = ((bf16[128,16,128]{0,2,1:T(8,128)(2,1)}), bf16[128,16,128]{0,2,1:T(8,128)(2,1)S(1)}, u32[]{:S(2)}, u32[]{:S(2)}) async-start(bf16[128,16,128]{0,2,1:T(8,128)(2,1)} %copy.35), calls=%async_computation.2 | async-start | bytes 1048576 | tf_op jit(solution)/shard_map/all_to_all | solution.py:162
  165.5 1.5 fusion.6
  166.9 10.1 %shard_map.85.p_ref = f32[2048,2048]{1,0:T(8,128)} custom-call(s32[1]{0:T(128)S(6)} %copy.44.length_ref, bf16[2048,128]{1,0:T(8,128)(2,1)S(1)} %bitcast.50, bf16[2048,128]{1,0:T(8,128)(2,1)S(1)} %bitcast.48), custom_call_target="tpu_custom_call" | custom-call | flops 1073741824 | bytes 17825792 | tf_op jit(solution)/shard_map/pallas_call | solution.py:31
  177.0 0.3 copy.36
  177.3 13.2 %shard_map.86 = (bf16[2048,128]{1,0:T(8,128)(2,1)S(1)}, bf16[2048,128]{1,0:T(8,128)(2,1)S(1)}, bf16[2048,128]{1,0:T(8,128)(2,1)S(1)}) custom-call(f32[2048,2048]{1,0:T(8,128)} %shard_map.85.p_ref, bf16[2048,128]{1,0:T(8,128)(2,1)S(1)} %bitcast.51, bf16[2048,128]{1,0:T(8,128)(2,1)S(1)} %bitcast.49, bf16[2048,128]{1,0:T(8,128)(2,1)S(1)} %bitcast.53, ...), custom_call_target="tpu_custom_call" | custom-call | flops 4294967296 | bytes 20447232 | tf_op jit(solution)/shard_map/pallas_call | solution.py:89
  190.7 27.2 %all_to_all.41.block_ref = bf16[16,3,128,128]{3,2,1,0:T(8,128)(2,1)} all-to-all(bf16[16,3,128,128]{3,2,1,0:T(8,128)(2,1)S(1)} %maximum_bitcast_fusion), channel_id=1, replica_groups=mesh['dp'=16,'z'=16,'core'=2] {'dp'}, dimensions={0} | all-to-all | bytes 3145728 | tf_op jit(solution)/shard_map/all_to_all | solution.py:178
  217.9 3.0 %shard_map.87 = (bf16[128,2048]{1,0:T(8,128)(2,1)}, bf16[128,2048]{1,0:T(8,128)(2,1)}, bf16[128,2048]{1,0:T(8,128)(2,1)}) custom-call(bf16[16,3,128,128]{3,2,1,0:T(8,128)(2,1)} %all_to_all.41.block_ref), custom_call_target="tpu_custom_call" | custom-call | bytes 3145728 | tf_op jit(solution)/shard_map/pallas_call | solution.py:125
  (21 shorter events, 0.3 us)
Async XLA Ops:
  7.2 130.1 %copy-start = (bf16[1,128,3072]{2,1,0:T(8,128)(2,1)S(1)}, bf16[1,128,3072]{2,1,0:T(8,128)(2,1)}, u32[]{:S(2)}) copy-start(bf16[1,128,3072]{2,1,0:T(8,128)(2,1)} %param.9) | copy-start | bytes 2359300
  7.2 104.9 %all-gather.3.cloned.1.call-start = ((), (), s32[]{:S(2)}) async-start(), calls=%async_computation.4 | async-start | bytes 6684672 | tf_op jit(solution)/shard_map/all_gather | solution.py:146
  112.1 13.7 %copy-start.1 = (bf16[1,128,2048]{2,1,0:T(8,128)(2,1)S(1)}, bf16[1,128,2048]{2,1,0:T(8,128)(2,1)}, u32[]{:S(2)}) copy-start(bf16[1,128,2048]{2,1,0:T(8,128)(2,1)} %param.6) | copy-start | bytes 1572868
  112.1 14.0 %copy-start.2 = (bf16[1,128,2048]{2,1,0:T(8,128)(2,1)S(1)}, bf16[1,128,2048]{2,1,0:T(8,128)(2,1)}, u32[]{:S(2)}) copy-start(bf16[1,128,2048]{2,1,0:T(8,128)(2,1)} %param.7) | copy-start | bytes 1572868
  121.0 5.3 %copy-start.3 = (bf16[1,128,2048]{2,1,0:T(8,128)(2,1)S(1)}, bf16[1,128,2048]{2,1,0:T(8,128)(2,1)}, u32[]{:S(2)}) copy-start(bf16[1,128,2048]{2,1,0:T(8,128)(2,1)} %param.8) | copy-start | bytes 1572868
  121.1 16.2 %collective-permute-start = (bf16[16,16,4,3072]{3,1,2,0:T(8,128)(2,1)}, bf16[16,16,4,3072]{3,1,2,0:T(8,128)(2,1)}, u32[]{:S(2)}, u32[]{:S(2)}) collective-permute-start(bf16[16,16,4,3072]{3,1,2,0:T(8,128)(2,1)} %copy.31), channel_id=1, source_target_pairs={{0,1},{1,0},{2,3},{3,2},{4,5},{5,4},{6,7},{7,6},{8,9},{9,8},{10,11... | collective-permute-start | bytes 18874376 | tf_op jit(solution)/shard_map/ppermute | solution.py:147
  128.0 14.1 %slice-start = ((s8[6291456]{0:T(1024)(128)(4,1)}), s8[2097152]{0:T(1024)(128)(4,1)S(1)}, s32[]{:S(2)}) async-start(s8[6291456]{0:T(1024)(128)(4,1)} %bitcast.58), calls=%async_computation.5 | async-start | bytes 4194304
  130.7 30.3 %all-to-all-start = ((bf16[3,128,16,128]{3,1,0,2:T(8,128)(2,1)}), bf16[3,128,16,128]{3,1,0,2:T(8,128)(2,1)}, u32[]{:S(2)}, u32[]{:S(2)}) async-start(bf16[3,128,16,128]{3,1,0,2:T(8,128)(2,1)} %copy.29), calls=%async_computation | async-start | bytes 3145728 | tf_op jit(solution)/shard_map/all_to_all | solution.py:150
  137.3 4.8 %slice-start.1 = ((s8[6291456]{0:T(1024)(128)(4,1)}), s8[4194304]{0:T(1024)(128)(4,1)S(1)}, s32[]{:S(2)}) async-start(s8[6291456]{0:T(1024)(128)(4,1)} %bitcast.58), calls=%async_computation.6 | async-start | bytes 8388608
  161.0 16.0 %all-to-all-start.2 = ((bf16[128,16,128]{0,2,1:T(8,128)(2,1)}), bf16[128,16,128]{0,2,1:T(8,128)(2,1)S(1)}, u32[]{:S(2)}, u32[]{:S(2)}) async-start(bf16[128,16,128]{0,2,1:T(8,128)(2,1)} %copy.35), calls=%async_computation.2 | async-start | bytes 1048576 | tf_op jit(solution)/shard_map/all_to_all | solution.py:162
Sparse Core Ops, SparseCore 0:
  24.7 87.4 all-gather.2

commit v11 on v9

--- a/solution.py
+++ b/solution.py
@@ -142,15 +142,23 @@
 
     slot_text = (jnp.arange(devices) * tok_rows < TXT)[:, None, None]
     outgoing = jnp.where(slot_text, out_weight[0][None], out_weight[1][None])
-    stream_rows = lax.all_to_all(outgoing, "dp", split_axis=0, concat_axis=0, tiled=True)
-    weight = lax.all_gather(stream_rows, "seq", axis=1, tiled=True)
+    half = outgoing.shape[1] // 2
+    first_rows = lax.all_to_all(outgoing[:, :half], "dp", split_axis=0, concat_axis=0, tiled=True)
+    first_weight = lax.all_gather(first_rows, "seq", axis=1, tiled=True)
+    second_rows = lax.all_to_all(outgoing[:, half:], "dp", split_axis=0, concat_axis=0, tiled=True)
+    second_rows, first_weight = lax.optimization_barrier((second_rows, first_weight))
+    second_weight = lax.all_gather(second_rows, "seq", axis=1, tiled=True)
 
     qkv = jnp.stack([by_heads(query_rows), by_heads(key_rows), by_heads(value_rows)])
     qkv_heads = lax.all_to_all(qkv, "dp", split_axis=2, concat_axis=1, tiled=True)
 
-    projected = jnp.einsum(
-        "te,kre->tkr", out_grad[0], weight, preferred_element_type=jnp.float32
-    )
+    parts = [
+        jnp.einsum("te,kre->tkr", out_grad[0], weight, preferred_element_type=jnp.float32).reshape(
+            tok_rows, HEADS, -1, half
+        )
+        for weight in (first_weight, second_weight)
+    ]
+    projected = jnp.concatenate(parts, axis=3).reshape(tok_rows, HEADS, HEAD_DIM)
     grad_heads = lax.all_to_all(
         projected.astype(jnp.bfloat16), "dp", split_axis=1, concat_axis=0, tiled=True
     )

time: 194 us -> 258 us (1.33)
  waiting for transfers between devices: 82.8 us -> 130 us
  blocking collectives: 43.6 us -> 53.1 us
  starting transfers between devices: 10.2 us -> 13.2 us
  matrix products: 6.46 us -> 9.14 us
    all_gather x1 -> x2, waiting for transfers between devices: 82.8 us -> 130 us  [the longest x1 69.4 us: per_device(): first_weight = lax.all_gather(first_rows, 'seq', axis=1, tiled=True)]
    all_to_all x1 -> x2, blocking collectives: 15.5 us -> 25 us  [the longest x1 14.6 us: per_device(): lax.all_to_all(outgoing[:, :half], 'dp', split_axis=0, concat_axis=0, til...]
    all_to_all x1, starting transfers between devices: 3.73 us -> 6.52 us  [per_device(): lax.all_to_all(qkv, 'dp', split_axis=2, concat_axis=1, tiled=True)]
    dot_general x1 -> x2, matrix products: 6.46 us -> 9.14 us  [per_device(): jnp.einsum('te,kre->tkr', out_grad[0], weight, preferred_element_type=jnp...]
  transfers between devices with their start and end apart: 3 -> 4, of which waited for: 1 -> 2; matrix products, arithmetic and copies ran while one was open for 7% -> 6% of each run, Pallas kernels for 5% -> 4%
where the time goes in v11:
time: 258 us; the launch traced here: 257 us
  waiting for transfers between devices  130 us (50%)
  blocking collectives  53.1 us (21%)
  Pallas kernels  26.3 us (10%)
  between operations  14.9 us (6%)
  starting transfers between devices  13.2 us (5%)
  matrix products  9.14 us (4%)
  local copies, waits for them, and re-layouts  8.38 us (3%)
    all_gather x1, waiting for transfers between devices, per_device(): first_weight = lax.all_gather(first_rows, 'seq', axis=1, tiled=True)  69.4 us
    all_gather x1, waiting for transfers between devices, per_device(): second_weight = lax.all_gather(second_rows, 'seq', axis=1, tiled=True)  60.7 us
    all_to_all x1, blocking collectives, per_device(): lax.all_to_all(grads.transpose(1, 0, 2, 3), 'dp', split_axis=0, concat_ax...  28.1 us
    all_to_all x1, blocking collectives, per_device(): lax.all_to_all(outgoing[:, :half], 'dp', split_axis=0, concat_axis=0, til...  14.6 us
    pallas_call x1, Pallas kernels, attention_grads(): pl.pallas_call(gradient_kernel, grid=(rows // block,), in_specs=[pl.Block...  13.2 us
    all_to_all x1, blocking collectives, per_device(): lax.all_to_all(outgoing[:, half:], 'dp', split_axis=0, concat_axis=0, til...  10.5 us
    pallas_call x1, Pallas kernels, attention_probs(): pl.pallas_call(softmax_kernel, grid=(rows // block,), in_specs=[pl.BlockS...  10.1 us
    dot_general x2, matrix products, per_device(): jnp.einsum('te,kre->tkr', out_grad[0], weight, preferred_element_type=jnp...  9.14 us
  transfers between devices with their start and end apart: 4, of which 2 were waited for; matrix products, arithmetic and copies ran while one was open for 6% of the time, Pallas kernels for 4%

profile of v11, /device:TPU:1, one launch (start us, length us, event | category | flops | bytes accessed | tf_op | source)
XLA Modules:
  0.0 256.7 jit_solution(6648516794077793570)
XLA Ops:
  7.2 0.8 slice_bitcast_fusion.1
  8.3 0.3 fusion.3
  8.6 14.6 %all_to_all.45 = bf16[16,2,3072]{2,1,0:T(2,128)(2,1)S(1)} all-to-all(bf16[16,2,3072]{2,1,0:T(2,128)(2,1)S(1)} %get-tuple-element.22), channel_id=1, replica_groups=mesh['dp'=16,'seq'=32] {'dp'}, dimensions={0} | all-to-all | bytes 393216 | tf_op jit(solution)/shard_map/all_to_all | solution.py:146
  23.2 0.7 copy.35
  24.0 10.5 %all_to_all.46 = bf16[16,2,3072]{2,1,0:T(2,128)(2,1)S(1)} all-to-all(bf16[16,2,3072]{2,1,0:T(2,128)(2,1)S(1)} %get-tuple-element.23), channel_id=1, replica_groups=mesh['dp'=16,'seq'=32] {'dp'}, dimensions={0} | all-to-all | bytes 393216 | tf_op jit(solution)/shard_map/all_to_all | solution.py:148
  34.4 69.4 %all-gather.3.cloned.1.call-done = bf16[16,64,3072]{2,0,1:T(8,128)(2,1)} async-done(((bf16[16,2,3072]{2,0,1:T(8,128)(2,1)}), bf16[16,64,3072]{2,0,1:T(8,128)(2,1)}) %all-gather.3.cloned.1.call-update) | async-done | bytes 6291472 | tf_op jit(solution)/shard_map/all_gather | solution.py:147
  103.8 0.7 copy.36
  104.6 0.3 copy.31
  104.9 0.3 copy.32
  105.1 1.0 copy.33
  106.1 1.2 pad_maximum_fusion
  107.4 1.6 copy.34
  109.0 6.5 %all-to-all-start = ((bf16[3,128,16,128]{3,1,0,2:T(8,128)(2,1)}), bf16[3,128,16,128]{3,1,0,2:T(8,128)(2,1)S(1)}, u32[]{:S(2)}, u32[]{:S(2)}) async-start(bf16[3,128,16,128]{3,1,0,2:T(8,128)(2,1)} %copy.34), calls=%async_computation | async-start | bytes 3145728 | tf_op jit(solution)/shard_map/all_to_all | solution.py:153
  115.5 4.6 %convolution_convert_fusion.1 = bf16[16,64,128]{2,0,1:T(8,128)(2,1)S(1)} fusion(bf16[16,64,3072]{2,0,1:T(8,128)(2,1)} %all-gather.3.cloned.1.call-done, bf16[1,128,3072]{2,1,0:T(8,128)(2,1)S(1)} %copy-done), kind=kOutput, calls=%fused_computation.3 | convolution fusion | flops 805437440 | bytes 7340032 | tf_op jit(solution)/shard_map/te,kre->tkr/dot_general | solution.py:156
  120.1 60.7 %all-gather.5.cloned.1.call-done = bf16[16,64,3072]{2,0,1:T(8,128)(2,1)} async-done(((bf16[16,2,3072]{2,0,1:T(8,128)(2,1)}), bf16[16,64,3072]{2,0,1:T(8,128)(2,1)}) %all-gather.5.cloned.1.call-update) | async-done | bytes 6291472 | tf_op jit(solution)/shard_map/all_gather | solution.py:150
  180.8 4.6 %convolution_convert_fusion = bf16[16,64,128]{2,0,1:T(8,128)(2,1)S(1)} fusion(bf16[16,64,3072]{2,0,1:T(8,128)(2,1)} %all-gather.5.cloned.1.call-done, bf16[1,128,3072]{2,1,0:T(8,128)(2,1)S(1)} %copy-done), kind=kOutput, calls=%fused_computation.2 | convolution fusion | flops 805437440 | bytes 7340032 | tf_op jit(solution)/shard_map/te,kre->tkr/dot_general | solution.py:156
  185.5 0.9 copy.37
  186.4 6.6 %all-to-all-start.3 = ((bf16[128,16,128]{0,2,1:T(8,128)(2,1)}), bf16[128,16,128]{0,2,1:T(8,128)(2,1)S(1)}, u32[]{:S(2)}, u32[]{:S(2)}) async-start(bf16[128,16,128]{0,2,1:T(8,128)(2,1)} %copy.37), calls=%async_computation.3 | async-start | bytes 1048576 | tf_op jit(solution)/shard_map/all_to_all | solution.py:162
  193.6 1.5 fusion.2
  195.1 10.1 %shard_map.85.p_ref = f32[2048,2048]{1,0:T(8,128)} custom-call(s32[1]{0:T(128)S(6)} %copy.39.length_ref, bf16[2048,128]{1,0:T(8,128)(2,1)S(1)} %bitcast.42, bf16[2048,128]{1,0:T(8,128)(2,1)S(1)} %bitcast.40), custom_call_target="tpu_custom_call" | custom-call | flops 1073741824 | bytes 17825792 | tf_op jit(solution)/shard_map/pallas_call | solution.py:31
  205.2 0.3 copy.38
  205.5 13.2 %shard_map.86 = (bf16[2048,128]{1,0:T(8,128)(2,1)S(1)}, bf16[2048,128]{1,0:T(8,128)(2,1)S(1)}, bf16[2048,128]{1,0:T(8,128)(2,1)S(1)}) custom-call(f32[2048,2048]{1,0:T(8,128)} %shard_map.85.p_ref, bf16[2048,128]{1,0:T(8,128)(2,1)S(1)} %bitcast.43, bf16[2048,128]{1,0:T(8,128)(2,1)S(1)} %bitcast.41, bf16[2048,128]{1,0:T(8,128)(2,1)S(1)} %bitcast.45, ...), custom_call_target="tpu_custom_call" | custom-call | flops 4294967296 | bytes 20447232 | tf_op jit(solution)/shard_map/pallas_call | solution.py:89
  218.9 28.1 %all_to_all.47.block_ref = bf16[16,3,128,128]{3,2,1,0:T(8,128)(2,1)} all-to-all(bf16[16,3,128,128]{3,2,1,0:T(8,128)(2,1)S(1)} %maximum_bitcast_fusion), channel_id=1, replica_groups=mesh['dp'=16,'seq'=32] {'dp'}, dimensions={0} | all-to-all | bytes 3145728 | tf_op jit(solution)/shard_map/all_to_all | solution.py:178
  246.9 3.0 %shard_map.87 = (bf16[128,2048]{1,0:T(8,128)(2,1)}, bf16[128,2048]{1,0:T(8,128)(2,1)}, bf16[128,2048]{1,0:T(8,128)(2,1)}) custom-call(bf16[16,3,128,128]{3,2,1,0:T(8,128)(2,1)} %all_to_all.47.block_ref), custom_call_target="tpu_custom_call" | custom-call | bytes 3145728 | tf_op jit(solution)/shard_map/pallas_call | solution.py:125
  (20 shorter events, 0.6 us)
Async XLA Ops:
  7.2 108.3 %copy-start = (bf16[1,128,3072]{2,1,0:T(8,128)(2,1)S(1)}, bf16[1,128,3072]{2,1,0:T(8,128)(2,1)}, u32[]{:S(2)}) copy-start(bf16[1,128,3072]{2,1,0:T(8,128)(2,1)} %param.9) | copy-start | bytes 2359300
  7.2 96.6 %all-gather.3.cloned.1.call-start = ((), (), s32[]{:S(2)}) async-start(), calls=%async_computation.5 | async-start | bytes 6488064 | tf_op jit(solution)/shard_map/all_gather | solution.py:147
  8.1 96.5 %copy-start.2 = (bf16[1,128,2048]{2,1,0:T(8,128)(2,1)S(1)}, bf16[1,128,2048]{2,1,0:T(8,128)(2,1)}, u32[]{:S(2)}) copy-start(bf16[1,128,2048]{2,1,0:T(8,128)(2,1)} %param.6) | copy-start | bytes 1572868
  8.6 96.3 %copy-start.3 = (bf16[1,128,2048]{2,1,0:T(8,128)(2,1)S(1)}, bf16[1,128,2048]{2,1,0:T(8,128)(2,1)}, u32[]{:S(2)}) copy-start(bf16[1,128,2048]{2,1,0:T(8,128)(2,1)} %param.7) | copy-start | bytes 1572868
  23.9 81.2 %copy-start.4 = (bf16[1,128,2048]{2,1,0:T(8,128)(2,1)S(1)}, bf16[1,128,2048]{2,1,0:T(8,128)(2,1)}, u32[]{:S(2)}) copy-start(bf16[1,128,2048]{2,1,0:T(8,128)(2,1)} %param.8) | copy-start | bytes 1572868
  23.9 156.9 %all-gather.5.cloned.1.call-start = ((), (), s32[]{:S(2)}) async-start(), calls=%async_computation.6 | async-start | bytes 6488064 | tf_op jit(solution)/shard_map/all_gather | solution.py:150
  109.0 77.4 %all-to-all-start = ((bf16[3,128,16,128]{3,1,0,2:T(8,128)(2,1)}), bf16[3,128,16,128]{3,1,0,2:T(8,128)(2,1)S(1)}, u32[]{:S(2)}, u32[]{:S(2)}) async-start(bf16[3,128,16,128]{3,1,0,2:T(8,128)(2,1)} %copy.34), calls=%async_computation | async-start | bytes 3145728 | tf_op jit(solution)/shard_map/all_to_all | solution.py:153
  186.4 7.2 %copy-start.1 = (bf16[3,128,16,128]{3,1,0,2:T(8,128)(2,1)}, bf16[3,128,16,128]{3,1,0,2:T(8,128)(2,1)S(1)}, u32[]{:S(2)}) copy-start(bf16[3,128,16,128]{3,1,0,2:T(8,128)(2,1)S(1)} %all-to-all-done) | copy-start | bytes 4718596
  186.4 18.8 %all-to-all-start.3 = ((bf16[128,16,128]{0,2,1:T(8,128)(2,1)}), bf16[128,16,128]{0,2,1:T(8,128)(2,1)S(1)}, u32[]{:S(2)}, u32[]{:S(2)}) async-start(bf16[128,16,128]{0,2,1:T(8,128)(2,1)} %copy.37), calls=%async_computation.3 | async-start | bytes 1048576 | tf_op jit(solution)/shard_map/all_to_all | solution.py:162
Sparse Core Ops, SparseCore 0:
  24.0 79.7 all-gather.2
  106.5 74.2 all-gather.4

commit v12 on v9

--- a/solution.py
+++ b/solution.py
@@ -140,10 +140,11 @@
     def by_heads(array):
         return array[0].reshape(tok_rows, HEADS, HEAD_DIM)
 
-    slot_text = (jnp.arange(devices) * tok_rows < TXT)[:, None, None]
-    outgoing = jnp.where(slot_text, out_weight[0][None], out_weight[1][None])
-    stream_rows = lax.all_to_all(outgoing, "dp", split_axis=0, concat_axis=0, tiled=True)
-    weight = lax.all_gather(stream_rows, "seq", axis=1, tiled=True)
+    both_streams = lax.all_gather(out_weight, ("dp", "seq"), axis=1, tiled=True)
+    stream = (lax.axis_index("dp") * tok_rows >= TXT).astype(jnp.int32)
+    weight = lax.dynamic_index_in_dim(both_streams, stream, 0, keepdims=False).reshape(
+        HEADS, -1, out_weight.shape[-1]
+    )
 
     qkv = jnp.stack([by_heads(query_rows), by_heads(key_rows), by_heads(value_rows)])
     qkv_heads = lax.all_to_all(qkv, "dp", split_axis=2, concat_axis=1, tiled=True)

time: 194 us -> 366 us (1.89)
  waiting for transfers between devices: 82.8 us -> 225 us
  local copies, waits for them, and re-layouts: 7.58 us -> 49.8 us
  blocking collectives: 43.6 us -> 28.1 us
    all_gather x1, waiting for transfers between devices: 82.8 us -> 225 us  [per_device(): both_streams = lax.all_gather(out_weight, ('dp', 'seq'), axis=1, tiled=True)]
    dynamic_slice x0 -> x1, local copies, waits for them, and re-layouts: none -> 28.2 us  [per_device(): lax.dynamic_index_in_dim(both_streams, stream, 0, keepdims=False)]
    unnamed x13 -> x11, local copies, waits for them, and re-layouts: 1.57 us -> 18.3 us
    all_to_all x1 -> x0, blocking collectives: 15.5 us -> none  [per_device(): lax.all_to_all(outgoing, 'dp', split_axis=0, concat_axis=0, tiled=True)]
    all_to_all x1, starting transfers between devices: 3.73 us -> 7.58 us  [per_device(): lax.all_to_all(qkv, 'dp', split_axis=2, concat_axis=1, tiled=True)]
  transfers between devices with their start and end apart: 3 -> 3, of which waited for: 1 -> 1; matrix products, arithmetic and copies ran while one was open for 7% -> 15% of each run, Pallas kernels for 5% -> 3%
where the time goes in v12:
time: 366 us; the launch traced here: 365 us
  waiting for transfers between devices  225 us (61%)
  local copies, waits for them, and re-layouts  49.8 us (14%)
  blocking collectives  28.1 us (8%)
  Pallas kernels  26.2 us (7%)
  between operations  14.8 us (4%)
  starting transfers between devices  12.9 us (4%)
  matrix products  7.24 us (2%)
    all_gather x1, waiting for transfers between devices, per_device(): both_streams = lax.all_gather(out_weight, ('dp', 'seq'), axis=1, tiled=True)  225 us
    dynamic_slice x1, local copies, waits for them, and re-layouts, per_device(): lax.dynamic_index_in_dim(both_streams, stream, 0, keepdims=False)  28.2 us
    all_to_all x1, blocking collectives, per_device(): lax.all_to_all(grads.transpose(1, 0, 2, 3), 'dp', split_axis=0, concat_ax...  28.1 us
    unnamed x11, local copies, waits for them, and re-layouts  18.3 us
    pallas_call x1, Pallas kernels, attention_grads(): pl.pallas_call(gradient_kernel, grid=(rows // block,), in_specs=[pl.Block...  13.2 us
    pallas_call x1, Pallas kernels, attention_probs(): pl.pallas_call(softmax_kernel, grid=(rows // block,), in_specs=[pl.BlockS...  10 us
    all_to_all x1, starting transfers between devices, per_device(): lax.all_to_all(qkv, 'dp', split_axis=2, concat_axis=1, tiled=True)  7.58 us
  transfers between devices with their start and end apart: 3, of which 1 were waited for; matrix products, arithmetic and copies ran while one was open for 15% of the time, Pallas kernels for 3%

profile of v12, /device:TPU:1, one launch (start us, length us, event | category | flops | bytes accessed | tf_op | source)
XLA Modules:
  0.0 364.9 jit_solution(15919076537912087492)
XLA Ops:
  7.2 0.0 copy-start
  7.2 0.0 all-gather.2.cloned.1.call-start
  7.2 1.6 copy.19
  8.8 0.0 all-gather.2.cloned.1.call-update
  8.8 1.3 copy.15
  10.1 1.3 copy.16
  11.5 1.0 copy.17
  12.5 1.2 pad_maximum_fusion
  13.7 1.6 copy.18
  15.3 7.6 %all-to-all-start = ((bf16[3,128,16,128]{3,1,0,2:T(8,128)(2,1)}), bf16[3,128,16,128]{3,1,0,2:T(8,128)(2,1)S(1)}, u32[]{:S(2)}, u32[]{:S(2)}) async-start(bf16[3,128,16,128]{3,1,0,2:T(8,128)(2,1)} %copy.18), calls=%async_computation | async-start | bytes 3145728 | tf_op jit(solution)/shard_map/all_to_all | solution.py:150
  22.9 224.5 %all-gather.2.cloned.1.call-done = bf16[2,2048,3072]{2,0,1:T(2,128)(2,1)} async-done(((bf16[2,4,3072]{2,0,1:T(2,128)(2,1)}), bf16[2,2048,3072]{2,0,1:T(2,128)(2,1)}) %all-gather.2.cloned.1.call-update) | async-done | bytes 25165840 | tf_op jit(solution)/shard_map/all_gather | solution.py:143
  247.4 28.2 %constant_dynamic-slice_fusion = bf16[1,2048,3072]{2,0,1:T(2,128)(2,1)S(1)} fusion(bf16[2,2048,3072]{2,0,1:T(2,128)(2,1)} %all-gather.2.cloned.1.call-done, s32[]{:T(128)S(6)} %select_n.4), kind=kLoop, calls=%fused_computation.5 | loop fusion | bytes 25165828 | tf_op jit(solution)/shard_map/jit(dynamic_index_in_dim)/dynamic_slice | solution.py:145
  275.6 13.1 %copy.22 = bf16[1,2048,3072]{2,1,0:T(8,128)(2,1)} copy(bf16[1,2048,3072]{2,0,1:T(2,128)(2,1)S(1)} %constant_dynamic-slice_fusion) | data formatting | bytes 25165824
  288.6 7.2 %fusion = bf16[128,16,128]{0,2,1:T(8,128)(2,1)} fusion(bf16[16,128,3072]{2,1,0:T(8,128)(2,1)} %bitcast.38, bf16[1,128,3072]{2,1,0:T(8,128)(2,1)S(1)} %copy-done), kind=kOutput, calls=%fused_computation.3 | convolution fusion | flops 1610874880 | bytes 13893632 | tf_op jit(solution)/shard_map/te,kre->tkr/dot_general | solution.py:152
  295.9 0.0 all-to-all-done
  295.9 5.3 %all-to-all-start.1 = ((bf16[128,16,128]{0,2,1:T(8,128)(2,1)}), bf16[128,16,128]{0,2,1:T(8,128)(2,1)S(1)}, u32[]{:S(2)}, u32[]{:S(2)}) async-start(bf16[128,16,128]{0,2,1:T(8,128)(2,1)} %fusion), calls=%async_computation.1 | async-start | bytes 1048576 | tf_op jit(solution)/shard_map/all_to_all | solution.py:155
  301.9 1.5 fusion.2
  303.3 10.0 %shard_map.85.p_ref = f32[2048,2048]{1,0:T(8,128)} custom-call(s32[1]{0:T(128)S(6)} %copy.23.length_ref, bf16[2048,128]{1,0:T(8,128)(2,1)S(1)} %bitcast.31, bf16[2048,128]{1,0:T(8,128)(2,1)S(1)} %bitcast.29), custom_call_target="tpu_custom_call" | custom-call | flops 1073741824 | bytes 17825792 | tf_op jit(solution)/shard_map/pallas_call | solution.py:31
  313.3 0.0 all-to-all-done.1
  313.3 0.3 copy.21
  313.6 13.2 %shard_map.86 = (bf16[2048,128]{1,0:T(8,128)(2,1)S(1)}, bf16[2048,128]{1,0:T(8,128)(2,1)S(1)}, bf16[2048,128]{1,0:T(8,128)(2,1)S(1)}) custom-call(f32[2048,2048]{1,0:T(8,128)} %shard_map.85.p_ref, bf16[2048,128]{1,0:T(8,128)(2,1)S(1)} %bitcast.32, bf16[2048,128]{1,0:T(8,128)(2,1)S(1)} %bitcast.30, bf16[2048,128]{1,0:T(8,128)(2,1)S(1)} %bitcast.34, ...), custom_call_target="tpu_custom_call" | custom-call | flops 4294967296 | bytes 20447232 | tf_op jit(solution)/shard_map/pallas_call | solution.py:89
  326.9 0.2 maximum_bitcast_fusion
  327.0 28.1 %all_to_all.35.block_ref = bf16[16,3,128,128]{3,2,1,0:T(8,128)(2,1)} all-to-all(bf16[16,3,128,128]{3,2,1,0:T(8,128)(2,1)S(1)} %maximum_bitcast_fusion), channel_id=1, replica_groups=mesh['dp'=16,'seq'=32] {'dp'}, dimensions={0} | all-to-all | bytes 3145728 | tf_op jit(solution)/shard_map/all_to_all | solution.py:171
  355.1 3.0 shard_map.87
  (5 shorter events, 0.0 us)
Async XLA Ops:
  7.2 281.5 %copy-start = (bf16[1,128,3072]{2,1,0:T(8,128)(2,1)S(1)}, bf16[1,128,3072]{2,1,0:T(8,128)(2,1)}, u32[]{:S(2)}) copy-start(bf16[1,128,3072]{2,1,0:T(8,128)(2,1)} %param.9) | copy-start | bytes 2359300
  7.2 4.3 %copy-start.2 = (bf16[1,128,2048]{2,1,0:T(8,128)(2,1)S(1)}, bf16[1,128,2048]{2,1,0:T(8,128)(2,1)}, u32[]{:S(2)}) copy-start(bf16[1,128,2048]{2,1,0:T(8,128)(2,1)} %param.8) | copy-start | bytes 1572868
  7.2 240.2 %all-gather.2.cloned.1.call-start = ((), (), s32[]{:S(2)}) async-start(), calls=%async_computation.3 | async-start | bytes 25214976 | tf_op jit(solution)/shard_map/all_gather | solution.py:143
  15.3 280.6 %all-to-all-start = ((bf16[3,128,16,128]{3,1,0,2:T(8,128)(2,1)}), bf16[3,128,16,128]{3,1,0,2:T(8,128)(2,1)S(1)}, u32[]{:S(2)}, u32[]{:S(2)}) async-start(bf16[3,128,16,128]{3,1,0,2:T(8,128)(2,1)} %copy.18), calls=%async_computation | async-start | bytes 3145728 | tf_op jit(solution)/shard_map/all_to_all | solution.py:150
  295.9 6.0 %copy-start.1 = (bf16[3,128,16,128]{3,1,0,2:T(8,128)(2,1)}, bf16[3,128,16,128]{3,1,0,2:T(8,128)(2,1)S(1)}, u32[]{:S(2)}) copy-start(bf16[3,128,16,128]{3,1,0,2:T(8,128)(2,1)S(1)} %all-to-all-done) | copy-start | bytes 4718596
  295.9 17.5 %all-to-all-start.1 = ((bf16[128,16,128]{0,2,1:T(8,128)(2,1)}), bf16[128,16,128]{0,2,1:T(8,128)(2,1)S(1)}, u32[]{:S(2)}, u32[]{:S(2)}) async-start(bf16[128,16,128]{0,2,1:T(8,128)(2,1)} %fusion), calls=%async_computation.1 | async-start | bytes 1048576 | tf_op jit(solution)/shard_map/all_to_all | solution.py:155
Sparse Core Ops, SparseCore 0:
  13.3 234.0 all-gather.1

commit v13 on v9

--- a/solution.py
+++ b/solution.py
@@ -11,7 +11,7 @@
 HEADS = 16
 HEAD_DIM = 128
 TXT = 512
-BLOCK_ROWS = 256
+BLOCK_ROWS = 512
 
 
 def softmax_kernel(length_ref, q_ref, k_ref, p_ref):

time: 194 us -> 193 us (level)
  no operation moved by 1% of the time
where the time goes in v13:
time: 193 us; the launch traced here: 192 us
  waiting for transfers between devices  82.8 us (43%)
  blocking collectives  43.6 us (23%)
  Pallas kernels  25.1 us (13%)
  between operations  14.8 us (8%)
  starting transfers between devices  10.2 us (5%)
  local copies, waits for them, and re-layouts  7.58 us (4%)
  matrix products  6.46 us (3%)
    all_gather x1, waiting for transfers between devices, per_device(): weight = lax.all_gather(stream_rows, 'seq', axis=1, tiled=True)  82.8 us
    all_to_all x1, blocking collectives, per_device(): lax.all_to_all(grads.transpose(1, 0, 2, 3), 'dp', split_axis=0, concat_ax...  28.1 us
    all_to_all x1, blocking collectives, per_device(): lax.all_to_all(outgoing, 'dp', split_axis=0, concat_axis=0, tiled=True)  15.5 us
    pallas_call x1, Pallas kernels, attention_grads(): pl.pallas_call(gradient_kernel, grid=(rows // block,), in_specs=[pl.Block...  13.1 us
    pallas_call x1, Pallas kernels, attention_probs(): pl.pallas_call(softmax_kernel, grid=(rows // block,), in_specs=[pl.BlockS...  9.07 us
    dot_general x1, matrix products, per_device(): jnp.einsum('te,kre->tkr', out_grad[0], weight, preferred_element_type=jnp...  6.46 us
    all_to_all x1, starting transfers between devices, per_device(): lax.all_to_all(projected.astype(jnp.bfloat16), 'dp', split_axis=1, concat...  6.39 us
  transfers between devices with their start and end apart: 3, of which 1 were waited for; matrix products, arithmetic and copies ran while one was open for 7% of the time, Pallas kernels for 5%

profile of v13, /device:TPU:1, one launch (start us, length us, event | category | flops | bytes accessed | tf_op | source)
XLA Modules:
  0.0 192.1 jit_solution(17563107383615076303)
XLA Ops:
  7.2 0.0 copy-start
  7.2 0.0 all-gather.2.cloned.1.call-start
  7.2 0.9 slice_bitcast_fusion.1
  8.1 0.2 broadcast_select_fusion
  8.4 15.5 %all_to_all.40 = bf16[16,4,3072]{2,1,0:T(4,128)(2,1)S(1)} all-to-all(bf16[16,4,3072]{2,1,0:T(4,128)(2,1)S(1)} %broadcast_select_fusion), channel_id=1, replica_groups=mesh['dp'=16,'seq'=32] {'dp'}, dimensions={0} | all-to-all | bytes 786432 | tf_op jit(solution)/shard_map/all_to_all | solution.py:145
  23.9 0.9 copy.24
  24.7 0.0 all-gather.2.cloned.1.call-update
  24.8 0.3 copy.20
  25.0 0.3 copy.21
  25.3 1.0 copy.22
  26.3 1.2 pad_maximum_fusion
  27.5 1.6 copy.23
  29.1 3.7 %all-to-all-start = ((bf16[3,128,16,128]{3,1,0,2:T(8,128)(2,1)}), bf16[3,128,16,128]{3,1,0,2:T(8,128)(2,1)S(1)}, u32[]{:S(2)}, u32[]{:S(2)}) async-start(bf16[3,128,16,128]{3,1,0,2:T(8,128)(2,1)} %copy.23), calls=%async_computation | async-start | bytes 3145728 | tf_op jit(solution)/shard_map/all_to_all | solution.py:149
  32.9 82.8 %all-gather.2.cloned.1.call-done = bf16[16,128,3072]{2,0,1:T(8,128)(2,1)} async-done(((bf16[16,4,3072]{2,0,1:T(8,128)(2,1)}), bf16[16,128,3072]{2,0,1:T(8,128)(2,1)}) %all-gather.2.cloned.1.call-update) | async-done | bytes 12582928 | tf_op jit(solution)/shard_map/all_gather | solution.py:146
  115.7 6.5 %fusion = bf16[128,16,128]{0,1,2:T(8,128)(2,1)S(1)} fusion(bf16[16,128,3072]{2,0,1:T(8,128)(2,1)} %all-gather.2.cloned.1.call-done, bf16[1,128,3072]{2,1,0:T(8,128)(2,1)S(1)} %copy-done), kind=kOutput, calls=%fused_computation.3 | convolution fusion | flops 1610874880 | bytes 13893632 | tf_op jit(solution)/shard_map/te,kre->tkr/dot_general | solution.py:151
  122.1 0.9 copy.25
  123.1 6.4 %all-to-all-start.2 = ((bf16[128,16,128]{0,2,1:T(8,128)(2,1)}), bf16[128,16,128]{0,2,1:T(8,128)(2,1)S(1)}, u32[]{:S(2)}, u32[]{:S(2)}) async-start(bf16[128,16,128]{0,2,1:T(8,128)(2,1)} %copy.25), calls=%async_computation.2 | async-start | bytes 1048576 | tf_op jit(solution)/shard_map/all_to_all | solution.py:154
  130.1 1.5 fusion.2
  131.6 9.1 %shard_map.85.p_ref = f32[2048,2048]{1,0:T(8,128)} custom-call(s32[1]{0:T(128)S(6)} %copy.27.length_ref, bf16[2048,128]{1,0:T(8,128)(2,1)S(1)} %bitcast.34, bf16[2048,128]{1,0:T(8,128)(2,1)S(1)} %bitcast.32), custom_call_target="tpu_custom_call" | custom-call | flops 1073741824 | bytes 17825792 | tf_op jit(solution)/shard_map/pallas_call | solution.py:31
  140.7 0.3 copy.26
  141.0 13.1 %shard_map.86 = (bf16[2048,128]{1,0:T(8,128)(2,1)S(1)}, bf16[2048,128]{1,0:T(8,128)(2,1)S(1)}, bf16[2048,128]{1,0:T(8,128)(2,1)S(1)}) custom-call(f32[2048,2048]{1,0:T(8,128)} %shard_map.85.p_ref, bf16[2048,128]{1,0:T(8,128)(2,1)S(1)} %bitcast.35, bf16[2048,128]{1,0:T(8,128)(2,1)S(1)} %bitcast.33, bf16[2048,128]{1,0:T(8,128)(2,1)S(1)} %bitcast.37, ...), custom_call_target="tpu_custom_call" | custom-call | flops 4294967296 | bytes 20447232 | tf_op jit(solution)/shard_map/pallas_call | solution.py:89
  154.1 0.2 maximum_bitcast_fusion
  154.2 28.1 %all_to_all.41.block_ref = bf16[16,3,128,128]{3,2,1,0:T(8,128)(2,1)} all-to-all(bf16[16,3,128,128]{3,2,1,0:T(8,128)(2,1)S(1)} %maximum_bitcast_fusion), channel_id=1, replica_groups=mesh['dp'=16,'seq'=32] {'dp'}, dimensions={0} | all-to-all | bytes 3145728 | tf_op jit(solution)/shard_map/all_to_all | solution.py:170
  182.3 3.0 %shard_map.87 = (bf16[128,2048]{1,0:T(8,128)(2,1)}, bf16[128,2048]{1,0:T(8,128)(2,1)}, bf16[128,2048]{1,0:T(8,128)(2,1)}) custom-call(bf16[16,3,128,128]{3,2,1,0:T(8,128)(2,1)} %all_to_all.41.block_ref), custom_call_target="tpu_custom_call" | custom-call | bytes 3145728 | tf_op jit(solution)/shard_map/pallas_call | solution.py:125
  (12 shorter events, 0.0 us)
Async XLA Ops:
  7.2 108.5 %copy-start = (bf16[1,128,3072]{2,1,0:T(8,128)(2,1)S(1)}, bf16[1,128,3072]{2,1,0:T(8,128)(2,1)}, u32[]{:S(2)}) copy-start(bf16[1,128,3072]{2,1,0:T(8,128)(2,1)} %param.9) | copy-start | bytes 2359300
  7.2 17.6 %copy-start.2 = (bf16[1,128,2048]{2,1,0:T(8,128)(2,1)S(1)}, bf16[1,128,2048]{2,1,0:T(8,128)(2,1)}, u32[]{:S(2)}) copy-start(bf16[1,128,2048]{2,1,0:T(8,128)(2,1)} %param.6) | copy-start | bytes 1572868
  7.2 108.5 %all-gather.2.cloned.1.call-start = ((), (), s32[]{:S(2)}) async-start(), calls=%async_computation.4 | async-start | bytes 12976128 | tf_op jit(solution)/shard_map/all_gather | solution.py:146
  8.3 16.7 %copy-start.3 = (bf16[1,128,2048]{2,1,0:T(8,128)(2,1)S(1)}, bf16[1,128,2048]{2,1,0:T(8,128)(2,1)}, u32[]{:S(2)}) copy-start(bf16[1,128,2048]{2,1,0:T(8,128)(2,1)} %param.7) | copy-start | bytes 1572868
  23.9 1.5 copy-start.4
  29.1 94.0 %all-to-all-start = ((bf16[3,128,16,128]{3,1,0,2:T(8,128)(2,1)}), bf16[3,128,16,128]{3,1,0,2:T(8,128)(2,1)S(1)}, u32[]{:S(2)}, u32[]{:S(2)}) async-start(bf16[3,128,16,128]{3,1,0,2:T(8,128)(2,1)} %copy.23), calls=%async_computation | async-start | bytes 3145728 | tf_op jit(solution)/shard_map/all_to_all | solution.py:149
  123.1 7.0 %copy-start.1 = (bf16[3,128,16,128]{3,1,0,2:T(8,128)(2,1)}, bf16[3,128,16,128]{3,1,0,2:T(8,128)(2,1)S(1)}, u32[]{:S(2)}) copy-start(bf16[3,128,16,128]{3,1,0,2:T(8,128)(2,1)S(1)} %all-to-all-done) | copy-start | bytes 4718596
  123.1 17.6 %all-to-all-start.2 = ((bf16[128,16,128]{0,2,1:T(8,128)(2,1)}), bf16[128,16,128]{0,2,1:T(8,128)(2,1)S(1)}, u32[]{:S(2)}, u32[]{:S(2)}) async-start(bf16[128,16,128]{0,2,1:T(8,128)(2,1)} %copy.25), calls=%async_computation.2 | async-start | bytes 1048576 | tf_op jit(solution)/shard_map/all_to_all | solution.py:154
Sparse Core Ops, SparseCore 0:
  24.9 90.7 all-gather.1

commit v14 on v13

--- a/solution.py
+++ b/solution.py
@@ -11,7 +11,7 @@
 HEADS = 16
 HEAD_DIM = 128
 TXT = 512
-BLOCK_ROWS = 512
+BLOCK_ROWS = 1024
 
 
 def softmax_kernel(length_ref, q_ref, k_ref, p_ref):

time: 193 us -> 194 us (level)
  no operation moved by 1% of the time
where the time goes in v14:
time: 194 us; the launch traced here: 193 us
  waiting for transfers between devices  82.8 us (43%)
  blocking collectives  43.6 us (22%)
  Pallas kernels  26.2 us (14%)
  between operations  14.8 us (8%)
  starting transfers between devices  10.2 us (5%)
  local copies, waits for them, and re-layouts  7.58 us (4%)
  matrix products  6.46 us (3%)
    all_gather x1, waiting for transfers between devices, per_device(): weight = lax.all_gather(stream_rows, 'seq', axis=1, tiled=True)  82.8 us
    all_to_all x1, blocking collectives, per_device(): lax.all_to_all(grads.transpose(1, 0, 2, 3), 'dp', split_axis=0, concat_ax...  28.1 us
    all_to_all x1, blocking collectives, per_device(): lax.all_to_all(outgoing, 'dp', split_axis=0, concat_axis=0, tiled=True)  15.5 us
    pallas_call x1, Pallas kernels, attention_grads(): pl.pallas_call(gradient_kernel, grid=(rows // block,), in_specs=[pl.Block...  13.5 us
    pallas_call x1, Pallas kernels, attention_probs(): pl.pallas_call(softmax_kernel, grid=(rows // block,), in_specs=[pl.BlockS...  9.74 us
    dot_general x1, matrix products, per_device(): jnp.einsum('te,kre->tkr', out_grad[0], weight, preferred_element_type=jnp...  6.46 us
    all_to_all x1, starting transfers between devices, per_device(): lax.all_to_all(projected.astype(jnp.bfloat16), 'dp', split_axis=1, concat...  6.39 us
  transfers between devices with their start and end apart: 3, of which 1 were waited for; matrix products, arithmetic and copies ran while one was open for 7% of the time, Pallas kernels for 5%

profile of v14, /device:TPU:1, one launch (start us, length us, event | category | flops | bytes accessed | tf_op | source)
XLA Modules:
  0.0 193.1 jit_solution(2866549722158862675)
XLA Ops:
  7.2 0.0 copy-start
  7.2 0.0 all-gather.2.cloned.1.call-start
  7.2 0.9 slice_bitcast_fusion.1
  8.1 0.2 broadcast_select_fusion
  8.4 15.5 %all_to_all.40 = bf16[16,4,3072]{2,1,0:T(4,128)(2,1)S(1)} all-to-all(bf16[16,4,3072]{2,1,0:T(4,128)(2,1)S(1)} %broadcast_select_fusion), channel_id=1, replica_groups=mesh['dp'=16,'seq'=32] {'dp'}, dimensions={0} | all-to-all | bytes 786432 | tf_op jit(solution)/shard_map/all_to_all | solution.py:145
  23.9 0.9 copy.24
  24.7 0.0 all-gather.2.cloned.1.call-update
  24.8 0.3 copy.20
  25.0 0.3 copy.21
  25.3 1.0 copy.22
  26.3 1.2 pad_maximum_fusion
  27.5 1.6 copy.23
  29.1 3.7 %all-to-all-start = ((bf16[3,128,16,128]{3,1,0,2:T(8,128)(2,1)}), bf16[3,128,16,128]{3,1,0,2:T(8,128)(2,1)S(1)}, u32[]{:S(2)}, u32[]{:S(2)}) async-start(bf16[3,128,16,128]{3,1,0,2:T(8,128)(2,1)} %copy.23), calls=%async_computation | async-start | bytes 3145728 | tf_op jit(solution)/shard_map/all_to_all | solution.py:149
  32.9 82.8 %all-gather.2.cloned.1.call-done = bf16[16,128,3072]{2,0,1:T(8,128)(2,1)} async-done(((bf16[16,4,3072]{2,0,1:T(8,128)(2,1)}), bf16[16,128,3072]{2,0,1:T(8,128)(2,1)}) %all-gather.2.cloned.1.call-update) | async-done | bytes 12582928 | tf_op jit(solution)/shard_map/all_gather | solution.py:146
  115.7 6.5 %fusion = bf16[128,16,128]{0,1,2:T(8,128)(2,1)S(1)} fusion(bf16[16,128,3072]{2,0,1:T(8,128)(2,1)} %all-gather.2.cloned.1.call-done, bf16[1,128,3072]{2,1,0:T(8,128)(2,1)S(1)} %copy-done), kind=kOutput, calls=%fused_computation.3 | convolution fusion | flops 1610874880 | bytes 13893632 | tf_op jit(solution)/shard_map/te,kre->tkr/dot_general | solution.py:151
  122.1 0.9 copy.25
  123.1 6.4 %all-to-all-start.2 = ((bf16[128,16,128]{0,2,1:T(8,128)(2,1)}), bf16[128,16,128]{0,2,1:T(8,128)(2,1)S(1)}, u32[]{:S(2)}, u32[]{:S(2)}) async-start(bf16[128,16,128]{0,2,1:T(8,128)(2,1)} %copy.25), calls=%async_computation.2 | async-start | bytes 1048576 | tf_op jit(solution)/shard_map/all_to_all | solution.py:154
  130.1 1.5 fusion.2
  131.6 9.7 %shard_map.85.p_ref = f32[2048,2048]{1,0:T(8,128)} custom-call(s32[1]{0:T(128)S(6)} %copy.27.length_ref, bf16[2048,128]{1,0:T(8,128)(2,1)S(1)} %bitcast.34, bf16[2048,128]{1,0:T(8,128)(2,1)S(1)} %bitcast.32), custom_call_target="tpu_custom_call" | custom-call | flops 1073741824 | bytes 17825792 | tf_op jit(solution)/shard_map/pallas_call | solution.py:31
  141.4 0.3 copy.26
  141.6 13.5 %shard_map.86 = (bf16[2048,128]{1,0:T(8,128)(2,1)S(1)}, bf16[2048,128]{1,0:T(8,128)(2,1)S(1)}, bf16[2048,128]{1,0:T(8,128)(2,1)S(1)}) custom-call(f32[2048,2048]{1,0:T(8,128)} %shard_map.85.p_ref, bf16[2048,128]{1,0:T(8,128)(2,1)S(1)} %bitcast.35, bf16[2048,128]{1,0:T(8,128)(2,1)S(1)} %bitcast.33, bf16[2048,128]{1,0:T(8,128)(2,1)S(1)} %bitcast.37, ...), custom_call_target="tpu_custom_call" | custom-call | flops 4294967296 | bytes 20447232 | tf_op jit(solution)/shard_map/pallas_call | solution.py:89
  155.1 0.2 maximum_bitcast_fusion
  155.3 28.1 %all_to_all.41.block_ref = bf16[16,3,128,128]{3,2,1,0:T(8,128)(2,1)} all-to-all(bf16[16,3,128,128]{3,2,1,0:T(8,128)(2,1)S(1)} %maximum_bitcast_fusion), channel_id=1, replica_groups=mesh['dp'=16,'seq'=32] {'dp'}, dimensions={0} | all-to-all | bytes 3145728 | tf_op jit(solution)/shard_map/all_to_all | solution.py:170
  183.3 3.0 %shard_map.87 = (bf16[128,2048]{1,0:T(8,128)(2,1)}, bf16[128,2048]{1,0:T(8,128)(2,1)}, bf16[128,2048]{1,0:T(8,128)(2,1)}) custom-call(bf16[16,3,128,128]{3,2,1,0:T(8,128)(2,1)} %all_to_all.41.block_ref), custom_call_target="tpu_custom_call" | custom-call | bytes 3145728 | tf_op jit(solution)/shard_map/pallas_call | solution.py:125
  (12 shorter events, 0.0 us)
Async XLA Ops:
  7.2 108.5 %copy-start = (bf16[1,128,3072]{2,1,0:T(8,128)(2,1)S(1)}, bf16[1,128,3072]{2,1,0:T(8,128)(2,1)}, u32[]{:S(2)}) copy-start(bf16[1,128,3072]{2,1,0:T(8,128)(2,1)} %param.9) | copy-start | bytes 2359300
  7.2 17.6 %copy-start.2 = (bf16[1,128,2048]{2,1,0:T(8,128)(2,1)S(1)}, bf16[1,128,2048]{2,1,0:T(8,128)(2,1)}, u32[]{:S(2)}) copy-start(bf16[1,128,2048]{2,1,0:T(8,128)(2,1)} %param.6) | copy-start | bytes 1572868
  7.2 108.5 %all-gather.2.cloned.1.call-start = ((), (), s32[]{:S(2)}) async-start(), calls=%async_computation.4 | async-start | bytes 12976128 | tf_op jit(solution)/shard_map/all_gather | solution.py:146
  8.3 16.7 %copy-start.3 = (bf16[1,128,2048]{2,1,0:T(8,128)(2,1)S(1)}, bf16[1,128,2048]{2,1,0:T(8,128)(2,1)}, u32[]{:S(2)}) copy-start(bf16[1,128,2048]{2,1,0:T(8,128)(2,1)} %param.7) | copy-start | bytes 1572868
  23.9 1.5 copy-start.4
  29.1 94.0 %all-to-all-start = ((bf16[3,128,16,128]{3,1,0,2:T(8,128)(2,1)}), bf16[3,128,16,128]{3,1,0,2:T(8,128)(2,1)S(1)}, u32[]{:S(2)}, u32[]{:S(2)}) async-start(bf16[3,128,16,128]{3,1,0,2:T(8,128)(2,1)} %copy.23), calls=%async_computation | async-start | bytes 3145728 | tf_op jit(solution)/shard_map/all_to_all | solution.py:149
  123.1 7.1 %copy-start.1 = (bf16[3,128,16,128]{3,1,0,2:T(8,128)(2,1)}, bf16[3,128,16,128]{3,1,0,2:T(8,128)(2,1)S(1)}, u32[]{:S(2)}) copy-start(bf16[3,128,16,128]{3,1,0,2:T(8,128)(2,1)S(1)} %all-to-all-done) | copy-start | bytes 4718596
  123.1 18.3 %all-to-all-start.2 = ((bf16[128,16,128]{0,2,1:T(8,128)(2,1)}), bf16[128,16,128]{0,2,1:T(8,128)(2,1)S(1)}, u32[]{:S(2)}, u32[]{:S(2)}) async-start(bf16[128,16,128]{0,2,1:T(8,128)(2,1)} %copy.25), calls=%async_computation.2 | async-start | bytes 1048576 | tf_op jit(solution)/shard_map/all_to_all | solution.py:154
Sparse Core Ops, SparseCore 0:
  24.9 90.7 all-gather.1
